TPU v7x, 32 devices: a whole 2x2x4 slice. The times are simulated.
32 devices in a mesh: site: 2 (over x), handler: 16 (over z, y, core).
Axes of the slice: x: 2, y: 2, z: 4, core: 2. Of those that a mesh axis runs over, the one named last changes fastest.
Arguments:
- sgt: bfloat16 [8192, 6, 2048], P(('site', 'handler')), parts along dimension 0, may hold values from -6 to 6
- taps: bfloat16 [32], replicated, may hold values from 0.019897461 to 0.099609375
- moment: float32 [6, 2048], replicated, may hold values from -2.5 to 2.5
- index: int32 [512, 32], P('handler'), may hold values from 0 to 2047
- slip: bfloat16 [512, 32, 200], P('handler'), may hold values from 0 to 0.049804688
Outputs:
- seismogram: float32 [1024, 1024], P(('site', 'handler')), parts along dimension 0
There are 2 independent parts, one for each index of `site`. A program takes and returns all parts, laid end to end along the dimension named above; an argument that names none is the same for every part. Nothing has to cross between parts.
All inputs are finite; a program needn't handle non-finite values.
Results may differ from a plain program's by a relative error of at most 0.0014.
Values may be sent and summed in bfloat16 or wider, within the bound.
No kernel may reach another device: no remote copies, remote signals or barrier semaphores. Data moves between devices by JAX's collectives and lax.ppermute only.
A program may use at most 128 MiB of HBM per device.

v0:
```python
import jax
import jax.numpy as jnp
from jax import lax
from jax.experimental import pallas as pl
from jax.experimental.pallas import tpu as pltpu
from jax.sharding import PartitionSpec as P

DEC = 4
V_BLOCK = 8


def band_matrix(taps, rows, cols):
    row_ids = lax.broadcasted_iota(jnp.int32, (rows, cols), 0)
    col_ids = lax.broadcasted_iota(jnp.int32, (rows, cols), 1)
    lag = DEC * col_ids - row_ids
    matrix = jnp.zeros((rows, cols), jnp.bfloat16)
    for which in range(taps.shape[0]):
        matrix = jnp.where(lag == which, taps[which], matrix)
    return matrix


def conv_kernel(slip_ref, picked_ref, out_ref, spread_ref):
    vb = out_ref.shape[0]
    span = slip_ref.shape[1]
    width = out_ref.shape[1]
    col = lax.broadcasted_iota(jnp.int32, (8, width), 1)
    row = lax.broadcasted_iota(jnp.int32, (8, width), 0)
    lag = col - row

    def one(v, carry):
        spread_ref[...] = jnp.dot(slip_ref[v], picked_ref[v], preferred_element_type=jnp.float32)
        acc = jnp.zeros((8, width), jnp.float32)
        for g in range(span // 8):
            blk = spread_ref[8 * g:8 * g + 8, :]
            moved = pltpu.roll(blk, 8 * g, 1, stride=1, stride_axis=0)
            acc = acc + jnp.where(lag >= 8 * g, moved, 0.0)
        out_ref[pl.ds(v, 1), :] = jnp.sum(acc, axis=0, keepdims=True)
        return carry

    lax.fori_loop(0, vb, one, 0)


def convolve(picked, slip):
    v_local, k, width = picked.shape
    span = slip.shape[2]
    slip_t = jnp.swapaxes(slip, 1, 2)
    vb = min(V_BLOCK, v_local)
    return pl.pallas_call(
        conv_kernel,
        grid=(v_local // vb,),
        in_specs=[
            pl.BlockSpec((vb, span, k), lambda i: (i, 0, 0)),
            pl.BlockSpec((vb, k, width), lambda i: (i, 0, 0)),
        ],
        out_specs=pl.BlockSpec((vb, width), lambda i: (i, 0)),
        out_shape=jax.ShapeDtypeStruct((v_local, width), jnp.float32),
        scratch_shapes=[pltpu.VMEM((span, width), jnp.float32)],
    )(slip_t, picked)


def body(sgt, taps, moment, index, slip):
    n_handler = lax.axis_size("handler")
    me = lax.axis_index("handler")
    local_t = sgt.shape[0]
    local_j = local_t // DEC
    n_taps = taps.shape[0]
    halo = (n_taps - 1 + DEC - 1) // DEC
    lowpass = band_matrix(taps, local_t, local_j + halo)
    filtered = jnp.einsum("tj,tcp->jcp", lowpass, sgt, preferred_element_type=jnp.float32)
    partial = jnp.sum(moment[None, :, :] * filtered, axis=1)
    carried = lax.ppermute(partial[local_j:], "handler", [(i, i + 1) for i in range(n_handler - 1)])
    own = partial[:local_j]
    own = own.at[:halo].add(carried)
    green = own.astype(jnp.bfloat16).T
    piece = lax.all_gather(green, "handler", axis=1, tiled=True)
    length = piece.shape[0]
    v_local, k = index.shape
    flat_index = jnp.clip(index.reshape(-1), 0, length - 1)
    rows = jnp.take(piece, flat_index, axis=0)
    picked = rows.reshape(v_local, k, piece.shape[1])
    return convolve(picked, slip)


def solution(mesh):
    in_specs = (
        P(("site", "handler"), None, None),
        P(),
        P(),
        P("handler", None),
        P("handler", None, None),
    )
    out_specs = P(("site", "handler"), None)
    return jax.shard_map(body, mesh=mesh, in_specs=in_specs, out_specs=out_specs, check_vma=False)
```

profile of v0, /device:TPU:0, one launch (start us, length us, event | category | flops | bytes accessed | tf_op | source)
XLA Modules:
  0.0 132.6 jit_solution(8045771229032057363)
XLA Ops:
  6.5 0.0 all-gather.2.cloned.1.call-start
  6.5 2.1 %fusion.166 = (bf16[1]{0:T(256)(128)(2,1)}, bf16[1]{0:T(256)(128)(2,1)}, bf16[1]{0:T(256)(128)(2,1)}, bf16[1]{0:T(256)(128)(2,1)}, bf16[1]{0:T(256)(128)(2,1)}, ...) fusion(bf16[32]{0:T(256)(128)(2,1)} %param.8), kind=kLoop, calls=%fused_computation.177 | loop fusion | bytes 76 | tf_op jit(solution)/shard_map/slice | solution.py:18
  8.6 1.8 %fusion.167 = (bf16[1]{0:T(256)(128)(2,1)}, bf16[1]{0:T(256)(128)(2,1)}, bf16[1]{0:T(256)(128)(2,1)}, bf16[1]{0:T(256)(128)(2,1)}, bf16[1]{0:T(256)(128)(2,1)}, ...) fusion(bf16[32]{0:T(256)(128)(2,1)} %param.8), kind=kLoop, calls=%fused_computation.178 | loop fusion | bytes 52 | tf_op jit(solution)/shard_map/slice | solution.py:18
  10.4 0.0 copy-start.2
  10.5 0.0 copy-start.1
  10.5 24.4 %multiply_reduce_fusion = f32[72,2048]{1,0:T(8,128)S(1)} fusion(bf16[256,6,2048]{2,0,1:T(8,128)(2,1)} %param.7, f32[6,2048]{1,0:T(8,128)} %param.9, s32[72]{0:T(128)S(1)} %iota_multiply_fusion, bf16[]{:T(256)} %bitcast.32, bf16[]{:T(256)} %bitcast.31, bf16[]{:T(256)} %bitcast.30, bf16[]{:T(256)} %bitcast.29, bf16[]{:T(256)} %bitcast.28, bf16[]{:T(256)} %bitcast.27, ...), kind=kOutput, calls=%fused_computation.1 | convolution fusion | flops 455804928 | bytes 6930784 | tf_op jit(solution)/shard_map/tj,tcp->jcp/dot_general | solution.py:69
  34.9 2.4 %collective-permute-start = (f32[8,2048]{1,0:T(8,128)S(1)}, f32[8,2048]{1,0:T(8,128)S(1)}, u32[]{:S(2)}, u32[]{:S(2)}) collective-permute-start(f32[8,2048]{1,0:T(8,128)S(1)} %slice.161), channel_id=1, source_target_pairs={{0,1},{1,2},{2,3},{3,4},{4,5},{5,6},{6,7},{7,8},{8,9},{9,10},{10,1... | collective-permute-start | bytes 196616 | tf_op jit(solution)/shard_map/ppermute | solution.py:71
  37.3 0.8 collective-permute-done
  38.1 0.0 copy-start
  38.1 0.7 copy-done
  38.8 0.0 all-gather.2.cloned.1.call-update
  38.9 0.0 copy-done.2
  38.9 0.1 min.12
  39.0 0.0 copy-done.1
  39.0 1.6 %copy.7 = bf16[32,32,200]{1,2,0:T(8,128)(2,1)} copy(bf16[32,32,200]{2,1,0:T(8,128)(2,1)S(1)} %copy-done.1) | data formatting | bytes 819200 | tf_op args[4]
  40.6 54.0 %all-gather.2.cloned.1.call-done = bf16[2048,1024]{0,1:T(8,128)(2,1)} async-done(((bf16[2048,64]{0,1:T(8,128)(2,1)}), bf16[2048,1024]{0,1:T(8,128)(2,1)}) %all-gather.2.cloned.1.call-update) | async-done | bytes 4194320 | tf_op jit(solution)/shard_map/all_gather | solution.py:75
  94.6 6.4 %copy.8 = bf16[2048,1024]{1,0:T(8,128)(2,1)} copy(bf16[2048,1024]{0,1:T(8,128)(2,1)} %all-gather.2.cloned.1.call-done) | data formatting | bytes 8388608 | tf_op jit(solution)/shard_map/all_gather | solution.py:75
  101.1 7.7 %gather_fusion = bf16[1024,1024]{1,0:T(8,128)(2,1)S(1)} fusion(bf16[2048,1024]{1,0:T(8,128)(2,1)} %copy.8, s32[1024]{0:T(1024)S(1)} %broadcast_clamp_fusion.1), kind=kCustom, calls=%fused_computation | custom fusion | bytes 4198400 | tf_op jit(solution)/shard_map/jit(_take)/gather | solution.py:79
  108.8 1.6 %broadcast_select_fusion.picked_ref = bf16[32,32,1024]{2,1,0:T(8,128)(2,1)} fusion(bf16[32,32,1024]{2,1,0:T(8,128)(2,1)S(1)} %bitcast.42, pred[32,32]{1,0:T(8,128)(4,1)S(1)} %compare_and_fusion), kind=kLoop, calls=%fused_computation.2 | loop fusion | flops 1048576 | bytes 4195328 | tf_op jit(solution)/shard_map/jit(_take)/select_n | solution.py:79
  110.4 15.4 %shard_map.55 = f32[32,1024]{1,0:T(8,128)} custom-call(bf16[32,200,32]{2,1,0:T(8,128)(2,1)} %bitcast.43, bf16[32,32,1024]{2,1,0:T(8,128)(2,1)} %broadcast_select_fusion.picked_ref), custom_call_target="tpu_custom_call" | custom-call | tf_op jit(solution)/shard_map/pallas_call | solution.py:48
  (8 shorter events, 0.1 us)
Async XLA Ops:
  6.5 88.1 %all-gather.2.cloned.1.call-start = ((), (), s32[]{:S(2)}) async-start(), calls=%async_computation | async-start | bytes 4456448 | tf_op jit(solution)/shard_map/all_gather | solution.py:75
  10.4 28.4 %copy-start.2 = (s32[32,32]{1,0:T(8,128)S(1)}, s32[32,32]{1,0:T(8,128)}, u32[]{:S(2)}) copy-start(s32[32,32]{1,0:T(8,128)} %param.10) | copy-start | bytes 12292
  10.5 28.5 %copy-start.1 = (bf16[32,32,200]{2,1,0:T(8,128)(2,1)S(1)}, bf16[32,32,200]{2,1,0:T(8,128)(2,1)}, u32[]{:S(2)}) copy-start(bf16[32,32,200]{2,1,0:T(8,128)(2,1)} %param.11) | copy-start | bytes 1228804
  34.9 3.2 %collective-permute-start = (f32[8,2048]{1,0:T(8,128)S(1)}, f32[8,2048]{1,0:T(8,128)S(1)}, u32[]{:S(2)}, u32[]{:S(2)}) collective-permute-start(f32[8,2048]{1,0:T(8,128)S(1)} %slice.161), channel_id=1, source_target_pairs={{0,1},{1,2},{2,3},{3,4},{4,5},{5,6},{6,7},{7,8},{8,9},{9,10},{10,1... | collective-permute-start | bytes 196616 | tf_op jit(solution)/shard_map/ppermute | solution.py:71
  38.1 0.7 copy-start
Sparse Core Ops, SparseCore 0:
  39.0 55.5 all-gather.1
where the time goes:
time: 133 us
  waiting for transfers between devices  54.9 us (41%)
  matrix products  24.4 us (18%)
  local copies, waits for them, and re-layouts  20.4 us (15%)
  Pallas kernels  15.4 us (12%)
  between operations  13.5 us (10%)
  starting transfers between devices  2.36 us (2%)
  other arithmetic  1.67 us (1%)
    all_gather x1, waiting for transfers between devices, body(): piece = lax.all_gather(green, 'handler', axis=1, tiled=True)  54 us
    dot_general x1, matrix products, body(): jnp.einsum('tj,tcp->jcp', lowpass, sgt, preferred_element_type=jnp.float32)  24.4 us
    pallas_call x1, Pallas kernels, convolve(): pl.pallas_call(conv_kernel, grid=(v_local // vb,), in_specs=[pl.BlockSpec...  15.4 us
    gather x1, local copies, waits for them, and re-layouts, body(): rows = jnp.take(piece, flat_index, axis=0)  7.7 us
    all_gather x1, local copies, waits for them, and re-layouts, body(): piece = lax.all_gather(green, 'handler', axis=1, tiled=True)  6.44 us
    slice x2, local copies, waits for them, and re-layouts, band_matrix(): matrix = jnp.where(lag == which, taps[which], matrix)  3.89 us
  transfers between devices with their start and end apart: 2, of which 2 were waited for; matrix products, arithmetic and copies ran while one was open for 1% of the time, Pallas kernels for 0%

commit v1 on v0

--- a/solution.py
+++ b/solution.py
@@ -3,7 +3,7 @@
 from jax import lax
 from jax.experimental import pallas as pl
 from jax.experimental.pallas import tpu as pltpu
-from jax.sharding import PartitionSpec as P
+from jax.sharding import Mesh, PartitionSpec as P
 
 DEC = 4
 V_BLOCK = 8
@@ -59,8 +59,8 @@
 
 
 def body(sgt, taps, moment, index, slip):
-    n_handler = lax.axis_size("handler")
-    me = lax.axis_index("handler")
+    handler = ("chip", "core")
+    n_handler = lax.axis_size(handler)
     local_t = sgt.shape[0]
     local_j = local_t // DEC
     n_taps = taps.shape[0]
@@ -68,11 +68,13 @@
     lowpass = band_matrix(taps, local_t, local_j + halo)
     filtered = jnp.einsum("tj,tcp->jcp", lowpass, sgt, preferred_element_type=jnp.float32)
     partial = jnp.sum(moment[None, :, :] * filtered, axis=1)
-    carried = lax.ppermute(partial[local_j:], "handler", [(i, i + 1) for i in range(n_handler - 1)])
+    carried = lax.ppermute(partial[local_j:], handler, [(i, i + 1) for i in range(n_handler - 1)])
     own = partial[:local_j]
     own = own.at[:halo].add(carried)
-    green = own.astype(jnp.bfloat16).T
-    piece = lax.all_gather(green, "handler", axis=1, tiled=True)
+    green = own.astype(jnp.bfloat16)
+    across = lax.all_gather(green, "chip", axis=0)
+    both = lax.all_gather(across, "core", axis=1)
+    piece = both.reshape(-1, both.shape[-1]).T
     length = piece.shape[0]
     v_local, k = index.shape
     flat_index = jnp.clip(index.reshape(-1), 0, length - 1)
@@ -82,12 +84,15 @@
 
 
 def solution(mesh):
+    n_site, n_handler = mesh.devices.shape
+    split = Mesh(mesh.devices.reshape(n_site, n_handler // 2, 2), ("site", "chip", "core"))
+    points = ("site", "chip", "core")
     in_specs = (
-        P(("site", "handler"), None, None),
+        P(points, None, None),
         P(),
         P(),
-        P("handler", None),
-        P("handler", None, None),
+        P(("chip", "core"), None),
+        P(("chip", "core"), None, None),
     )
-    out_specs = P(("site", "handler"), None)
-    return jax.shard_map(body, mesh=mesh, in_specs=in_specs, out_specs=out_specs, check_vma=False)
+    out_specs = P(points, None)
+    return jax.shard_map(body, mesh=split, in_specs=in_specs, out_specs=out_specs, check_vma=False)

time: 133 us -> 146 us (1.098)
  waiting for transfers between devices: 54.9 us -> 67.3 us
    all_gather x1 -> x2, waiting for transfers between devices: 54 us -> 66.4 us  [the longest x1 54.4 us: body(): across = lax.all_gather(green, 'chip', axis=0)]
    all_gather x1 -> x0, local copies, waits for them, and re-layouts: 6.44 us -> none  [body(): piece = lax.all_gather(green, 'handler', axis=1, tiled=True)]
    reshape x0 -> x1, local copies, waits for them, and re-layouts: none -> 6.43 us  [body(): piece = both.reshape(-1, both.shape[-1]).T]
  transfers between devices with their start and end apart: 2 -> 3, of which waited for: 2 -> 3; matrix products, arithmetic and copies ran while one was open for 1% -> 1% of each run, Pallas kernels for 0% -> 0%
where the time goes in v1:
time: 146 us; the launch traced here: 145 us
  waiting for transfers between devices  67.3 us (46%)
  matrix products  24.3 us (17%)
  local copies, waits for them, and re-layouts  20.4 us (14%)
  Pallas kernels  15.4 us (11%)
  between operations  13.5 us (9%)
  starting transfers between devices  2.4 us (2%)
  other arithmetic  1.65 us (1%)
    all_gather x1, waiting for transfers between devices, body(): across = lax.all_gather(green, 'chip', axis=0)  54.4 us
    dot_general x1, matrix products, body(): jnp.einsum('tj,tcp->jcp', lowpass, sgt, preferred_element_type=jnp.float32)  24.3 us
    pallas_call x1, Pallas kernels, convolve(): pl.pallas_call(conv_kernel, grid=(v_local // vb,), in_specs=[pl.BlockSpec...  15.4 us
    all_gather x1, waiting for transfers between devices, body(): both = lax.all_gather(across, 'core', axis=1)  12 us
    gather x1, local copies, waits for them, and re-layouts, body(): rows = jnp.take(piece, flat_index, axis=0)  7.7 us
    reshape x1, local copies, waits for them, and re-layouts, body(): piece = both.reshape(-1, both.shape[-1]).T  6.43 us
    slice x2, local copies, waits for them, and re-layouts, band_matrix(): matrix = jnp.where(lag == which, taps[which], matrix)  3.91 us
  transfers between devices with their start and end apart: 3, of which 3 were waited for; matrix products, arithmetic and copies ran while one was open for 1% of the time, Pallas kernels for 0%

profile of v1, /device:TPU:0, one launch (start us, length us, event | category | flops | bytes accessed | tf_op | source)
XLA Modules:
  0.0 145.0 jit_solution(7759535380034219938)
XLA Ops:
  6.5 0.0 all-gather.5.cloned.1.call-start
  6.5 2.1 %fusion.166 = (bf16[1]{0:T(256)(128)(2,1)}, bf16[1]{0:T(256)(128)(2,1)}, bf16[1]{0:T(256)(128)(2,1)}, bf16[1]{0:T(256)(128)(2,1)}, bf16[1]{0:T(256)(128)(2,1)}, ...) fusion(bf16[32]{0:T(256)(128)(2,1)} %param.8), kind=kLoop, calls=%fused_computation.176 | loop fusion | bytes 76 | tf_op jit(solution)/shard_map/slice | solution.py:18
  8.6 1.8 %fusion.167 = (bf16[1]{0:T(256)(128)(2,1)}, bf16[1]{0:T(256)(128)(2,1)}, bf16[1]{0:T(256)(128)(2,1)}, bf16[1]{0:T(256)(128)(2,1)}, bf16[1]{0:T(256)(128)(2,1)}, ...) fusion(bf16[32]{0:T(256)(128)(2,1)} %param.8), kind=kLoop, calls=%fused_computation.177 | loop fusion | bytes 52 | tf_op jit(solution)/shard_map/slice | solution.py:18
  10.5 0.0 copy-start.2
  10.5 0.0 copy-start.1
  10.5 24.3 %multiply_reduce_fusion = f32[72,2048]{1,0:T(8,128)S(1)} fusion(bf16[256,6,2048]{2,0,1:T(8,128)(2,1)} %param.7, f32[6,2048]{1,0:T(8,128)} %param.9, s32[72]{0:T(128)S(1)} %iota_multiply_fusion, bf16[]{:T(256)} %bitcast.32, bf16[]{:T(256)} %bitcast.31, bf16[]{:T(256)} %bitcast.30, bf16[]{:T(256)} %bitcast.29, bf16[]{:T(256)} %bitcast.28, bf16[]{:T(256)} %bitcast.27, ...), kind=kOutput, calls=%fused_computation.1 | convolution fusion | flops 455804928 | bytes 6930784 | tf_op jit(solution)/shard_map/tj,tcp->jcp/dot_general | solution.py:69
  34.8 2.4 %collective-permute-start = (f32[8,2048]{1,0:T(8,128)S(1)}, f32[8,2048]{1,0:T(8,128)S(1)}, u32[]{:S(2)}, u32[]{:S(2)}) collective-permute-start(f32[8,2048]{1,0:T(8,128)S(1)} %slice.161), channel_id=1, source_target_pairs={{0,1},{1,2},{2,3},{3,4},{4,5},{5,6},{6,7},{7,8},{8,9},{9,10},{10,1... | collective-permute-start | bytes 196616 | tf_op jit(solution)/shard_map/ppermute | solution.py:71
  37.2 0.8 collective-permute-done
  38.1 0.0 copy-start
  38.1 0.7 copy-done
  38.8 0.0 all-gather.5.cloned.1.call-update
  38.8 0.0 all-gather.7.cloned.1.call-start
  38.9 54.4 %all-gather.5.cloned.1.call-done = bf16[512,2048]{1,0:T(8,128)(2,1)} async-done(((bf16[64,2048]{1,0:T(8,128)(2,1)}), bf16[512,2048]{1,0:T(8,128)(2,1)}) %all-gather.5.cloned.1.call-update) | async-done | bytes 2097168 | tf_op jit(solution)/shard_map/all_gather | solution.py:75
  93.3 0.0 all-gather.7.cloned.1.call-update
  93.3 0.0 copy-done.2
  93.3 0.1 min.12
  93.4 0.0 copy-done.1
  93.4 1.6 %copy.7 = bf16[32,32,200]{1,2,0:T(8,128)(2,1)} copy(bf16[32,32,200]{2,1,0:T(8,128)(2,1)S(1)} %copy-done.1) | data formatting | bytes 819200 | tf_op args[4]
  95.0 12.0 %all-gather.7.cloned.1.call-done = bf16[8,128,2048]{2,1,0:T(8,128)(2,1)} async-done(((bf16[8,64,2048]{2,1,0:T(8,128)(2,1)}), bf16[8,128,2048]{2,1,0:T(8,128)(2,1)}) %all-gather.7.cloned.1.call-update) | async-done | bytes 4194320 | tf_op jit(solution)/shard_map/all_gather | solution.py:76
  107.0 6.4 %copy.9 = bf16[1024,2048]{0,1:T(8,128)(2,1)} copy(bf16[1024,2048]{1,0:T(8,128)(2,1)} %bitcast.45) | data formatting | bytes 8388608 | tf_op jit(solution)/shard_map/reshape | solution.py:77
  113.5 7.7 %gather_fusion = bf16[1024,1024]{1,0:T(8,128)(2,1)S(1)} fusion(bf16[2048,1024]{1,0:T(8,128)(2,1)} %bitcast.42, s32[1024]{0:T(1024)S(1)} %broadcast_clamp_fusion.1), kind=kCustom, calls=%fused_computation | custom fusion | bytes 4198400 | tf_op jit(solution)/shard_map/jit(_take)/gather | solution.py:81
  121.2 1.6 %broadcast_select_fusion.picked_ref = bf16[32,32,1024]{2,1,0:T(8,128)(2,1)} fusion(bf16[32,32,1024]{2,1,0:T(8,128)(2,1)S(1)} %bitcast.43, pred[32,32]{1,0:T(8,128)(4,1)S(1)} %compare_and_fusion), kind=kLoop, calls=%fused_computation.2 | loop fusion | flops 1048576 | bytes 4195328 | tf_op jit(solution)/shard_map/jit(_take)/select_n | solution.py:81
  122.8 15.4 %shard_map.55 = f32[32,1024]{1,0:T(8,128)} custom-call(bf16[32,200,32]{2,1,0:T(8,128)(2,1)} %bitcast.44, bf16[32,32,1024]{2,1,0:T(8,128)(2,1)} %broadcast_select_fusion.picked_ref), custom_call_target="tpu_custom_call" | custom-call | tf_op jit(solution)/shard_map/pallas_call | solution.py:48
  (8 shorter events, 0.1 us)
Async XLA Ops:
  6.5 86.8 %all-gather.5.cloned.1.call-start = ((), (), s32[]{:S(2)}) async-start(), calls=%async_computation | async-start | bytes 2359296 | tf_op jit(solution)/shard_map/all_gather | solution.py:75
  10.5 82.9 %copy-start.2 = (s32[32,32]{1,0:T(8,128)S(1)}, s32[32,32]{1,0:T(8,128)}, u32[]{:S(2)}) copy-start(s32[32,32]{1,0:T(8,128)} %param.10) | copy-start | bytes 12292
  10.5 83.0 %copy-start.1 = (bf16[32,32,200]{2,1,0:T(8,128)(2,1)S(1)}, bf16[32,32,200]{2,1,0:T(8,128)(2,1)}, u32[]{:S(2)}) copy-start(bf16[32,32,200]{2,1,0:T(8,128)(2,1)} %param.11) | copy-start | bytes 1228804
  34.8 3.2 %collective-permute-start = (f32[8,2048]{1,0:T(8,128)S(1)}, f32[8,2048]{1,0:T(8,128)S(1)}, u32[]{:S(2)}, u32[]{:S(2)}) collective-permute-start(f32[8,2048]{1,0:T(8,128)S(1)} %slice.161), channel_id=1, source_target_pairs={{0,1},{1,2},{2,3},{3,4},{4,5},{5,6},{6,7},{7,8},{8,9},{9,10},{10,1... | collective-permute-start | bytes 196616 | tf_op jit(solution)/shard_map/ppermute | solution.py:71
  38.1 0.7 copy-start
  38.8 68.2 %all-gather.7.cloned.1.call-start = ((), (), s32[]{:S(2)}) async-start(), calls=%async_computation.1 | async-start | bytes 6291456 | tf_op jit(solution)/shard_map/all_gather | solution.py:76
Sparse Core Ops, SparseCore 0:
  38.9 54.3 all-gather.4
  94.8 12.1 all-gather.6

commit v2 on v0

--- a/solution.py
+++ b/solution.py
@@ -65,9 +65,10 @@
     local_j = local_t // DEC
     n_taps = taps.shape[0]
     halo = (n_taps - 1 + DEC - 1) // DEC
-    lowpass = band_matrix(taps, local_t, local_j + halo)
-    filtered = jnp.einsum("tj,tcp->jcp", lowpass, sgt, preferred_element_type=jnp.float32)
-    partial = jnp.sum(moment[None, :, :] * filtered, axis=1)
+    lowpass = lax.optimization_barrier(band_matrix(taps, local_t, local_j + halo))
+    by_component = jnp.transpose(sgt, (1, 0, 2))
+    filtered = jnp.einsum("tj,ctp->cjp", lowpass, by_component, preferred_element_type=jnp.float32)
+    partial = jnp.sum(moment[:, None, :] * filtered, axis=0)
     carried = lax.ppermute(partial[local_j:], "handler", [(i, i + 1) for i in range(n_handler - 1)])
     own = partial[:local_j]
     own = own.at[:halo].add(carried)

time: 133 us -> 133 us (level)
  other arithmetic: 1.67 us -> 22 us
  matrix products: 24.4 us -> 4.11 us
    select_n x0 -> x1, other arithmetic: none -> 20.3 us  [band_matrix(): matrix = jnp.where(lag == which, taps[which], matrix)]
    dot_general x1, matrix products: 24.4 us -> 4.11 us  [body(): jnp.einsum('tj,ctp->cjp', lowpass, by_component, preferred_element_type=j...]
where the time goes in v2:
time: 133 us
  waiting for transfers between devices  54.9 us (41%)
  other arithmetic  22 us (17%)
  local copies, waits for them, and re-layouts  20.4 us (15%)
  Pallas kernels  15.4 us (12%)
  between operations  13.5 us (10%)
  matrix products  4.11 us (3%)
  starting transfers between devices  2.36 us (2%)
    all_gather x1, waiting for transfers between devices, body(): piece = lax.all_gather(green, 'handler', axis=1, tiled=True)  54 us
    select_n x1, other arithmetic, band_matrix(): matrix = jnp.where(lag == which, taps[which], matrix)  20.3 us
    pallas_call x1, Pallas kernels, convolve(): pl.pallas_call(conv_kernel, grid=(v_local // vb,), in_specs=[pl.BlockSpec...  15.4 us
    gather x1, local copies, waits for them, and re-layouts, body(): rows = jnp.take(piece, flat_index, axis=0)  7.7 us
    all_gather x1, local copies, waits for them, and re-layouts, body(): piece = lax.all_gather(green, 'handler', axis=1, tiled=True)  6.44 us
    dot_general x1, matrix products, body(): jnp.einsum('tj,ctp->cjp', lowpass, by_component, preferred_element_type=j...  4.11 us
    slice x2, local copies, waits for them, and re-layouts, band_matrix(): matrix = jnp.where(lag == which, taps[which], matrix)  3.89 us
  transfers between devices with their start and end apart: 2, of which 2 were waited for; matrix products, arithmetic and copies ran while one was open for 1% of the time, Pallas kernels for 0%

profile of v2, /device:TPU:0, one launch (start us, length us, event | category | flops | bytes accessed | tf_op | source)
XLA Modules:
  0.0 132.7 jit_solution(9289883219778101889)
XLA Ops:
  6.5 0.0 all-gather.2.cloned.1.call-start
  6.5 2.1 %fusion.70 = (bf16[1]{0:T(256)(128)(2,1)}, bf16[1]{0:T(256)(128)(2,1)}, bf16[1]{0:T(256)(128)(2,1)}, bf16[1]{0:T(256)(128)(2,1)}, bf16[1]{0:T(256)(128)(2,1)}, /...) fusion(bf16[32]{0:T(256)(128)(2,1)} %param.8), kind=kLoop, calls=%fused_computation.80 | loop fusion | bytes 76 | tf_op jit(solution)/shard_map/slice | solution.py:18
  8.6 1.8 %fusion.71 = (bf16[1]{0:T(256)(128)(2,1)}, bf16[1]{0:T(256)(128)(2,1)}, bf16[1]{0:T(256)(128)(2,1)}, bf16[1]{0:T(256)(128)(2,1)}, bf16[1]{0:T(256)(128)(2,1)}, /...) fusion(bf16[32]{0:T(256)(128)(2,1)} %param.8), kind=kLoop, calls=%fused_computation.81 | loop fusion | bytes 52 | tf_op jit(solution)/shard_map/slice | solution.py:18
  10.4 20.3 %fusion.36 = bf16[256,72]{0,1:T(8,128)(2,1)S(1)} fusion(s32[72]{0:T(128)S(1)} %iota_multiply_fusion, bf16[]{:T(256)} %bitcast.32, bf16[]{:T(256)} %bitcast.31, bf16[]{:T(256)} %bitcast.30, bf16[]{:T(256)} %bitcast.29, bf16[]{:T(256)} %bitcast.28, bf16[]{:T(256)} %bitcast.27, bf16[]{:T(256)} %bitcast.26, bf16[]{:T(256)} %bitcast.25, bf16[]{:T(256)} %bitcast.24, ...), kind=kLoop, calls=%fused_computation.39 | loop fusion | flops 1198080 | bytes 37216 | tf_op jit(solution)/shard_map/jit(_where)/select_n | solution.py:18
  30.8 0.0 copy-start.2
  30.8 0.0 copy-start.1
  30.8 4.1 %multiply_reduce_fusion = f32[72,2048]{1,0:T(8,128)S(1)} fusion(bf16[256,6,2048]{2,0,1:T(8,128)(2,1)} %param.7, f32[6,2048]{1,0:T(8,128)} %param.9, bf16[256,72]{0,1:T(8,128)(2,1)S(1)} %fusion.36), kind=kOutput, calls=%fused_computation.3 | convolution fusion | flops 454606848 | bytes 6967296 | tf_op jit(solution)/shard_map/tj,ctp->cjp/dot_general | solution.py:70
  34.9 2.4 %collective-permute-start = (f32[8,2048]{1,0:T(8,128)S(1)}, f32[8,2048]{1,0:T(8,128)S(1)}, u32[]{:S(2)}, u32[]{:S(2)}) collective-permute-start(f32[8,2048]{1,0:T(8,128)S(1)} %slice.161), channel_id=1, source_target_pairs={{0,1},{1,2},{2,3},{3,4},{4,5},{5,6},{6,7},{7,8},{8,9},{9,10},{10,1... | collective-permute-start | bytes 196616 | tf_op jit(solution)/shard_map/ppermute | solution.py:72
  37.3 0.8 collective-permute-done
  38.2 0.0 copy-start
  38.2 0.7 copy-done
  38.9 0.0 all-gather.2.cloned.1.call-update
  38.9 0.0 copy-done.2
  38.9 0.1 min.12
  39.0 0.0 copy-done.1
  39.0 1.6 %copy.7 = bf16[32,32,200]{1,2,0:T(8,128)(2,1)} copy(bf16[32,32,200]{2,1,0:T(8,128)(2,1)S(1)} %copy-done.1) | data formatting | bytes 819200 | tf_op args[4]
  40.6 54.0 %all-gather.2.cloned.1.call-done = bf16[2048,1024]{0,1:T(8,128)(2,1)} async-done(((bf16[2048,64]{0,1:T(8,128)(2,1)}), bf16[2048,1024]{0,1:T(8,128)(2,1)}) %all-gather.2.cloned.1.call-update) | async-done | bytes 4194320 | tf_op jit(solution)/shard_map/all_gather | solution.py:76
  94.7 6.4 %copy.8 = bf16[2048,1024]{1,0:T(8,128)(2,1)} copy(bf16[2048,1024]{0,1:T(8,128)(2,1)} %all-gather.2.cloned.1.call-done) | data formatting | bytes 8388608 | tf_op jit(solution)/shard_map/all_gather | solution.py:76
  101.1 7.7 %gather_fusion = bf16[1024,1024]{1,0:T(8,128)(2,1)S(1)} fusion(bf16[2048,1024]{1,0:T(8,128)(2,1)} %copy.8, s32[1024]{0:T(1024)S(1)} %broadcast_clamp_fusion.1), kind=kCustom, calls=%fused_computation | custom fusion | bytes 4198400 | tf_op jit(solution)/shard_map/jit(_take)/gather | solution.py:80
  108.8 1.6 %broadcast_select_fusion.picked_ref = bf16[32,32,1024]{2,1,0:T(8,128)(2,1)} fusion(bf16[32,32,1024]{2,1,0:T(8,128)(2,1)S(1)} %bitcast.46, pred[32,32]{1,0:T(8,128)(4,1)S(1)} %compare_and_fusion), kind=kLoop, calls=%fused_computation.4 | loop fusion | flops 1048576 | bytes 4195328 | tf_op jit(solution)/shard_map/jit(_take)/select_n | solution.py:80
  110.4 15.4 %shard_map.55 = f32[32,1024]{1,0:T(8,128)} custom-call(bf16[32,200,32]{2,1,0:T(8,128)(2,1)} %bitcast.47, bf16[32,32,1024]{2,1,0:T(8,128)(2,1)} %broadcast_select_fusion.picked_ref), custom_call_target="tpu_custom_call" | custom-call | tf_op jit(solution)/shard_map/pallas_call | solution.py:48
  (8 shorter events, 0.1 us)
Async XLA Ops:
  6.5 88.1 %all-gather.2.cloned.1.call-start = ((), (), s32[]{:S(2)}) async-start(), calls=%async_computation | async-start | bytes 4456448 | tf_op jit(solution)/shard_map/all_gather | solution.py:76
  30.8 8.1 %copy-start.2 = (s32[32,32]{1,0:T(8,128)S(1)}, s32[32,32]{1,0:T(8,128)}, u32[]{:S(2)}) copy-start(s32[32,32]{1,0:T(8,128)} %param.10) | copy-start | bytes 12292
  30.8 8.2 %copy-start.1 = (bf16[32,32,200]{2,1,0:T(8,128)(2,1)S(1)}, bf16[32,32,200]{2,1,0:T(8,128)(2,1)}, u32[]{:S(2)}) copy-start(bf16[32,32,200]{2,1,0:T(8,128)(2,1)} %param.11) | copy-start | bytes 1228804
  34.9 3.2 %collective-permute-start = (f32[8,2048]{1,0:T(8,128)S(1)}, f32[8,2048]{1,0:T(8,128)S(1)}, u32[]{:S(2)}, u32[]{:S(2)}) collective-permute-start(f32[8,2048]{1,0:T(8,128)S(1)} %slice.161), channel_id=1, source_target_pairs={{0,1},{1,2},{2,3},{3,4},{4,5},{5,6},{6,7},{7,8},{8,9},{9,10},{10,1... | collective-permute-start | bytes 196616 | tf_op jit(solution)/shard_map/ppermute | solution.py:72
  38.2 0.7 copy-start
Sparse Core Ops, SparseCore 0:
  39.0 55.5 all-gather.1

commit v3 on v2

--- a/solution.py
+++ b/solution.py
@@ -10,13 +10,13 @@
 
 
 def band_matrix(taps, rows, cols):
-    row_ids = lax.broadcasted_iota(jnp.int32, (rows, cols), 0)
-    col_ids = lax.broadcasted_iota(jnp.int32, (rows, cols), 1)
-    lag = DEC * col_ids - row_ids
-    matrix = jnp.zeros((rows, cols), jnp.bfloat16)
-    for which in range(taps.shape[0]):
-        matrix = jnp.where(lag == which, taps[which], matrix)
-    return matrix
+    n_taps = taps.shape[0]
+    row_ids = lax.broadcasted_iota(jnp.int32, (rows, cols, n_taps), 0)
+    col_ids = lax.broadcasted_iota(jnp.int32, (rows, cols, n_taps), 1)
+    tap_ids = lax.broadcasted_iota(jnp.int32, (rows, cols, n_taps), 2)
+    hit = DEC * col_ids - row_ids == tap_ids
+    picked = jnp.where(hit, taps.astype(jnp.float32)[None, None, :], 0.0)
+    return jnp.sum(picked, axis=2).astype(jnp.bfloat16)
 
 
 def conv_kernel(slip_ref, picked_ref, out_ref, spread_ref):

time: 133 us -> 110 us (0.83)
  other arithmetic: 22 us -> 3.44 us
  local copies, waits for them, and re-layouts: 20.4 us -> 16.5 us
    select_n x1 -> x0, other arithmetic: 20.3 us -> none  [band_matrix(): matrix = jnp.where(lag == which, taps[which], matrix)]
    slice x2 -> x0, local copies, waits for them, and re-layouts: 3.89 us -> none  [band_matrix(): matrix = jnp.where(lag == which, taps[which], matrix)]
  transfers between devices with their start and end apart: 2 -> 2, of which waited for: 2 -> 2; matrix products, arithmetic and copies ran while one was open for 1% -> 2% of each run, Pallas kernels for 0% -> 0%
where the time goes in v3:
time: 110 us
  waiting for transfers between devices  54.9 us (50%)
  local copies, waits for them, and re-layouts  16.5 us (15%)
  Pallas kernels  15.4 us (14%)
  between operations  13.5 us (12%)
  matrix products  4.11 us (4%)
  other arithmetic  3.44 us (3%)
  starting transfers between devices  2.36 us (2%)
    all_gather x1, waiting for transfers between devices, body(): piece = lax.all_gather(green, 'handler', axis=1, tiled=True)  54 us
    pallas_call x1, Pallas kernels, convolve(): pl.pallas_call(conv_kernel, grid=(v_local // vb,), in_specs=[pl.BlockSpec...  15.4 us
    gather x1, local copies, waits for them, and re-layouts, body(): rows = jnp.take(piece, flat_index, axis=0)  7.7 us
    all_gather x1, local copies, waits for them, and re-layouts, body(): piece = lax.all_gather(green, 'handler', axis=1, tiled=True)  6.41 us
    dot_general x1, matrix products, body(): jnp.einsum('tj,ctp->cjp', lowpass, by_component, preferred_element_type=j...  4.11 us
    ppermute x1, starting transfers between devices, body(): lax.ppermute(partial[local_j:], 'handler', [(i, i + 1) for i in range(n_h...  2.36 us
    unnamed x7, local copies, waits for them, and re-layouts  2.31 us
  transfers between devices with their start and end apart: 2, of which 2 were waited for; matrix products, arithmetic and copies ran while one was open for 2% of the time, Pallas kernels for 0%

profile of v3, /device:TPU:0, one launch (start us, length us, event | category | flops | bytes accessed | tf_op | source)
XLA Modules:
  0.0 110.2 jit_solution(14667496574559550917)
XLA Ops:
  6.5 0.0 all-gather.2.cloned.1.call-start
  6.5 0.7 convert_element_type.9
  7.2 1.1 %select_reduce_fusion = bf16[256,72]{0,1:T(8,128)(2,1)S(1)} fusion(f32[32]{0:T(128)S(1)} %convert_element_type.9, s32[72]{0:T(128)S(1)} %iota_multiply_fusion), kind=kLoop, calls=%fused_computation.4 | loop fusion | flops 2340864 | bytes 37280 | tf_op jit(solution)/shard_map/reduce_sum | solution.py:19
  8.3 0.0 copy-start.2
  8.3 0.0 copy-start.1
  8.4 4.1 %multiply_reduce_fusion = f32[72,2048]{1,0:T(8,128)S(1)} fusion(bf16[256,6,2048]{2,0,1:T(8,128)(2,1)} %param.7, f32[6,2048]{1,0:T(8,128)} %param.9, bf16[256,72]{0,1:T(8,128)(2,1)S(1)} %select_reduce_fusion), kind=kOutput, calls=%fused_computation.3 | convolution fusion | flops 454606848 | bytes 6967296 | tf_op jit(solution)/shard_map/tj,ctp->cjp/dot_general | solution.py:70
  12.5 2.4 %collective-permute-start = (f32[8,2048]{1,0:T(8,128)S(1)}, f32[8,2048]{1,0:T(8,128)S(1)}, u32[]{:S(2)}, u32[]{:S(2)}) collective-permute-start(f32[8,2048]{1,0:T(8,128)S(1)} %slice.33), channel_id=1, source_target_pairs={{0,1},{1,2},{2,3},{3,4},{4,5},{5,6},{6,7},{7,8},{8,9},{9,10},{10,1... | collective-permute-start | bytes 196616 | tf_op jit(solution)/shard_map/ppermute | solution.py:72
  14.9 0.8 collective-permute-done
  15.7 0.0 copy-start
  15.8 0.7 copy-done
  16.4 0.0 all-gather.2.cloned.1.call-update
  16.5 0.0 copy-done.2
  16.5 0.1 min.12
  16.6 0.0 copy-done.1
  16.6 1.6 %copy.9 = bf16[32,32,200]{1,2,0:T(8,128)(2,1)} copy(bf16[32,32,200]{2,1,0:T(8,128)(2,1)S(1)} %copy-done.1) | data formatting | bytes 819200 | tf_op args[4]
  18.2 54.0 %all-gather.2.cloned.1.call-done = bf16[2048,1024]{0,1:T(8,128)(2,1)} async-done(((bf16[2048,64]{0,1:T(8,128)(2,1)}), bf16[2048,1024]{0,1:T(8,128)(2,1)}) %all-gather.2.cloned.1.call-update) | async-done | bytes 4194320 | tf_op jit(solution)/shard_map/all_gather | solution.py:76
  72.2 6.4 %copy.10 = bf16[2048,1024]{1,0:T(8,128)(2,1)} copy(bf16[2048,1024]{0,1:T(8,128)(2,1)} %all-gather.2.cloned.1.call-done) | data formatting | bytes 8388608 | tf_op jit(solution)/shard_map/all_gather | solution.py:76
  78.6 7.7 %gather_fusion = bf16[1024,1024]{1,0:T(8,128)(2,1)S(1)} fusion(bf16[2048,1024]{1,0:T(8,128)(2,1)} %copy.10, s32[1024]{0:T(1024)S(1)} %broadcast_clamp_fusion.1), kind=kCustom, calls=%fused_computation | custom fusion | bytes 4198400 | tf_op jit(solution)/shard_map/jit(_take)/gather | solution.py:80
  86.3 1.6 %broadcast_select_fusion.picked_ref = bf16[32,32,1024]{2,1,0:T(8,128)(2,1)} fusion(bf16[32,32,1024]{2,1,0:T(8,128)(2,1)S(1)} %bitcast.14, pred[32,32]{1,0:T(8,128)(4,1)S(1)} %compare_and_fusion), kind=kLoop, calls=%fused_computation.6 | loop fusion | flops 1048576 | bytes 4195328 | tf_op jit(solution)/shard_map/jit(_take)/select_n | solution.py:80
  87.9 15.4 %shard_map.55 = f32[32,1024]{1,0:T(8,128)} custom-call(bf16[32,200,32]{2,1,0:T(8,128)(2,1)} %bitcast.15, bf16[32,32,1024]{2,1,0:T(8,128)(2,1)} %broadcast_select_fusion.picked_ref), custom_call_target="tpu_custom_call" | custom-call | tf_op jit(solution)/shard_map/pallas_call | solution.py:48
  (8 shorter events, 0.1 us)
Async XLA Ops:
  6.5 65.7 %all-gather.2.cloned.1.call-start = ((), (), s32[]{:S(2)}) async-start(), calls=%async_computation | async-start | bytes 4456448 | tf_op jit(solution)/shard_map/all_gather | solution.py:76
  8.3 8.1 %copy-start.2 = (s32[32,32]{1,0:T(8,128)S(1)}, s32[32,32]{1,0:T(8,128)}, u32[]{:S(2)}) copy-start(s32[32,32]{1,0:T(8,128)} %param.10) | copy-start | bytes 12292
  8.3 8.2 %copy-start.1 = (bf16[32,32,200]{2,1,0:T(8,128)(2,1)S(1)}, bf16[32,32,200]{2,1,0:T(8,128)(2,1)}, u32[]{:S(2)}) copy-start(bf16[32,32,200]{2,1,0:T(8,128)(2,1)} %param.11) | copy-start | bytes 1228804
  12.5 3.3 %collective-permute-start = (f32[8,2048]{1,0:T(8,128)S(1)}, f32[8,2048]{1,0:T(8,128)S(1)}, u32[]{:S(2)}, u32[]{:S(2)}) collective-permute-start(f32[8,2048]{1,0:T(8,128)S(1)} %slice.33), channel_id=1, source_target_pairs={{0,1},{1,2},{2,3},{3,4},{4,5},{5,6},{6,7},{7,8},{8,9},{9,10},{10,1... | collective-permute-start | bytes 196616 | tf_op jit(solution)/shard_map/ppermute | solution.py:72
  15.7 0.7 copy-start
Sparse Core Ops, SparseCore 0:
  16.6 55.5 all-gather.1

commit v4 on v3

--- a/solution.py
+++ b/solution.py
@@ -58,31 +58,84 @@
     )(slip_t, picked)
 
 
-def body(sgt, taps, moment, index, slip):
-    n_handler = lax.axis_size("handler")
+def ring_order(devices):
+    try:
+        keys = [(tuple(d.coords), int(d.core_on_chip)) for d in devices]
+    except AttributeError:
+        return list(range(len(devices)))
+    chips = sorted({c for c, _ in keys})
+    dims = [a for a in range(len(chips[0])) if len({c[a] for c in chips}) > 1]
+    if len(dims) == 2:
+        dims.sort(key=lambda a: len({c[a] for c in chips}))
+        slow, fast = dims
+        lanes = sorted({c[slow] for c in chips})
+        ordered = []
+        for i, lane in enumerate(lanes):
+            row = sorted((c for c in chips if c[slow] == lane), key=lambda c: c[fast])
+            ordered += row if i % 2 == 0 else row[::-1]
+        chips = ordered
+    order = []
+    for chip in chips:
+        order += sorted((i for i, (c, _) in enumerate(keys) if c == chip), key=lambda i: keys[i][1])
+    return order
+
+
+def ring_gather(block, ring):
+    n = len(ring)
+    position = [0] * n
+    for i, h in enumerate(ring):
+        position[h] = i
+    ring_ids = jnp.asarray(ring, jnp.int32)
     me = lax.axis_index("handler")
-    local_t = sgt.shape[0]
-    local_j = local_t // DEC
-    n_taps = taps.shape[0]
-    halo = (n_taps - 1 + DEC - 1) // DEC
-    lowpass = lax.optimization_barrier(band_matrix(taps, local_t, local_j + halo))
-    by_component = jnp.transpose(sgt, (1, 0, 2))
-    filtered = jnp.einsum("tj,ctp->cjp", lowpass, by_component, preferred_element_type=jnp.float32)
-    partial = jnp.sum(moment[:, None, :] * filtered, axis=0)
-    carried = lax.ppermute(partial[local_j:], "handler", [(i, i + 1) for i in range(n_handler - 1)])
-    own = partial[:local_j]
-    own = own.at[:halo].add(carried)
-    green = own.astype(jnp.bfloat16).T
-    piece = lax.all_gather(green, "handler", axis=1, tiled=True)
-    length = piece.shape[0]
-    v_local, k = index.shape
-    flat_index = jnp.clip(index.reshape(-1), 0, length - 1)
-    rows = jnp.take(piece, flat_index, axis=0)
-    picked = rows.reshape(v_local, k, piece.shape[1])
-    return convolve(picked, slip)
+    mine = jnp.asarray(position, jnp.int32)[me]
+    ahead = [(ring[i], ring[(i + 1) % n]) for i in range(n)]
+    behind = [(ring[(i + 1) % n], ring[i]) for i in range(n)]
+    n_ahead = n // 2
+    n_behind = n - 1 - n_ahead
+    out = jnp.zeros((n,) + block.shape, block.dtype)
+    out = lax.dynamic_update_index_in_dim(out, block, me, 0)
+    from_behind = block
+    from_ahead = block
+    for step in range(1, n_ahead + 1):
+        from_behind = lax.ppermute(from_behind, "handler", ahead)
+        source = ring_ids[(mine - step) % n]
+        out = lax.dynamic_update_index_in_dim(out, from_behind, source, 0)
+        if step <= n_behind:
+            from_ahead = lax.ppermute(from_ahead, "handler", behind)
+            source = ring_ids[(mine + step) % n]
+            out = lax.dynamic_update_index_in_dim(out, from_ahead, source, 0)
+    return out
+
+
+def make_body(ring):
+    def body(sgt, taps, moment, index, slip):
+        n_handler = lax.axis_size("handler")
+        local_t = sgt.shape[0]
+        local_j = local_t // DEC
+        n_taps = taps.shape[0]
+        halo = (n_taps - 1 + DEC - 1) // DEC
+        lowpass = lax.optimization_barrier(band_matrix(taps, local_t, local_j + halo))
+        by_component = jnp.transpose(sgt, (1, 0, 2))
+        filtered = jnp.einsum("tj,ctp->cjp", lowpass, by_component, preferred_element_type=jnp.float32)
+        partial = jnp.sum(moment[:, None, :] * filtered, axis=0)
+        carried = lax.ppermute(partial[local_j:], "handler", [(i, i + 1) for i in range(n_handler - 1)])
+        own = partial[:local_j]
+        own = own.at[:halo].add(carried)
+        green = own.astype(jnp.bfloat16)
+        stacked = ring_gather(green, ring)
+        piece = stacked.reshape(-1, stacked.shape[-1]).T
+        length = piece.shape[0]
+        v_local, k = index.shape
+        flat_index = jnp.clip(index.reshape(-1), 0, length - 1)
+        rows = jnp.take(piece, flat_index, axis=0)
+        picked = rows.reshape(v_local, k, piece.shape[1])
+        return convolve(picked, slip)
+
+    return body
 
 
 def solution(mesh):
+    ring = ring_order(list(mesh.devices[0]))
     in_specs = (
         P(("site", "handler"), None, None),
         P(),
@@ -91,4 +144,4 @@
         P("handler", None, None),
     )
     out_specs = P(("site", "handler"), None)
-    return jax.shard_map(body, mesh=mesh, in_specs=in_specs, out_specs=out_specs, check_vma=False)
+    return jax.shard_map(make_body(ring), mesh=mesh, in_specs=in_specs, out_specs=out_specs, check_vma=False)

time: 110 us -> 131 us (1.19)
  waiting for transfers between devices: 54.9 us -> 20.4 us
  between operations: 13.5 us -> 38.7 us
  local copies, waits for them, and re-layouts: 16.5 us -> 31.3 us
  starting transfers between devices: 2.36 us -> 17.1 us
    all_gather x1 -> x0, waiting for transfers between devices: 54 us -> none  [body(): piece = lax.all_gather(green, 'handler', axis=1, tiled=True)]
    ppermute x0 -> x15, waiting for transfers between devices: none -> 20.4 us  [the longest x8 20.4 us: ring_gather(): from_behind = lax.ppermute(from_behind, 'handler', ahead)]
    ppermute x0 -> x15, starting transfers between devices: none -> 14.7 us  [the longest x7 12 us: ring_gather(): from_ahead = lax.ppermute(from_ahead, 'handler', behind)]
    dynamic_update_slice x0 -> x16, local copies, waits for them, and re-layouts: none -> 11.6 us  [the longest x8 5.83 us: ring_gather(): out = lax.dynamic_update_index_in_dim(out, from_behind, source, 0)]
    reshape x0 -> x1, local copies, waits for them, and re-layouts: none -> 6.42 us  [body(): piece = stacked.reshape(-1, stacked.shape[-1]).T]
    all_gather x1 -> x0, local copies, waits for them, and re-layouts: 6.41 us -> none  [body(): piece = lax.all_gather(green, 'handler', axis=1, tiled=True)]
    broadcast_in_dim x0 -> x1, local copies, waits for them, and re-layouts: none -> 2.48 us  [ring_gather(): out = jnp.zeros((n,) + block.shape, block.dtype)]
    dynamic_slice x0 -> x2, local copies, waits for them, and re-layouts: none -> 1.36 us  [the longest x1 0.77 us: ring_gather(): source = ring_ids[(mine - step) % n]]
  transfers between devices with their start and end apart: 2 -> 16, of which waited for: 2 -> 8; matrix products, arithmetic and copies ran while one was open for 2% -> 13% of each run, Pallas kernels for 0% -> 0%
where the time goes in v4:
time: 131 us; the launch traced here: 130 us
  between operations  38.7 us (30%)
  local copies, waits for them, and re-layouts  31.3 us (24%)
  waiting for transfers between devices  20.4 us (16%)
  starting transfers between devices  17.1 us (13%)
  Pallas kernels  15.4 us (12%)
  matrix products  4.06 us (3%)
  other arithmetic  3.45 us (3%)
    ppermute x8, waiting for transfers between devices, ring_gather(): from_behind = lax.ppermute(from_behind, 'handler', ahead)  20.4 us
    pallas_call x1, Pallas kernels, convolve(): pl.pallas_call(conv_kernel, grid=(v_local // vb,), in_specs=[pl.BlockSpec...  15.4 us
    ppermute x7, starting transfers between devices, ring_gather(): from_ahead = lax.ppermute(from_ahead, 'handler', behind)  12 us
    gather x1, local copies, waits for them, and re-layouts, body(): rows = jnp.take(piece, flat_index, axis=0)  7.7 us
    reshape x1, local copies, waits for them, and re-layouts, body(): piece = stacked.reshape(-1, stacked.shape[-1]).T  6.42 us
    dynamic_update_slice x8, local copies, waits for them, and re-layouts, ring_gather(): out = lax.dynamic_update_index_in_dim(out, from_behind, source, 0)  5.83 us
    dynamic_update_slice x7, local copies, waits for them, and re-layouts, ring_gather(): out = lax.dynamic_update_index_in_dim(out, from_ahead, source, 0)  5.05 us
    dot_general x1, matrix products, body(): jnp.einsum('tj,ctp->cjp', lowpass, by_component, preferred_element_type=j...  4.06 us
  transfers between devices with their start and end apart: 16, of which 8 were waited for; matrix products, arithmetic and copies ran while one was open for 13% of the time, Pallas kernels for 0%

profile of v4, /device:TPU:0, one launch (start us, length us, event | category | flops | bytes accessed | tf_op | source)
XLA Modules:
  0.0 130.3 jit_solution(1795069395234749263)
XLA Ops:
  0.0 0.7 convert_element_type.9
  0.7 1.1 select_reduce_fusion
  1.8 4.1 %multiply_reduce_fusion = f32[72,2048]{1,0:T(8,128)S(1)} fusion(bf16[256,6,2048]{2,0,1:T(8,128)(2,1)} %param.9, f32[6,2048]{1,0:T(8,128)} %param.11, bf16[256,72]{0,1:T(8,128)(2,1)S(1)} %select_reduce_fusion), kind=kOutput, calls=%fused_computation.3 | convolution fusion | flops 454606848 | bytes 6967296 | tf_op jit(solution)/shard_map/tj,ctp->cjp/dot_general | solution.py:119
  5.9 2.4 %collective-permute-start = (f32[8,2048]{1,0:T(8,128)S(1)}, f32[8,2048]{1,0:T(8,128)S(1)}, u32[]{:S(2)}, u32[]{:S(2)}) collective-permute-start(f32[8,2048]{1,0:T(8,128)S(1)} %slice.33), channel_id=1, source_target_pairs={{0,1},{1,2},{2,3},{3,4},{4,5},{5,6},{6,7},{7,8},{8,9},{9,10},{10,1... | collective-permute-start | bytes 196616 | tf_op jit(solution)/shard_map/ppermute | solution.py:121
  8.3 0.0 copy-done.2
  8.3 0.1 min.12
  8.4 0.0 copy-done.3
  8.4 0.6 dynamic_slice.48
  19.0 0.0 copy-done.1
  19.0 0.8 fusion.6
  38.9 0.0 copy-done
  38.9 1.6 %copy.26 = bf16[32,32,200]{1,2,0:T(8,128)(2,1)} copy(bf16[32,32,200]{2,1,0:T(8,128)(2,1)S(1)} %copy-done) | data formatting | bytes 819200 | tf_op args[4]
  50.0 0.0 collective-permute-done
  50.0 2.7 %collective-permute-start.1 = (bf16[64,2048]{1,0:T(8,128)(2,1)S(1)}, bf16[64,2048]{1,0:T(8,128)(2,1)S(1)}, u32[]{:S(2)}, u32[]{:S(2)}) collective-permute-start(bf16[64,2048]{1,0:T(8,128)(2,1)S(1)} %fusion.4), channel_id=1, source_target_pairs={{0,1},{1,4},{4,5},{5,8},{8,9},{9,12},{12,13},{13,14},{14,15},{15,1... | collective-permute-start | bytes 786440 | tf_op jit(solution)/shard_map/ppermute | solution.py:100
  52.7 1.2 collective-permute-start.2
  53.9 2.5 %broadcast_in_dim.77 = bf16[16,64,2048]{2,1,0:T(8,128)(2,1)} broadcast(bf16[]{:T(256)} %constant.185.clone.1), dimensions={} | broadcast | bytes 4194306 | tf_op jit(solution)/shard_map/broadcast_in_dim | solution.py:95
  56.4 0.7 bitcast_dynamic-update-slice_fusion.15
  57.1 0.8 collective-permute-done.1
  57.9 0.0 collective-permute-start.3
  57.9 0.0 collective-permute-done.2
  57.9 1.8 %collective-permute-start.4 = (bf16[64,2048]{1,0:T(8,128)(2,1)S(1)}, bf16[64,2048]{1,0:T(8,128)(2,1)S(1)}, u32[]{:S(2)}, u32[]{:S(2)}) collective-permute-start(bf16[64,2048]{1,0:T(8,128)(2,1)S(1)} %collective-permute-done.2), channel_id=1, source_target_pairs={{1,0},{4,1},{5,4},{8,5},{9,8},{12,9},{13,12},{14,13},{15,14},{10,1... | collective-permute-start | bytes 786440 | tf_op jit(solution)/shard_map/ppermute | solution.py:104
  59.7 0.7 bitcast_dynamic-update-slice_fusion.14
  60.4 0.7 bitcast_dynamic-update-slice_fusion.13
  61.1 2.5 %collective-permute-done.3 = bf16[64,2048]{1,0:T(8,128)(2,1)S(1)} collective-permute-done((bf16[64,2048]{1,0:T(8,128)(2,1)S(1)}, bf16[64,2048]{1,0:T(8,128)(2,1)S(1)}, u32[]{:S(2)}, u32[]{:S(2)}) %collective-permute-start.3) | collective-permute-done | bytes 262176 | tf_op jit(solution)/shard_map/ppermute | solution.py:100
  63.7 0.0 collective-permute-start.5
  63.7 0.0 collective-permute-done.4
  63.7 1.8 %collective-permute-start.6 = (bf16[64,2048]{1,0:T(8,128)(2,1)S(1)}, bf16[64,2048]{1,0:T(8,128)(2,1)S(1)}, u32[]{:S(2)}, u32[]{:S(2)}) collective-permute-start(bf16[64,2048]{1,0:T(8,128)(2,1)S(1)} %collective-permute-done.4), channel_id=1, source_target_pairs={{1,0},{4,1},{5,4},{8,5},{9,8},{12,9},{13,12},{14,13},{15,14},{10,1... | collective-permute-start | bytes 786440 | tf_op jit(solution)/shard_map/ppermute | solution.py:104
  65.5 0.7 bitcast_dynamic-update-slice_fusion.12
  66.2 0.7 bitcast_dynamic-update-slice_fusion.11
  66.9 2.5 %collective-permute-done.5 = bf16[64,2048]{1,0:T(8,128)(2,1)S(1)} collective-permute-done((bf16[64,2048]{1,0:T(8,128)(2,1)S(1)}, bf16[64,2048]{1,0:T(8,128)(2,1)S(1)}, u32[]{:S(2)}, u32[]{:S(2)}) %collective-permute-start.5) | collective-permute-done | bytes 262176 | tf_op jit(solution)/shard_map/ppermute | solution.py:100
  69.5 0.0 collective-permute-start.7
  69.5 0.0 collective-permute-done.6
  69.5 1.8 %collective-permute-start.8 = (bf16[64,2048]{1,0:T(8,128)(2,1)S(1)}, bf16[64,2048]{1,0:T(8,128)(2,1)S(1)}, u32[]{:S(2)}, u32[]{:S(2)}) collective-permute-start(bf16[64,2048]{1,0:T(8,128)(2,1)S(1)} %collective-permute-done.6), channel_id=1, source_target_pairs={{1,0},{4,1},{5,4},{8,5},{9,8},{12,9},{13,12},{14,13},{15,14},{10,1... | collective-permute-start | bytes 786440 | tf_op jit(solution)/shard_map/ppermute | solution.py:104
  71.3 0.7 bitcast_dynamic-update-slice_fusion.10
  72.0 0.7 bitcast_dynamic-update-slice_fusion.9
  72.7 2.5 %collective-permute-done.7 = bf16[64,2048]{1,0:T(8,128)(2,1)S(1)} collective-permute-done((bf16[64,2048]{1,0:T(8,128)(2,1)S(1)}, bf16[64,2048]{1,0:T(8,128)(2,1)S(1)}, u32[]{:S(2)}, u32[]{:S(2)}) %collective-permute-start.7) | collective-permute-done | bytes 262176 | tf_op jit(solution)/shard_map/ppermute | solution.py:100
  75.3 0.0 collective-permute-start.9
  75.3 0.0 collective-permute-done.8
  75.3 1.8 %collective-permute-start.10 = (bf16[64,2048]{1,0:T(8,128)(2,1)S(1)}, bf16[64,2048]{1,0:T(8,128)(2,1)S(1)}, u32[]{:S(2)}, u32[]{:S(2)}) collective-permute-start(bf16[64,2048]{1,0:T(8,128)(2,1)S(1)} %collective-permute-done.8), channel_id=1, source_target_pairs={{1,0},{4,1},{5,4},{8,5},{9,8},{12,9},{13,12},{14,13},{15,14},{10,1... | collective-permute-start | bytes 786440 | tf_op jit(solution)/shard_map/ppermute | solution.py:104
  77.1 0.7 bitcast_dynamic-update-slice_fusion.8
  77.8 0.7 bitcast_dynamic-update-slice_fusion.7
  78.5 2.5 %collective-permute-done.9 = bf16[64,2048]{1,0:T(8,128)(2,1)S(1)} collective-permute-done((bf16[64,2048]{1,0:T(8,128)(2,1)S(1)}, bf16[64,2048]{1,0:T(8,128)(2,1)S(1)}, u32[]{:S(2)}, u32[]{:S(2)}) %collective-permute-start.9) | collective-permute-done | bytes 262176 | tf_op jit(solution)/shard_map/ppermute | solution.py:100
  81.1 0.0 collective-permute-start.11
  81.1 0.0 collective-permute-done.10
  81.1 1.8 %collective-permute-start.12 = (bf16[64,2048]{1,0:T(8,128)(2,1)S(1)}, bf16[64,2048]{1,0:T(8,128)(2,1)S(1)}, u32[]{:S(2)}, u32[]{:S(2)}) collective-permute-start(bf16[64,2048]{1,0:T(8,128)(2,1)S(1)} %collective-permute-done.10), channel_id=1, source_target_pairs={{1,0},{4,1},{5,4},{8,5},{9,8},{12,9},{13,12},{14,13},{15,14},{10,1... | collective-permute-start | bytes 786440 | tf_op jit(solution)/shard_map/ppermute | solution.py:104
  82.9 0.7 bitcast_dynamic-update-slice_fusion.6
  83.6 0.7 bitcast_dynamic-update-slice_fusion.5
  84.3 2.5 %collective-permute-done.11 = bf16[64,2048]{1,0:T(8,128)(2,1)S(1)} collective-permute-done((bf16[64,2048]{1,0:T(8,128)(2,1)S(1)}, bf16[64,2048]{1,0:T(8,128)(2,1)S(1)}, u32[]{:S(2)}, u32[]{:S(2)}) %collective-permute-start.11) | collective-permute-done | bytes 262176 | tf_op jit(solution)/shard_map/ppermute | solution.py:100
  86.9 0.0 collective-permute-start.13
  86.9 0.0 collective-permute-done.12
  86.9 1.8 %collective-permute-start.14 = (bf16[64,2048]{1,0:T(8,128)(2,1)S(1)}, bf16[64,2048]{1,0:T(8,128)(2,1)S(1)}, u32[]{:S(2)}, u32[]{:S(2)}) collective-permute-start(bf16[64,2048]{1,0:T(8,128)(2,1)S(1)} %collective-permute-done.12), channel_id=1, source_target_pairs={{1,0},{4,1},{5,4},{8,5},{9,8},{12,9},{13,12},{14,13},{15,14},{10,1... | collective-permute-start | bytes 786440 | tf_op jit(solution)/shard_map/ppermute | solution.py:104
  88.7 0.7 bitcast_dynamic-update-slice_fusion.4
  89.4 0.7 bitcast_dynamic-update-slice_fusion.3
  90.1 2.5 %collective-permute-done.13 = bf16[64,2048]{1,0:T(8,128)(2,1)S(1)} collective-permute-done((bf16[64,2048]{1,0:T(8,128)(2,1)S(1)}, bf16[64,2048]{1,0:T(8,128)(2,1)S(1)}, u32[]{:S(2)}, u32[]{:S(2)}) %collective-permute-start.13) | collective-permute-done | bytes 262176 | tf_op jit(solution)/shard_map/ppermute | solution.py:100
  92.7 0.0 collective-permute-start.15
  92.7 0.7 bitcast_dynamic-update-slice_fusion.2
  93.4 0.0 collective-permute-done.14
  93.4 0.7 bitcast_dynamic-update-slice_fusion.1
  94.1 4.4 %collective-permute-done.15 = bf16[64,2048]{1,0:T(8,128)(2,1)S(1)} collective-permute-done((bf16[64,2048]{1,0:T(8,128)(2,1)S(1)}, bf16[64,2048]{1,0:T(8,128)(2,1)S(1)}, u32[]{:S(2)}, u32[]{:S(2)}) %collective-permute-start.15) | collective-permute-done | bytes 262176 | tf_op jit(solution)/shard_map/ppermute | solution.py:100
  98.5 0.7 bitcast_dynamic-update-slice_fusion
  99.2 6.4 %copy.27 = bf16[1024,2048]{0,1:T(8,128)(2,1)} copy(bf16[1024,2048]{1,0:T(8,128)(2,1)} %bitcast.49) | data formatting | bytes 8388608 | tf_op jit(solution)/shard_map/reshape | solution.py:126
  105.6 7.7 %gather_fusion = bf16[1024,1024]{1,0:T(8,128)(2,1)S(1)} fusion(bf16[2048,1024]{1,0:T(8,128)(2,1)} %bitcast.75, s32[1024]{0:T(1024)S(1)} %broadcast_clamp_fusion.1), kind=kCustom, calls=%fused_computation | custom fusion | bytes 4198400 | tf_op jit(solution)/shard_map/jit(_take)/gather | solution.py:130
  113.3 1.6 %broadcast_select_fusion.picked_ref = bf16[32,32,1024]{2,1,0:T(8,128)(2,1)} fusion(bf16[32,32,1024]{2,1,0:T(8,128)(2,1)S(1)} %bitcast.76, pred[32,32]{1,0:T(8,128)(4,1)S(1)} %compare_and_fusion), kind=kLoop, calls=%fused_computation.6 | loop fusion | flops 1048576 | bytes 4195328 | tf_op jit(solution)/shard_map/jit(_take)/select_n | solution.py:130
  114.9 15.4 %shard_map.73 = f32[32,1024]{1,0:T(8,128)} custom-call(bf16[32,200,32]{2,1,0:T(8,128)(2,1)} %bitcast.77, bf16[32,32,1024]{2,1,0:T(8,128)(2,1)} %broadcast_select_fusion.picked_ref), custom_call_target="tpu_custom_call" | custom-call | tf_op jit(solution)/shard_map/pallas_call | solution.py:48
  (12 shorter events, 0.1 us)
Async XLA Ops:
  0.0 8.4 %copy-start.3 = (s32[16]{0:T(128)S(1)}, s32[16]{0:T(128)}, u32[]{:S(2)}) copy-start(s32[16]{0:T(128)} %constant.208.clone) | copy-start | bytes 196
  0.0 19.0 %copy-start.1 = (s32[16]{0:T(128)S(1)}, s32[16]{0:T(128)}, u32[]{:S(2)}) copy-start(s32[16]{0:T(128)} %constant.207.clone) | copy-start | bytes 196
  0.0 8.3 %copy-start.2 = (s32[32,32]{1,0:T(8,128)S(1)}, s32[32,32]{1,0:T(8,128)}, u32[]{:S(2)}) copy-start(s32[32,32]{1,0:T(8,128)} %param.12) | copy-start | bytes 12292
  0.7 38.2 %copy-start = (bf16[32,32,200]{2,1,0:T(8,128)(2,1)S(1)}, bf16[32,32,200]{2,1,0:T(8,128)(2,1)}, u32[]{:S(2)}) copy-start(bf16[32,32,200]{2,1,0:T(8,128)(2,1)} %param.13) | copy-start | bytes 1228804
  5.9 44.1 %collective-permute-start = (f32[8,2048]{1,0:T(8,128)S(1)}, f32[8,2048]{1,0:T(8,128)S(1)}, u32[]{:S(2)}, u32[]{:S(2)}) collective-permute-start(f32[8,2048]{1,0:T(8,128)S(1)} %slice.33), channel_id=1, source_target_pairs={{0,1},{1,2},{2,3},{3,4},{4,5},{5,6},{6,7},{7,8},{8,9},{9,10},{10,1... | collective-permute-start | bytes 196616 | tf_op jit(solution)/shard_map/ppermute | solution.py:121
  50.0 7.9 %collective-permute-start.1 = (bf16[64,2048]{1,0:T(8,128)(2,1)S(1)}, bf16[64,2048]{1,0:T(8,128)(2,1)S(1)}, u32[]{:S(2)}, u32[]{:S(2)}) collective-permute-start(bf16[64,2048]{1,0:T(8,128)(2,1)S(1)} %fusion.4), channel_id=1, source_target_pairs={{0,1},{1,4},{4,5},{5,8},{8,9},{9,12},{12,13},{13,14},{14,15},{15,1... | collective-permute-start | bytes 786440 | tf_op jit(solution)/shard_map/ppermute | solution.py:100
  52.7 5.2 %collective-permute-start.2 = (bf16[64,2048]{1,0:T(8,128)(2,1)S(1)}, bf16[64,2048]{1,0:T(8,128)(2,1)S(1)}, u32[]{:S(2)}, u32[]{:S(2)}) collective-permute-start(bf16[64,2048]{1,0:T(8,128)(2,1)S(1)} %fusion.4), channel_id=1, source_target_pairs={{1,0},{4,1},{5,4},{8,5},{9,8},{12,9},{13,12},{14,13},{15,14},{10,1... | collective-permute-start | bytes 786440 | tf_op jit(solution)/shard_map/ppermute | solution.py:104
  57.9 5.8 %collective-permute-start.3 = (bf16[64,2048]{1,0:T(8,128)(2,1)S(1)}, bf16[64,2048]{1,0:T(8,128)(2,1)S(1)}, u32[]{:S(2)}, u32[]{:S(2)}) collective-permute-start(bf16[64,2048]{1,0:T(8,128)(2,1)S(1)} %collective-permute-done.1), channel_id=1, source_target_pairs={{0,1},{1,4},{4,5},{5,8},{8,9},{9,12},{12,13},{13,14},{14,15},{15,1... | collective-permute-start | bytes 786440 | tf_op jit(solution)/shard_map/ppermute | solution.py:100
  57.9 5.8 %collective-permute-start.4 = (bf16[64,2048]{1,0:T(8,128)(2,1)S(1)}, bf16[64,2048]{1,0:T(8,128)(2,1)S(1)}, u32[]{:S(2)}, u32[]{:S(2)}) collective-permute-start(bf16[64,2048]{1,0:T(8,128)(2,1)S(1)} %collective-permute-done.2), channel_id=1, source_target_pairs={{1,0},{4,1},{5,4},{8,5},{9,8},{12,9},{13,12},{14,13},{15,14},{10,1... | collective-permute-start | bytes 786440 | tf_op jit(solution)/shard_map/ppermute | solution.py:104
  63.7 5.8 %collective-permute-start.5 = (bf16[64,2048]{1,0:T(8,128)(2,1)S(1)}, bf16[64,2048]{1,0:T(8,128)(2,1)S(1)}, u32[]{:S(2)}, u32[]{:S(2)}) collective-permute-start(bf16[64,2048]{1,0:T(8,128)(2,1)S(1)} %collective-permute-done.3), channel_id=1, source_target_pairs={{0,1},{1,4},{4,5},{5,8},{8,9},{9,12},{12,13},{13,14},{14,15},{15,1... | collective-permute-start | bytes 786440 | tf_op jit(solution)/shard_map/ppermute | solution.py:100
  63.7 5.8 %collective-permute-start.6 = (bf16[64,2048]{1,0:T(8,128)(2,1)S(1)}, bf16[64,2048]{1,0:T(8,128)(2,1)S(1)}, u32[]{:S(2)}, u32[]{:S(2)}) collective-permute-start(bf16[64,2048]{1,0:T(8,128)(2,1)S(1)} %collective-permute-done.4), channel_id=1, source_target_pairs={{1,0},{4,1},{5,4},{8,5},{9,8},{12,9},{13,12},{14,13},{15,14},{10,1... | collective-permute-start | bytes 786440 | tf_op jit(solution)/shard_map/ppermute | solution.py:104
  69.5 5.8 %collective-permute-start.7 = (bf16[64,2048]{1,0:T(8,128)(2,1)S(1)}, bf16[64,2048]{1,0:T(8,128)(2,1)S(1)}, u32[]{:S(2)}, u32[]{:S(2)}) collective-permute-start(bf16[64,2048]{1,0:T(8,128)(2,1)S(1)} %collective-permute-done.5), channel_id=1, source_target_pairs={{0,1},{1,4},{4,5},{5,8},{8,9},{9,12},{12,13},{13,14},{14,15},{15,1... | collective-permute-start | bytes 786440 | tf_op jit(solution)/shard_map/ppermute | solution.py:100
  69.5 5.8 %collective-permute-start.8 = (bf16[64,2048]{1,0:T(8,128)(2,1)S(1)}, bf16[64,2048]{1,0:T(8,128)(2,1)S(1)}, u32[]{:S(2)}, u32[]{:S(2)}) collective-permute-start(bf16[64,2048]{1,0:T(8,128)(2,1)S(1)} %collective-permute-done.6), channel_id=1, source_target_pairs={{1,0},{4,1},{5,4},{8,5},{9,8},{12,9},{13,12},{14,13},{15,14},{10,1... | collective-permute-start | bytes 786440 | tf_op jit(solution)/shard_map/ppermute | solution.py:104
  75.3 5.8 %collective-permute-start.9 = (bf16[64,2048]{1,0:T(8,128)(2,1)S(1)}, bf16[64,2048]{1,0:T(8,128)(2,1)S(1)}, u32[]{:S(2)}, u32[]{:S(2)}) collective-permute-start(bf16[64,2048]{1,0:T(8,128)(2,1)S(1)} %collective-permute-done.7), channel_id=1, source_target_pairs={{0,1},{1,4},{4,5},{5,8},{8,9},{9,12},{12,13},{13,14},{14,15},{15,1... | collective-permute-start | bytes 786440 | tf_op jit(solution)/shard_map/ppermute | solution.py:100
  75.3 5.8 %collective-permute-start.10 = (bf16[64,2048]{1,0:T(8,128)(2,1)S(1)}, bf16[64,2048]{1,0:T(8,128)(2,1)S(1)}, u32[]{:S(2)}, u32[]{:S(2)}) collective-permute-start(bf16[64,2048]{1,0:T(8,128)(2,1)S(1)} %collective-permute-done.8), channel_id=1, source_target_pairs={{1,0},{4,1},{5,4},{8,5},{9,8},{12,9},{13,12},{14,13},{15,14},{10,1... | collective-permute-start | bytes 786440 | tf_op jit(solution)/shard_map/ppermute | solution.py:104
  81.1 5.8 %collective-permute-start.11 = (bf16[64,2048]{1,0:T(8,128)(2,1)S(1)}, bf16[64,2048]{1,0:T(8,128)(2,1)S(1)}, u32[]{:S(2)}, u32[]{:S(2)}) collective-permute-start(bf16[64,2048]{1,0:T(8,128)(2,1)S(1)} %collective-permute-done.9), channel_id=1, source_target_pairs={{0,1},{1,4},{4,5},{5,8},{8,9},{9,12},{12,13},{13,14},{14,15},{15,1... | collective-permute-start | bytes 786440 | tf_op jit(solution)/shard_map/ppermute | solution.py:100
  81.1 5.8 %collective-permute-start.12 = (bf16[64,2048]{1,0:T(8,128)(2,1)S(1)}, bf16[64,2048]{1,0:T(8,128)(2,1)S(1)}, u32[]{:S(2)}, u32[]{:S(2)}) collective-permute-start(bf16[64,2048]{1,0:T(8,128)(2,1)S(1)} %collective-permute-done.10), channel_id=1, source_target_pairs={{1,0},{4,1},{5,4},{8,5},{9,8},{12,9},{13,12},{14,13},{15,14},{10,1... | collective-permute-start | bytes 786440 | tf_op jit(solution)/shard_map/ppermute | solution.py:104
  86.9 5.8 %collective-permute-start.13 = (bf16[64,2048]{1,0:T(8,128)(2,1)S(1)}, bf16[64,2048]{1,0:T(8,128)(2,1)S(1)}, u32[]{:S(2)}, u32[]{:S(2)}) collective-permute-start(bf16[64,2048]{1,0:T(8,128)(2,1)S(1)} %collective-permute-done.11), channel_id=1, source_target_pairs={{0,1},{1,4},{4,5},{5,8},{8,9},{9,12},{12,13},{13,14},{14,15},{15,1... | collective-permute-start | bytes 786440 | tf_op jit(solution)/shard_map/ppermute | solution.py:100
  86.9 6.5 %collective-permute-start.14 = (bf16[64,2048]{1,0:T(8,128)(2,1)S(1)}, bf16[64,2048]{1,0:T(8,128)(2,1)S(1)}, u32[]{:S(2)}, u32[]{:S(2)}) collective-permute-start(bf16[64,2048]{1,0:T(8,128)(2,1)S(1)} %collective-permute-done.12), channel_id=1, source_target_pairs={{1,0},{4,1},{5,4},{8,5},{9,8},{12,9},{13,12},{14,13},{15,14},{10,1... | collective-permute-start | bytes 786440 | tf_op jit(solution)/shard_map/ppermute | solution.py:104
  92.7 5.8 %collective-permute-start.15 = (bf16[64,2048]{1,0:T(8,128)(2,1)S(1)}, bf16[64,2048]{1,0:T(8,128)(2,1)S(1)}, u32[]{:S(2)}, u32[]{:S(2)}) collective-permute-start(bf16[64,2048]{1,0:T(8,128)(2,1)S(1)} %collective-permute-done.13), channel_id=1, source_target_pairs={{0,1},{1,4},{4,5},{5,8},{8,9},{9,12},{12,13},{13,14},{14,15},{15,1... | collective-permute-start | bytes 786440 | tf_op jit(solution)/shard_map/ppermute | solution.py:100

commit v5 on v3

--- a/solution.py
+++ b/solution.py
@@ -23,18 +23,22 @@
     vb = out_ref.shape[0]
     span = slip_ref.shape[1]
     width = out_ref.shape[1]
-    col = lax.broadcasted_iota(jnp.int32, (8, width), 1)
-    row = lax.broadcasted_iota(jnp.int32, (8, width), 0)
+    edge = min(width, -(-span // 128) * 128)
+    col = lax.broadcasted_iota(jnp.int32, (8, edge), 1)
+    row = lax.broadcasted_iota(jnp.int32, (8, edge), 0)
     lag = col - row
 
     def one(v, carry):
         spread_ref[...] = jnp.dot(slip_ref[v], picked_ref[v], preferred_element_type=jnp.float32)
-        acc = jnp.zeros((8, width), jnp.float32)
+        head = jnp.zeros((8, edge), jnp.float32)
+        tail = jnp.zeros((8, width - edge), jnp.float32)
         for g in range(span // 8):
             blk = spread_ref[8 * g:8 * g + 8, :]
             moved = pltpu.roll(blk, 8 * g, 1, stride=1, stride_axis=0)
-            acc = acc + jnp.where(lag >= 8 * g, moved, 0.0)
-        out_ref[pl.ds(v, 1), :] = jnp.sum(acc, axis=0, keepdims=True)
+            head = head + jnp.where(lag >= 8 * g, moved[:, :edge], 0.0)
+            tail = tail + moved[:, edge:]
+        out_ref[pl.ds(v, 1), :edge] = jnp.sum(head, axis=0, keepdims=True)
+        out_ref[pl.ds(v, 1), edge:] = jnp.sum(tail, axis=0, keepdims=True)
         return carry
 
     lax.fori_loop(0, vb, one, 0)
@@ -77,7 +81,7 @@
     length = piece.shape[0]
     v_local, k = index.shape
     flat_index = jnp.clip(index.reshape(-1), 0, length - 1)
-    rows = jnp.take(piece, flat_index, axis=0)
+    rows = jnp.take(piece, flat_index, axis=0, mode="clip")
     picked = rows.reshape(v_local, k, piece.shape[1])
     return convolve(picked, slip)
 

time: 110 us -> 110 us (level)
  other arithmetic: 3.44 us -> 1.8 us
  local copies, waits for them, and re-layouts: 16.5 us -> 17.6 us
    select_n x2 -> x0, other arithmetic: 1.62 us -> none  [body(): rows = jnp.take(piece, flat_index, axis=0)]
where the time goes in v5:
time: 110 us
  waiting for transfers between devices  54.9 us (50%)
  local copies, waits for them, and re-layouts  17.6 us (16%)
  Pallas kernels  15.6 us (14%)
  between operations  13.5 us (12%)
  matrix products  4.11 us (4%)
  starting transfers between devices  2.36 us (2%)
  other arithmetic  1.8 us (2%)
    all_gather x1, waiting for transfers between devices, body(): piece = lax.all_gather(green, 'handler', axis=1, tiled=True)  54 us
    pallas_call x1, Pallas kernels, convolve(): pl.pallas_call(conv_kernel, grid=(v_local // vb,), in_specs=[pl.BlockSpec...  15.6 us
    gather x1, local copies, waits for them, and re-layouts, body(): rows = jnp.take(piece, flat_index, axis=0, mode='clip')  8.73 us
    all_gather x1, local copies, waits for them, and re-layouts, body(): piece = lax.all_gather(green, 'handler', axis=1, tiled=True)  6.41 us
    dot_general x1, matrix products, body(): jnp.einsum('tj,ctp->cjp', lowpass, by_component, preferred_element_type=j...  4.11 us
    ppermute x1, starting transfers between devices, body(): lax.ppermute(partial[local_j:], 'handler', [(i, i + 1) for i in range(n_h...  2.36 us
    unnamed x7, local copies, waits for them, and re-layouts  2.31 us
  transfers between devices with their start and end apart: 2, of which 2 were waited for; matrix products, arithmetic and copies ran while one was open for 2% of the time, Pallas kernels for 0%

profile of v5, /device:TPU:0, one launch (start us, length us, event | category | flops | bytes accessed | tf_op | source)
XLA Modules:
  0.0 109.8 jit_solution(7546057141135905417)
XLA Ops:
  6.5 0.0 all-gather.2.cloned.1.call-start
  6.5 0.7 convert_element_type.9
  7.2 1.1 %select_reduce_fusion = bf16[256,72]{0,1:T(8,128)(2,1)S(1)} fusion(f32[32]{0:T(128)S(1)} %convert_element_type.9, s32[72]{0:T(128)S(1)} %iota_multiply_fusion), kind=kLoop, calls=%fused_computation.4 | loop fusion | flops 2340864 | bytes 37280 | tf_op jit(solution)/shard_map/reduce_sum | solution.py:19
  8.3 0.0 copy-start.2
  8.3 0.0 copy-start.1
  8.4 4.1 %multiply_reduce_fusion = f32[72,2048]{1,0:T(8,128)S(1)} fusion(bf16[256,6,2048]{2,0,1:T(8,128)(2,1)} %param.7, f32[6,2048]{1,0:T(8,128)} %param.9, bf16[256,72]{0,1:T(8,128)(2,1)S(1)} %select_reduce_fusion), kind=kOutput, calls=%fused_computation.3 | convolution fusion | flops 454606848 | bytes 6967296 | tf_op jit(solution)/shard_map/tj,ctp->cjp/dot_general | solution.py:74
  12.5 2.4 %collective-permute-start = (f32[8,2048]{1,0:T(8,128)S(1)}, f32[8,2048]{1,0:T(8,128)S(1)}, u32[]{:S(2)}, u32[]{:S(2)}) collective-permute-start(f32[8,2048]{1,0:T(8,128)S(1)} %slice.33), channel_id=1, source_target_pairs={{0,1},{1,2},{2,3},{3,4},{4,5},{5,6},{6,7},{7,8},{8,9},{9,10},{10,1... | collective-permute-start | bytes 196616 | tf_op jit(solution)/shard_map/ppermute | solution.py:76
  14.9 0.8 collective-permute-done
  15.7 0.0 copy-start
  15.8 0.7 copy-done
  16.4 0.0 all-gather.2.cloned.1.call-update
  16.5 0.0 copy-done.2
  16.5 0.1 reshape.48
  16.6 0.0 copy-done.1
  16.6 1.6 %copy.9 = bf16[32,32,200]{1,2,0:T(8,128)(2,1)} copy(bf16[32,32,200]{2,1,0:T(8,128)(2,1)S(1)} %copy-done.1) | data formatting | bytes 819200 | tf_op args[4]
  18.2 54.0 %all-gather.2.cloned.1.call-done = bf16[2048,1024]{0,1:T(8,128)(2,1)} async-done(((bf16[2048,64]{0,1:T(8,128)(2,1)}), bf16[2048,1024]{0,1:T(8,128)(2,1)}) %all-gather.2.cloned.1.call-update) | async-done | bytes 4194320 | tf_op jit(solution)/shard_map/all_gather | solution.py:80
  72.2 6.4 %copy.10 = bf16[2048,1024]{1,0:T(8,128)(2,1)} copy(bf16[2048,1024]{0,1:T(8,128)(2,1)} %all-gather.2.cloned.1.call-done) | data formatting | bytes 8388608 | tf_op jit(solution)/shard_map/all_gather | solution.py:80
  78.6 8.7 %gather_fusion = bf16[1024,1024]{1,0:T(8,128)(2,1)} fusion(bf16[2048,1024]{1,0:T(8,128)(2,1)} %copy.10, s32[1024]{0:T(1024)S(1)} %broadcast_clamp_fusion.1), kind=kCustom, calls=%fused_computation | custom fusion | bytes 4198400 | tf_op jit(solution)/shard_map/jit(_take)/gather | solution.py:84
  87.4 15.6 %shard_map.55 = f32[32,1024]{1,0:T(8,128)} custom-call(bf16[32,200,32]{2,1,0:T(8,128)(2,1)} %bitcast.14, bf16[32,32,1024]{2,1,0:T(8,128)(2,1)} %bitcast.13), custom_call_target="tpu_custom_call" | custom-call | tf_op jit(solution)/shard_map/pallas_call | solution.py:52
  (6 shorter events, 0.1 us)
Async XLA Ops:
  6.5 65.7 %all-gather.2.cloned.1.call-start = ((), (), s32[]{:S(2)}) async-start(), calls=%async_computation | async-start | bytes 4456448 | tf_op jit(solution)/shard_map/all_gather | solution.py:80
  8.3 8.1 %copy-start.2 = (s32[32,32]{1,0:T(8,128)S(1)}, s32[32,32]{1,0:T(8,128)}, u32[]{:S(2)}) copy-start(s32[32,32]{1,0:T(8,128)} %param.10) | copy-start | bytes 12292
  8.3 8.2 %copy-start.1 = (bf16[32,32,200]{2,1,0:T(8,128)(2,1)S(1)}, bf16[32,32,200]{2,1,0:T(8,128)(2,1)}, u32[]{:S(2)}) copy-start(bf16[32,32,200]{2,1,0:T(8,128)(2,1)} %param.11) | copy-start | bytes 1228804
  12.5 3.3 %collective-permute-start = (f32[8,2048]{1,0:T(8,128)S(1)}, f32[8,2048]{1,0:T(8,128)S(1)}, u32[]{:S(2)}, u32[]{:S(2)}) collective-permute-start(f32[8,2048]{1,0:T(8,128)S(1)} %slice.33), channel_id=1, source_target_pairs={{0,1},{1,2},{2,3},{3,4},{4,5},{5,6},{6,7},{7,8},{8,9},{9,10},{10,1... | collective-permute-start | bytes 196616 | tf_op jit(solution)/shard_map/ppermute | solution.py:76
  15.7 0.7 copy-start
Sparse Core Ops, SparseCore 0:
  16.6 55.5 all-gather.1

commit v6 on v5

--- a/solution.py
+++ b/solution.py
@@ -19,26 +19,40 @@
     return jnp.sum(picked, axis=2).astype(jnp.bfloat16)
 
 
-def conv_kernel(slip_ref, picked_ref, out_ref, spread_ref):
+SHIFTS = 8
+
+
+def conv_kernel(weight_ref, picked_ref, out_ref, shifted_ref):
     vb = out_ref.shape[0]
-    span = slip_ref.shape[1]
+    n_rows = weight_ref.shape[1]
+    k = picked_ref.shape[1]
     width = out_ref.shape[1]
-    edge = min(width, -(-span // 128) * 128)
+    edge = min(width, n_rows * SHIFTS)
+    edge = -(-edge // 128) * 128
+    col_in = lax.broadcasted_iota(jnp.int32, (k, 128), 1)
     col = lax.broadcasted_iota(jnp.int32, (8, edge), 1)
     row = lax.broadcasted_iota(jnp.int32, (8, edge), 0)
-    lag = col - row
+    lag = col - SHIFTS * row
 
     def one(v, carry):
-        spread_ref[...] = jnp.dot(slip_ref[v], picked_ref[v], preferred_element_type=jnp.float32)
+        rows = picked_ref[v].astype(jnp.float32)
+        shifted_ref[0:k, :] = rows.astype(jnp.bfloat16)
+        for b in range(1, SHIFTS):
+            moved = pltpu.roll(rows, b, 1)
+            shifted_ref[b * k:(b + 1) * k, :128] = jnp.where(col_in >= b, moved[:, :128], 0.0).astype(jnp.bfloat16)
+            shifted_ref[b * k:(b + 1) * k, 128:] = moved[:, 128:].astype(jnp.bfloat16)
+        spread = jnp.dot(weight_ref[v], shifted_ref[...], preferred_element_type=jnp.float32)
         head = jnp.zeros((8, edge), jnp.float32)
         tail = jnp.zeros((8, width - edge), jnp.float32)
-        for g in range(span // 8):
-            blk = spread_ref[8 * g:8 * g + 8, :]
-            moved = pltpu.roll(blk, 8 * g, 1, stride=1, stride_axis=0)
-            head = head + jnp.where(lag >= 8 * g, moved[:, :edge], 0.0)
-            tail = tail + moved[:, edge:]
+        for q in range(n_rows // 8):
+            blk = spread[8 * q:8 * q + 8, :]
+            moved = pltpu.roll(blk, 8 * SHIFTS * q, 1, stride=SHIFTS, stride_axis=0)
+            head = head + jnp.where(lag >= 8 * SHIFTS * q, moved[:, :edge], 0.0)
+            if width > edge:
+                tail = tail + moved[:, edge:]
         out_ref[pl.ds(v, 1), :edge] = jnp.sum(head, axis=0, keepdims=True)
-        out_ref[pl.ds(v, 1), edge:] = jnp.sum(tail, axis=0, keepdims=True)
+        if width > edge:
+            out_ref[pl.ds(v, 1), edge:] = jnp.sum(tail, axis=0, keepdims=True)
         return carry
 
     lax.fori_loop(0, vb, one, 0)
@@ -47,19 +61,22 @@
 def convolve(picked, slip):
     v_local, k, width = picked.shape
     span = slip.shape[2]
-    slip_t = jnp.swapaxes(slip, 1, 2)
+    n_rows = -(-span // SHIFTS)
+    n_rows = -(-n_rows // 8) * 8
+    padded = jnp.pad(slip, ((0, 0), (0, 0), (0, n_rows * SHIFTS - span)))
+    weight = padded.reshape(v_local, k, n_rows, SHIFTS).transpose(0, 2, 3, 1).reshape(v_local, n_rows, SHIFTS * k)
     vb = min(V_BLOCK, v_local)
     return pl.pallas_call(
         conv_kernel,
         grid=(v_local // vb,),
         in_specs=[
-            pl.BlockSpec((vb, span, k), lambda i: (i, 0, 0)),
+            pl.BlockSpec((vb, n_rows, SHIFTS * k), lambda i: (i, 0, 0)),
             pl.BlockSpec((vb, k, width), lambda i: (i, 0, 0)),
         ],
         out_specs=pl.BlockSpec((vb, width), lambda i: (i, 0)),
         out_shape=jax.ShapeDtypeStruct((v_local, width), jnp.float32),
-        scratch_shapes=[pltpu.VMEM((span, width), jnp.float32)],
-    )(slip_t, picked)
+        scratch_shapes=[pltpu.VMEM((SHIFTS * k, width), jnp.bfloat16)],
+    )(weight, picked)
 
 
 def body(sgt, taps, moment, index, slip):

time: 110 us -> 111 us (level)
  waiting for transfers between devices: 54.9 us -> 50.8 us
  local copies, waits for them, and re-layouts: 17.6 us -> 21.7 us
  Pallas kernels: 15.6 us -> 16.8 us
    all_gather x1, waiting for transfers between devices: 54 us -> 49.9 us  [body(): piece = lax.all_gather(green, 'handler', axis=1, tiled=True)]
    reshape x0 -> x1, local copies, waits for them, and re-layouts: none -> 2.15 us  [convolve(): padded.reshape(v_local, k, n_rows, SHIFTS).transpose(0, 2, 3, 1)]
    transpose x0 -> x1, local copies, waits for them, and re-layouts: none -> 1.99 us  [convolve(): padded.reshape(v_local, k, n_rows, SHIFTS).transpose(0, 2, 3, 1)]
    pallas_call x1, Pallas kernels: 15.6 us -> 16.8 us  [convolve(): pl.pallas_call(conv_kernel, grid=(v_local // vb,), in_specs=[pl.BlockSpec...]
  transfers between devices with their start and end apart: 2 -> 2, of which waited for: 2 -> 2; matrix products, arithmetic and copies ran while one was open for 2% -> 5% of each run, Pallas kernels for 0% -> 0%
where the time goes in v6:
time: 111 us
  waiting for transfers between devices  50.8 us (46%)
  local copies, waits for them, and re-layouts  21.7 us (20%)
  Pallas kernels  16.8 us (15%)
  between operations  13.5 us (12%)
  matrix products  4.11 us (4%)
  starting transfers between devices  2.36 us (2%)
  other arithmetic  1.8 us (2%)
    all_gather x1, waiting for transfers between devices, body(): piece = lax.all_gather(green, 'handler', axis=1, tiled=True)  49.9 us
    pallas_call x1, Pallas kernels, convolve(): pl.pallas_call(conv_kernel, grid=(v_local // vb,), in_specs=[pl.BlockSpec...  16.8 us
    gather x1, local copies, waits for them, and re-layouts, body(): rows = jnp.take(piece, flat_index, axis=0, mode='clip')  8.73 us
    all_gather x1, local copies, waits for them, and re-layouts, body(): piece = lax.all_gather(green, 'handler', axis=1, tiled=True)  6.41 us
    dot_general x1, matrix products, body(): jnp.einsum('tj,ctp->cjp', lowpass, by_component, preferred_element_type=j...  4.11 us
    ppermute x1, starting transfers between devices, body(): lax.ppermute(partial[local_j:], 'handler', [(i, i + 1) for i in range(n_h...  2.36 us
    unnamed x7, local copies, waits for them, and re-layouts  2.29 us
  transfers between devices with their start and end apart: 2, of which 2 were waited for; matrix products, arithmetic and copies ran while one was open for 5% of the time, Pallas kernels for 0%

profile of v6, /device:TPU:0, one launch (start us, length us, event | category | flops | bytes accessed | tf_op | source)
XLA Modules:
  0.0 111.0 jit_solution(12570911247081989762)
XLA Ops:
  6.5 0.0 all-gather.2.cloned.1.call-start
  6.5 0.7 convert_element_type.11
  7.2 1.1 %select_reduce_fusion = bf16[256,72]{0,1:T(8,128)(2,1)S(1)} fusion(f32[32]{0:T(128)S(1)} %convert_element_type.11, s32[72]{0:T(128)S(1)} %iota_multiply_fusion), kind=kLoop, calls=%fused_computation.4 | loop fusion | flops 2340864 | bytes 37280 | tf_op jit(solution)/shard_map/reduce_sum | solution.py:19
  8.3 0.0 copy-start.2
  8.3 0.0 copy-start.1
  8.4 4.1 %multiply_reduce_fusion = f32[72,2048]{1,0:T(8,128)S(1)} fusion(bf16[256,6,2048]{2,0,1:T(8,128)(2,1)} %param.7, f32[6,2048]{1,0:T(8,128)} %param.9, bf16[256,72]{0,1:T(8,128)(2,1)S(1)} %select_reduce_fusion), kind=kOutput, calls=%fused_computation.3 | convolution fusion | flops 454606848 | bytes 6967296 | tf_op jit(solution)/shard_map/tj,ctp->cjp/dot_general | solution.py:91
  12.5 2.4 %collective-permute-start = (f32[8,2048]{1,0:T(8,128)S(1)}, f32[8,2048]{1,0:T(8,128)S(1)}, u32[]{:S(2)}, u32[]{:S(2)}) collective-permute-start(f32[8,2048]{1,0:T(8,128)S(1)} %slice.33), channel_id=1, source_target_pairs={{0,1},{1,2},{2,3},{3,4},{4,5},{5,6},{6,7},{7,8},{8,9},{9,10},{10,1... | collective-permute-start | bytes 196616 | tf_op jit(solution)/shard_map/ppermute | solution.py:93
  14.9 0.8 collective-permute-done
  15.7 0.0 copy-start
  15.8 0.7 copy-done
  16.4 0.0 all-gather.2.cloned.1.call-update
  16.5 0.0 copy-done.2
  16.5 0.1 reshape.56
  16.6 0.0 copy-done.1
  16.6 1.6 %copy.10 = bf16[32,32,200]{1,2,0:T(8,128)(2,1)} copy(bf16[32,32,200]{2,1,0:T(8,128)(2,1)S(1)} %copy-done.1) | data formatting | bytes 819200 | tf_op args[4]
  18.1 2.0 %pad_bitcast_fusion = bf16[32,32,8,32]{3,2,1,0:T(8,128)(2,1)S(1)} fusion(bf16[32,32,200]{1,2,0:T(8,128)(2,1)} %copy.10), kind=kLoop, calls=%fused_computation.6 | loop fusion | bytes 933888 | tf_op jit(solution)/shard_map/transpose | solution.py:67
  20.1 2.2 %reshape.52.weight_ref = bf16[32,32,256]{2,1,0:T(8,128)(2,1)} reshape(bf16[32,32,8,32]{3,2,1,0:T(8,128)(2,1)S(1)} %pad_bitcast_fusion) | data formatting | bytes 1048576 | tf_op jit(solution)/shard_map/reshape | solution.py:67
  22.3 49.9 %all-gather.2.cloned.1.call-done = bf16[2048,1024]{0,1:T(8,128)(2,1)} async-done(((bf16[2048,64]{0,1:T(8,128)(2,1)}), bf16[2048,1024]{0,1:T(8,128)(2,1)}) %all-gather.2.cloned.1.call-update) | async-done | bytes 4194320 | tf_op jit(solution)/shard_map/all_gather | solution.py:97
  72.2 6.4 %copy.11 = bf16[2048,1024]{1,0:T(8,128)(2,1)} copy(bf16[2048,1024]{0,1:T(8,128)(2,1)} %all-gather.2.cloned.1.call-done) | data formatting | bytes 8388608 | tf_op jit(solution)/shard_map/all_gather | solution.py:97
  78.6 8.7 %gather_fusion = bf16[1024,1024]{1,0:T(8,128)(2,1)} fusion(bf16[2048,1024]{1,0:T(8,128)(2,1)} %copy.11, s32[1024]{0:T(1024)S(1)} %broadcast_clamp_fusion.1), kind=kCustom, calls=%fused_computation | custom fusion | bytes 4198400 | tf_op jit(solution)/shard_map/jit(_take)/gather | solution.py:101
  87.4 16.8 %shard_map.55 = f32[32,1024]{1,0:T(8,128)} custom-call(bf16[32,32,256]{2,1,0:T(8,128)(2,1)} %reshape.52.weight_ref, bf16[32,32,1024]{2,1,0:T(8,128)(2,1)} %bitcast.18), custom_call_target="tpu_custom_call" | custom-call | tf_op jit(solution)/shard_map/pallas_call | solution.py:69
  (6 shorter events, 0.1 us)
Async XLA Ops:
  6.5 65.7 %all-gather.2.cloned.1.call-start = ((), (), s32[]{:S(2)}) async-start(), calls=%async_computation | async-start | bytes 4456448 | tf_op jit(solution)/shard_map/all_gather | solution.py:97
  8.3 8.1 %copy-start.2 = (s32[32,32]{1,0:T(8,128)S(1)}, s32[32,32]{1,0:T(8,128)}, u32[]{:S(2)}) copy-start(s32[32,32]{1,0:T(8,128)} %param.10) | copy-start | bytes 12292
  8.3 8.2 %copy-start.1 = (bf16[32,32,200]{2,1,0:T(8,128)(2,1)S(1)}, bf16[32,32,200]{2,1,0:T(8,128)(2,1)}, u32[]{:S(2)}) copy-start(bf16[32,32,200]{2,1,0:T(8,128)(2,1)} %param.11) | copy-start | bytes 1228804
  12.5 3.3 %collective-permute-start = (f32[8,2048]{1,0:T(8,128)S(1)}, f32[8,2048]{1,0:T(8,128)S(1)}, u32[]{:S(2)}, u32[]{:S(2)}) collective-permute-start(f32[8,2048]{1,0:T(8,128)S(1)} %slice.33), channel_id=1, source_target_pairs={{0,1},{1,2},{2,3},{3,4},{4,5},{5,6},{6,7},{7,8},{8,9},{9,10},{10,1... | collective-permute-start | bytes 196616 | tf_op jit(solution)/shard_map/ppermute | solution.py:93
  15.7 0.7 copy-start
Sparse Core Ops, SparseCore 0:
  16.6 55.5 all-gather.1

commit v7 on v6

--- a/solution.py
+++ b/solution.py
@@ -19,7 +19,7 @@
     return jnp.sum(picked, axis=2).astype(jnp.bfloat16)
 
 
-SHIFTS = 8
+SHIFTS = 4
 
 
 def conv_kernel(weight_ref, picked_ref, out_ref, shifted_ref):
@@ -35,12 +35,12 @@
     lag = col - SHIFTS * row
 
     def one(v, carry):
-        rows = picked_ref[v].astype(jnp.float32)
-        shifted_ref[0:k, :] = rows.astype(jnp.bfloat16)
+        rows = picked_ref[v]
+        shifted_ref[0:k, :] = rows
         for b in range(1, SHIFTS):
             moved = pltpu.roll(rows, b, 1)
-            shifted_ref[b * k:(b + 1) * k, :128] = jnp.where(col_in >= b, moved[:, :128], 0.0).astype(jnp.bfloat16)
-            shifted_ref[b * k:(b + 1) * k, 128:] = moved[:, 128:].astype(jnp.bfloat16)
+            shifted_ref[b * k:(b + 1) * k, :128] = jnp.where(col_in >= b, moved[:, :128], jnp.zeros_like(moved[:, :128]))
+            shifted_ref[b * k:(b + 1) * k, 128:] = moved[:, 128:]
         spread = jnp.dot(weight_ref[v], shifted_ref[...], preferred_element_type=jnp.float32)
         head = jnp.zeros((8, edge), jnp.float32)
         tail = jnp.zeros((8, width - edge), jnp.float32)

time: 111 us -> 109 us (0.982)
  Pallas kernels: 16.8 us -> 14.3 us
    pallas_call x1, Pallas kernels: 16.8 us -> 14.3 us  [convolve(): pl.pallas_call(conv_kernel, grid=(v_local // vb,), in_specs=[pl.BlockSpec...]
where the time goes in v7:
time: 109 us
  waiting for transfers between devices  51.2 us (47%)
  local copies, waits for them, and re-layouts  21.2 us (19%)
  Pallas kernels  14.3 us (13%)
  between operations  13.5 us (12%)
  matrix products  4.11 us (4%)
  starting transfers between devices  2.36 us (2%)
  other arithmetic  1.8 us (2%)
    all_gather x1, waiting for transfers between devices, body(): piece = lax.all_gather(green, 'handler', axis=1, tiled=True)  50.4 us
    pallas_call x1, Pallas kernels, convolve(): pl.pallas_call(conv_kernel, grid=(v_local // vb,), in_specs=[pl.BlockSpec...  14.3 us
    gather x1, local copies, waits for them, and re-layouts, body(): rows = jnp.take(piece, flat_index, axis=0, mode='clip')  8.73 us
    all_gather x1, local copies, waits for them, and re-layouts, body(): piece = lax.all_gather(green, 'handler', axis=1, tiled=True)  6.41 us
    dot_general x1, matrix products, body(): jnp.einsum('tj,ctp->cjp', lowpass, by_component, preferred_element_type=j...  4.11 us
    ppermute x1, starting transfers between devices, body(): lax.ppermute(partial[local_j:], 'handler', [(i, i + 1) for i in range(n_h...  2.36 us
    transpose x1, local copies, waits for them, and re-layouts, convolve(): padded.reshape(v_local, k, n_rows, SHIFTS).transpose(0, 2, 3, 1)  2.28 us
    unnamed x7, local copies, waits for them, and re-layouts  2.18 us
  transfers between devices with their start and end apart: 2, of which 2 were waited for; matrix products, arithmetic and copies ran while one was open for 5% of the time, Pallas kernels for 0%

profile of v7, /device:TPU:0, one launch (start us, length us, event | category | flops | bytes accessed | tf_op | source)
XLA Modules:
  0.0 108.5 jit_solution(16056602448115605098)
XLA Ops:
  6.5 0.0 all-gather.2.cloned.1.call-start
  6.5 0.7 convert_element_type.11
  7.2 1.1 %select_reduce_fusion = bf16[256,72]{0,1:T(8,128)(2,1)S(1)} fusion(f32[32]{0:T(128)S(1)} %convert_element_type.11, s32[72]{0:T(128)S(1)} %iota_multiply_fusion), kind=kLoop, calls=%fused_computation.4 | loop fusion | flops 2340864 | bytes 37280 | tf_op jit(solution)/shard_map/reduce_sum | solution.py:19
  8.3 0.0 copy-start.2
  8.3 0.0 copy-start.1
  8.4 4.1 %multiply_reduce_fusion = f32[72,2048]{1,0:T(8,128)S(1)} fusion(bf16[256,6,2048]{2,0,1:T(8,128)(2,1)} %param.7, f32[6,2048]{1,0:T(8,128)} %param.9, bf16[256,72]{0,1:T(8,128)(2,1)S(1)} %select_reduce_fusion), kind=kOutput, calls=%fused_computation.3 | convolution fusion | flops 454606848 | bytes 6967296 | tf_op jit(solution)/shard_map/tj,ctp->cjp/dot_general | solution.py:91
  12.5 2.4 %collective-permute-start = (f32[8,2048]{1,0:T(8,128)S(1)}, f32[8,2048]{1,0:T(8,128)S(1)}, u32[]{:S(2)}, u32[]{:S(2)}) collective-permute-start(f32[8,2048]{1,0:T(8,128)S(1)} %slice.33), channel_id=1, source_target_pairs={{0,1},{1,2},{2,3},{3,4},{4,5},{5,6},{6,7},{7,8},{8,9},{9,10},{10,1... | collective-permute-start | bytes 196616 | tf_op jit(solution)/shard_map/ppermute | solution.py:93
  14.9 0.8 collective-permute-done
  15.7 0.0 copy-start
  15.8 0.7 copy-done
  16.4 0.0 all-gather.2.cloned.1.call-update
  16.5 0.0 copy-done.2
  16.5 0.1 reshape.56
  16.6 0.0 copy-done.1
  16.6 1.5 %copy.18 = bf16[32,32,200]{1,0,2:T(8,128)(2,1)S(1)} copy(bf16[32,32,200]{2,1,0:T(8,128)(2,1)S(1)} %copy-done.1) | data formatting | bytes 819200
  18.1 0.3 pad.6.clone
  18.4 2.3 %copy.15 = bf16[32,56,4,32]{1,3,2,0:T(8,128)(2,1)S(1)} copy(bf16[32,56,4,32]{3,0,2,1:T(8,128)(2,1)S(1)} %bitcast.17) | data formatting | bytes 917504 | tf_op jit(solution)/shard_map/transpose | solution.py:67
  20.7 1.2 %copy.17.weight_ref = bf16[32,56,128]{2,1,0:T(8,128)(2,1)} copy(bf16[32,56,128]{1,2,0:T(8,128)(2,1)S(1)} %bitcast.18) | data formatting | bytes 917504 | tf_op jit(solution)/shard_map/reshape | solution.py:67
  21.8 50.4 %all-gather.2.cloned.1.call-done = bf16[2048,1024]{0,1:T(8,128)(2,1)} async-done(((bf16[2048,64]{0,1:T(8,128)(2,1)}), bf16[2048,1024]{0,1:T(8,128)(2,1)}) %all-gather.2.cloned.1.call-update) | async-done | bytes 4194320 | tf_op jit(solution)/shard_map/all_gather | solution.py:97
  72.2 6.4 %copy.16 = bf16[2048,1024]{1,0:T(8,128)(2,1)} copy(bf16[2048,1024]{0,1:T(8,128)(2,1)} %all-gather.2.cloned.1.call-done) | data formatting | bytes 8388608 | tf_op jit(solution)/shard_map/all_gather | solution.py:97
  78.6 8.7 %gather_fusion = bf16[1024,1024]{1,0:T(8,128)(2,1)} fusion(bf16[2048,1024]{1,0:T(8,128)(2,1)} %copy.16, s32[1024]{0:T(1024)S(1)} %broadcast_clamp_fusion.1), kind=kCustom, calls=%fused_computation | custom fusion | bytes 4198400 | tf_op jit(solution)/shard_map/jit(_take)/gather | solution.py:101
  87.4 14.3 %shard_map.55 = f32[32,1024]{1,0:T(8,128)} custom-call(bf16[32,56,128]{2,1,0:T(8,128)(2,1)} %copy.17.weight_ref, bf16[32,32,1024]{2,1,0:T(8,128)(2,1)} %bitcast.16), custom_call_target="tpu_custom_call" | custom-call | tf_op jit(solution)/shard_map/pallas_call | solution.py:69
  (6 shorter events, 0.1 us)
Async XLA Ops:
  6.5 65.7 %all-gather.2.cloned.1.call-start = ((), (), s32[]{:S(2)}) async-start(), calls=%async_computation | async-start | bytes 4456448 | tf_op jit(solution)/shard_map/all_gather | solution.py:97
  8.3 8.1 %copy-start.2 = (s32[32,32]{1,0:T(8,128)S(1)}, s32[32,32]{1,0:T(8,128)}, u32[]{:S(2)}) copy-start(s32[32,32]{1,0:T(8,128)} %param.10) | copy-start | bytes 12292
  8.3 8.2 %copy-start.1 = (bf16[32,32,200]{2,1,0:T(8,128)(2,1)S(1)}, bf16[32,32,200]{2,1,0:T(8,128)(2,1)}, u32[]{:S(2)}) copy-start(bf16[32,32,200]{2,1,0:T(8,128)(2,1)} %param.11) | copy-start | bytes 1228804
  12.5 3.3 %collective-permute-start = (f32[8,2048]{1,0:T(8,128)S(1)}, f32[8,2048]{1,0:T(8,128)S(1)}, u32[]{:S(2)}, u32[]{:S(2)}) collective-permute-start(f32[8,2048]{1,0:T(8,128)S(1)} %slice.33), channel_id=1, source_target_pairs={{0,1},{1,2},{2,3},{3,4},{4,5},{5,6},{6,7},{7,8},{8,9},{9,10},{10,1... | collective-permute-start | bytes 196616 | tf_op jit(solution)/shard_map/ppermute | solution.py:93
  15.7 0.7 copy-start
Sparse Core Ops, SparseCore 0:
  16.6 55.5 all-gather.1

commit v8 on v7

--- a/solution.py
+++ b/solution.py
@@ -93,13 +93,13 @@
     carried = lax.ppermute(partial[local_j:], "handler", [(i, i + 1) for i in range(n_handler - 1)])
     own = partial[:local_j]
     own = own.at[:halo].add(carried)
-    green = own.astype(jnp.bfloat16).T
-    piece = lax.all_gather(green, "handler", axis=1, tiled=True)
-    length = piece.shape[0]
+    by_time = lax.all_gather(own.astype(jnp.bfloat16), "handler", axis=0, tiled=True)
+    length = by_time.shape[1]
     v_local, k = index.shape
     flat_index = jnp.clip(index.reshape(-1), 0, length - 1)
-    rows = jnp.take(piece, flat_index, axis=0, mode="clip")
-    picked = rows.reshape(v_local, k, piece.shape[1])
+    choose = (flat_index[:, None] == lax.broadcasted_iota(jnp.int32, (flat_index.shape[0], length), 1))
+    rows = jnp.einsum("np,jp->nj", choose.astype(jnp.bfloat16), by_time, preferred_element_type=jnp.float32)
+    picked = rows.astype(jnp.bfloat16).reshape(v_local, k, by_time.shape[0])
     return convolve(picked, slip)
 
 

time: 109 us -> 102 us (0.936)
  local copies, waits for them, and re-layouts: 21.2 us -> 6 us
  matrix products: 4.11 us -> 12.2 us
    gather x1 -> x0, local copies, waits for them, and re-layouts: 8.73 us -> none  [body(): rows = jnp.take(piece, flat_index, axis=0, mode='clip')]
    dot_general x0 -> x1, matrix products: none -> 8.07 us  [body(): jnp.einsum('np,jp->nj', choose.astype(jnp.bfloat16), by_time, preferred_e...]
    all_gather x1 -> x0, local copies, waits for them, and re-layouts: 6.41 us -> none  [body(): piece = lax.all_gather(green, 'handler', axis=1, tiled=True)]
where the time goes in v8:
time: 102 us; the launch traced here: 101 us
  waiting for transfers between devices  51.3 us (50%)
  Pallas kernels  14.3 us (14%)
  between operations  13.5 us (13%)
  matrix products  12.2 us (12%)
  local copies, waits for them, and re-layouts  6 us (6%)
  starting transfers between devices  2.36 us (2%)
  other arithmetic  1.8 us (2%)
    all_gather x1, waiting for transfers between devices, body(): lax.all_gather(own.astype(jnp.bfloat16), 'handler', axis=0, tiled=True)  50.4 us
    pallas_call x1, Pallas kernels, convolve(): pl.pallas_call(conv_kernel, grid=(v_local // vb,), in_specs=[pl.BlockSpec...  14.3 us
    dot_general x1, matrix products, body(): jnp.einsum('np,jp->nj', choose.astype(jnp.bfloat16), by_time, preferred_e...  8.07 us
    dot_general x1, matrix products, body(): jnp.einsum('tj,ctp->cjp', lowpass, by_component, preferred_element_type=j...  4.11 us
    ppermute x1, starting transfers between devices, body(): lax.ppermute(partial[local_j:], 'handler', [(i, i + 1) for i in range(n_h...  2.36 us
    transpose x1, local copies, waits for them, and re-layouts, convolve(): padded.reshape(v_local, k, n_rows, SHIFTS).transpose(0, 2, 3, 1)  2.28 us
    unnamed x7, local copies, waits for them, and re-layouts  2.18 us
  transfers between devices with their start and end apart: 2, of which 2 were waited for; matrix products, arithmetic and copies ran while one was open for 5% of the time, Pallas kernels for 0%

profile of v8, /device:TPU:0, one launch (start us, length us, event | category | flops | bytes accessed | tf_op | source)
XLA Modules:
  0.0 101.4 jit_solution(3590149367071029894)
XLA Ops:
  6.5 0.0 all-gather.2.cloned.1.call-start
  6.5 0.7 convert_element_type.15
  7.2 1.1 %select_reduce_fusion = bf16[256,72]{0,1:T(8,128)(2,1)S(1)} fusion(f32[32]{0:T(128)S(1)} %convert_element_type.15, s32[72]{0:T(128)S(1)} %iota_multiply_fusion), kind=kLoop, calls=%fused_computation.6 | loop fusion | flops 2340864 | bytes 37280 | tf_op jit(solution)/shard_map/reduce_sum | solution.py:19
  8.3 0.0 copy-start.2
  8.3 0.0 copy-start.1
  8.4 4.1 %multiply_reduce_fusion = f32[72,2048]{1,0:T(8,128)S(1)} fusion(bf16[256,6,2048]{2,0,1:T(8,128)(2,1)} %param.7, f32[6,2048]{1,0:T(8,128)} %param.9, bf16[256,72]{0,1:T(8,128)(2,1)S(1)} %select_reduce_fusion), kind=kOutput, calls=%fused_computation.5 | convolution fusion | flops 454606848 | bytes 6967296 | tf_op jit(solution)/shard_map/tj,ctp->cjp/dot_general | solution.py:91
  12.5 2.4 %collective-permute-start = (f32[8,2048]{1,0:T(8,128)S(1)}, f32[8,2048]{1,0:T(8,128)S(1)}, u32[]{:S(2)}, u32[]{:S(2)}) collective-permute-start(f32[8,2048]{1,0:T(8,128)S(1)} %slice.31), channel_id=1, source_target_pairs={{0,1},{1,2},{2,3},{3,4},{4,5},{5,6},{6,7},{7,8},{8,9},{9,10},{10,1... | collective-permute-start | bytes 196616 | tf_op jit(solution)/shard_map/ppermute | solution.py:93
  14.9 0.8 collective-permute-done
  15.7 0.0 copy-start
  15.8 0.7 copy-done
  16.4 0.0 all-gather.2.cloned.1.call-update
  16.5 0.0 copy-done.2
  16.5 0.1 min.12
  16.6 0.0 copy-done.1
  16.6 1.5 %copy.13 = bf16[32,32,200]{1,0,2:T(8,128)(2,1)S(1)} copy(bf16[32,32,200]{2,1,0:T(8,128)(2,1)S(1)} %copy-done.1) | data formatting | bytes 819200
  18.1 0.3 pad.6.clone
  18.4 2.3 %copy.11 = bf16[32,56,4,32]{1,3,2,0:T(8,128)(2,1)S(1)} copy(bf16[32,56,4,32]{3,0,2,1:T(8,128)(2,1)S(1)} %bitcast.14) | data formatting | bytes 917504 | tf_op jit(solution)/shard_map/transpose | solution.py:67
  20.7 1.1 %copy.12.weight_ref = bf16[32,56,128]{2,1,0:T(8,128)(2,1)} copy(bf16[32,56,128]{1,2,0:T(8,128)(2,1)S(1)} %bitcast.15) | data formatting | bytes 917504 | tf_op jit(solution)/shard_map/reshape | solution.py:67
  21.8 50.4 %all-gather.2.cloned.1.call-done = bf16[1024,2048]{1,0:T(8,128)(2,1)} async-done(((bf16[64,2048]{1,0:T(8,128)(2,1)}), bf16[1024,2048]{1,0:T(8,128)(2,1)}) %all-gather.2.cloned.1.call-update) | async-done | bytes 4194320 | tf_op jit(solution)/shard_map/all_gather | solution.py:96
  72.2 8.1 %fusion.6 = bf16[1024,1024]{1,0:T(8,128)(2,1)} fusion(bf16[1024,2048]{1,0:T(8,128)(2,1)} %all-gather.2.cloned.1.call-done, s32[1024]{0:T(1024)S(1)} %min.12), kind=kOutput, calls=%fused_computation.8 | convolution fusion | flops 4298113024 | bytes 6295552 | tf_op jit(solution)/shard_map/np,jp->nj/dot_general | solution.py:101
  80.3 14.3 %shard_map.55 = f32[32,1024]{1,0:T(8,128)} custom-call(bf16[32,56,128]{2,1,0:T(8,128)(2,1)} %copy.12.weight_ref, bf16[32,32,1024]{2,1,0:T(8,128)(2,1)} %bitcast.16), custom_call_target="tpu_custom_call" | custom-call | tf_op jit(solution)/shard_map/pallas_call | solution.py:69
  (5 shorter events, 0.1 us)
Async XLA Ops:
  6.5 65.7 %all-gather.2.cloned.1.call-start = ((), (), s32[]{:S(2)}) async-start(), calls=%async_computation | async-start | bytes 4456448 | tf_op jit(solution)/shard_map/all_gather | solution.py:96
  8.3 8.1 %copy-start.2 = (s32[32,32]{1,0:T(8,128)S(1)}, s32[32,32]{1,0:T(8,128)}, u32[]{:S(2)}) copy-start(s32[32,32]{1,0:T(8,128)} %param.10) | copy-start | bytes 12292
  8.3 8.2 %copy-start.1 = (bf16[32,32,200]{2,1,0:T(8,128)(2,1)S(1)}, bf16[32,32,200]{2,1,0:T(8,128)(2,1)}, u32[]{:S(2)}) copy-start(bf16[32,32,200]{2,1,0:T(8,128)(2,1)} %param.11) | copy-start | bytes 1228804
  12.5 3.3 %collective-permute-start = (f32[8,2048]{1,0:T(8,128)S(1)}, f32[8,2048]{1,0:T(8,128)S(1)}, u32[]{:S(2)}, u32[]{:S(2)}) collective-permute-start(f32[8,2048]{1,0:T(8,128)S(1)} %slice.31), channel_id=1, source_target_pairs={{0,1},{1,2},{2,3},{3,4},{4,5},{5,6},{6,7},{7,8},{8,9},{9,10},{10,1... | collective-permute-start | bytes 196616 | tf_op jit(solution)/shard_map/ppermute | solution.py:93
  15.7 0.7 copy-start
Sparse Core Ops, SparseCore 0:
  16.6 55.5 all-gather.1

commit v9 on v8

--- a/solution.py
+++ b/solution.py
@@ -79,27 +79,35 @@
     )(weight, picked)
 
 
+N_CHUNKS = 2
+
+
 def body(sgt, taps, moment, index, slip):
     n_handler = lax.axis_size("handler")
-    me = lax.axis_index("handler")
     local_t = sgt.shape[0]
     local_j = local_t // DEC
     n_taps = taps.shape[0]
     halo = (n_taps - 1 + DEC - 1) // DEC
+    length = sgt.shape[2]
+    width = length // N_CHUNKS
+    v_local, k = index.shape
+    flat_index = jnp.clip(index.reshape(-1), 0, length - 1)
     lowpass = lax.optimization_barrier(band_matrix(taps, local_t, local_j + halo))
     by_component = jnp.transpose(sgt, (1, 0, 2))
-    filtered = jnp.einsum("tj,ctp->cjp", lowpass, by_component, preferred_element_type=jnp.float32)
-    partial = jnp.sum(moment[:, None, :] * filtered, axis=0)
-    carried = lax.ppermute(partial[local_j:], "handler", [(i, i + 1) for i in range(n_handler - 1)])
-    own = partial[:local_j]
-    own = own.at[:halo].add(carried)
-    by_time = lax.all_gather(own.astype(jnp.bfloat16), "handler", axis=0, tiled=True)
-    length = by_time.shape[1]
-    v_local, k = index.shape
-    flat_index = jnp.clip(index.reshape(-1), 0, length - 1)
-    choose = (flat_index[:, None] == lax.broadcasted_iota(jnp.int32, (flat_index.shape[0], length), 1))
-    rows = jnp.einsum("np,jp->nj", choose.astype(jnp.bfloat16), by_time, preferred_element_type=jnp.float32)
-    picked = rows.astype(jnp.bfloat16).reshape(v_local, k, by_time.shape[0])
+    rows = None
+    for chunk in range(N_CHUNKS):
+        cols = slice(chunk * width, (chunk + 1) * width)
+        filtered = jnp.einsum("tj,ctp->cjp", lowpass, by_component[:, :, cols], preferred_element_type=jnp.float32)
+        partial = jnp.sum(moment[:, None, cols] * filtered, axis=0)
+        carried = lax.ppermute(partial[local_j:], "handler", [(i, i + 1) for i in range(n_handler - 1)])
+        own = partial[:local_j]
+        own = own.at[:halo].add(carried)
+        by_time = lax.all_gather(own.astype(jnp.bfloat16), "handler", axis=0, tiled=True)
+        point_ids = chunk * width + lax.broadcasted_iota(jnp.int32, (flat_index.shape[0], width), 1)
+        choose = (flat_index[:, None] == point_ids).astype(jnp.bfloat16)
+        part = jnp.einsum("np,jp->nj", choose, by_time, preferred_element_type=jnp.float32)
+        rows = part if rows is None else rows + part
+    picked = rows.astype(jnp.bfloat16).reshape(v_local, k, rows.shape[1])
     return convolve(picked, slip)
 
 

time: 102 us -> 132 us (1.29)
  waiting for transfers between devices: 51.3 us -> 70.1 us
  matrix products: 12.2 us -> 17.7 us
  starting transfers between devices: 2.36 us -> 7.1 us
  local copies, waits for them, and re-layouts: 6 us -> 7.46 us
    all_gather x1 -> x2, waiting for transfers between devices: 50.4 us -> 68.4 us  [body(): lax.all_gather(own.astype(jnp.bfloat16), 'handler', axis=0, tiled=True)]
    dot_general x2 -> x4, matrix products: 12.2 us -> 17.7 us  [the longest x2 12.4 us: body(): jnp.einsum('np,jp->nj', choose, by_time, preferred_element_type=jnp.float32)]
    ppermute x1 -> x2, starting transfers between devices: 2.36 us -> 7.06 us  [body(): lax.ppermute(partial[local_j:], 'handler', [(i, i + 1) for i in range(n_h...]
    unnamed x7 -> x9, local copies, waits for them, and re-layouts: 2.18 us -> 2.8 us
  transfers between devices with their start and end apart: 2 -> 4, of which waited for: 2 -> 4; matrix products, arithmetic and copies ran while one was open for 5% -> 11% of each run, Pallas kernels for 0% -> 0%
where the time goes in v9:
time: 132 us
  waiting for transfers between devices  70.1 us (53%)
  matrix products  17.7 us (13%)
  Pallas kernels  14.3 us (11%)
  between operations  13.5 us (10%)
  local copies, waits for them, and re-layouts  7.46 us (6%)
  starting transfers between devices  7.1 us (5%)
  other arithmetic  1.81 us (1%)
    all_gather x2, waiting for transfers between devices, body(): lax.all_gather(own.astype(jnp.bfloat16), 'handler', axis=0, tiled=True)  68.4 us
    pallas_call x1, Pallas kernels, convolve(): pl.pallas_call(conv_kernel, grid=(v_local // vb,), in_specs=[pl.BlockSpec...  14.3 us
    dot_general x2, matrix products, body(): jnp.einsum('np,jp->nj', choose, by_time, preferred_element_type=jnp.float32)  12.4 us
    ppermute x2, starting transfers between devices, body(): lax.ppermute(partial[local_j:], 'handler', [(i, i + 1) for i in range(n_h...  7.06 us
    dot_general x2, matrix products, body(): jnp.einsum('tj,ctp->cjp', lowpass, by_component[:, :, cols], preferred_el...  5.23 us
    unnamed x9, local copies, waits for them, and re-layouts  2.8 us
  transfers between devices with their start and end apart: 4, of which 4 were waited for; matrix products, arithmetic and copies ran while one was open for 11% of the time, Pallas kernels for 0%

profile of v9, /device:TPU:0, one launch (start us, length us, event | category | flops | bytes accessed | tf_op | source)
XLA Modules:
  0.0 131.9 jit_solution(3455311439973535524)
XLA Ops:
  6.5 0.0 all-gather.5.cloned.1.call-start
  6.5 0.8 fusion.18
  7.3 0.7 convert_element_type.19
  8.0 1.1 select_reduce_fusion
  9.1 2.6 %multiply_reduce_fusion = f32[72,1024]{1,0:T(8,128)S(1)} fusion(bf16[6,256,2048]{2,1,0:T(8,128)(2,1)} %bitcast.16, f32[6,1024]{1,0:T(8,128)S(1)} %get-tuple-element.30, bf16[256,72]{0,1:T(8,128)(2,1)S(1)} %select_reduce_fusion), kind=kOutput, calls=%fused_computation.14 | convolution fusion | flops 227303424 | bytes 3502080 | tf_op jit(solution)/shard_map/tj,ctp->cjp/dot_general | solution.py:100
  11.7 2.4 %collective-permute-start.1 = (f32[8,1024]{1,0:T(8,128)S(1)}, f32[8,1024]{1,0:T(8,128)S(1)}, u32[]{:S(2)}, u32[]{:S(2)}) collective-permute-start(f32[8,1024]{1,0:T(8,128)S(1)} %slice.81), channel_id=1, source_target_pairs={{0,1},{1,2},{2,3},{3,4},{4,5},{5,6},{6,7},{7,8},{8,9},{9,10},{10,1... | collective-permute-start | bytes 98312 | tf_op jit(solution)/shard_map/ppermute | solution.py:102
  14.1 0.8 collective-permute-done.1
  14.9 0.0 copy-start
  14.9 0.7 copy-done
  15.6 0.0 all-gather.5.cloned.1.call-update
  15.6 0.0 all-gather.3.cloned.1.call-start
  15.7 0.0 copy-start.3
  15.7 0.0 copy-start.2
  15.7 2.6 %multiply_reduce_fusion.1 = f32[72,1024]{1,0:T(8,128)S(1)} fusion(bf16[6,256,2048]{2,1,0:T(8,128)(2,1)} %bitcast.17, f32[6,1024]{1,0:T(8,128)S(1)} %get-tuple-element.29, bf16[256,72]{0,1:T(8,128)(2,1)S(1)} %select_reduce_fusion), kind=kOutput, calls=%fused_computation.15 | convolution fusion | flops 227303424 | bytes 3502080 | tf_op jit(solution)/shard_map/tj,ctp->cjp/dot_general | solution.py:100
  18.3 4.7 %collective-permute-start = (f32[8,1024]{1,0:T(8,128)S(1)}, f32[8,1024]{1,0:T(8,128)S(1)}, u32[]{:S(2)}, u32[]{:S(2)}) collective-permute-start(f32[8,1024]{1,0:T(8,128)S(1)} %slice.77), channel_id=1, source_target_pairs={{0,1},{1,2},{2,3},{3,4},{4,5},{5,6},{6,7},{7,8},{8,9},{9,10},{10,1... | collective-permute-start | bytes 98312 | tf_op jit(solution)/shard_map/ppermute | solution.py:102
  23.1 0.8 collective-permute-done
  23.9 0.0 copy-start.1
  23.9 0.6 copy-done.1
  24.5 0.0 all-gather.3.cloned.1.call-update
  24.6 0.0 copy-done.3
  24.6 0.1 min.12
  24.7 0.0 copy-done.2
  24.7 1.5 %copy.13 = bf16[32,32,200]{1,0,2:T(8,128)(2,1)S(1)} copy(bf16[32,32,200]{2,1,0:T(8,128)(2,1)S(1)} %copy-done.2) | data formatting | bytes 819200
  26.1 0.3 pad.8.clone
  26.5 2.3 %copy.11 = bf16[32,56,4,32]{1,3,2,0:T(8,128)(2,1)S(1)} copy(bf16[32,56,4,32]{3,0,2,1:T(8,128)(2,1)S(1)} %bitcast.13) | data formatting | bytes 917504 | tf_op jit(solution)/shard_map/transpose | solution.py:67
  28.8 1.2 copy.12.weight_ref
  29.9 31.9 %all-gather.5.cloned.1.call-done = bf16[1024,1024]{1,0:T(8,128)(2,1)} async-done(((bf16[64,1024]{1,0:T(8,128)(2,1)}), bf16[1024,1024]{1,0:T(8,128)(2,1)}) %all-gather.5.cloned.1.call-update) | async-done | bytes 2097168 | tf_op jit(solution)/shard_map/all_gather | solution.py:105
  61.9 5.9 %fusion.1 = f32[1024,1024]{1,0:T(8,128)} fusion(bf16[1024,1024]{1,0:T(8,128)(2,1)} %all-gather.5.cloned.1.call-done, s32[1024]{0:T(1024)S(1)} %iota_add_fusion, s32[1024]{0:T(1024)S(1)} %min.12), kind=kOutput, calls=%fused_computation.3 | convolution fusion | flops 2148532224 | bytes 6299648 | tf_op jit(solution)/shard_map/np,jp->nj/dot_general | solution.py:108
  67.8 36.5 %all-gather.3.cloned.1.call-done = bf16[1024,1024]{1,0:T(8,128)(2,1)} async-done(((bf16[64,1024]{1,0:T(8,128)(2,1)}), bf16[1024,1024]{1,0:T(8,128)(2,1)}) %all-gather.3.cloned.1.call-update) | async-done | bytes 2097168 | tf_op jit(solution)/shard_map/all_gather | solution.py:105
  104.2 6.5 %add_convert_fusion = bf16[1024,1024]{1,0:T(8,128)(2,1)} fusion(f32[1024,1024]{1,0:T(8,128)} %fusion.1, bf16[1024,1024]{1,0:T(8,128)(2,1)} %all-gather.3.cloned.1.call-done, s32[1024]{0:T(1024)S(1)} %min.12), kind=kOutput, calls=%fused_computation | convolution fusion | flops 2150629376 | bytes 8392704 | tf_op jit(solution)/shard_map/np,jp->nj/dot_general | solution.py:108
  110.8 14.3 %shard_map.55 = f32[32,1024]{1,0:T(8,128)} custom-call(bf16[32,56,128]{2,1,0:T(8,128)(2,1)} %copy.12.weight_ref, bf16[32,32,1024]{2,1,0:T(8,128)(2,1)} %bitcast.15), custom_call_target="tpu_custom_call" | custom-call | tf_op jit(solution)/shard_map/pallas_call | solution.py:69
  (9 shorter events, 0.1 us)
Async XLA Ops:
  6.5 55.3 %all-gather.5.cloned.1.call-start = ((), (), s32[]{:S(2)}) async-start(), calls=%async_computation.1 | async-start | bytes 2228224 | tf_op jit(solution)/shard_map/all_gather | solution.py:105
  11.7 3.2 %collective-permute-start.1 = (f32[8,1024]{1,0:T(8,128)S(1)}, f32[8,1024]{1,0:T(8,128)S(1)}, u32[]{:S(2)}, u32[]{:S(2)}) collective-permute-start(f32[8,1024]{1,0:T(8,128)S(1)} %slice.81), channel_id=1, source_target_pairs={{0,1},{1,2},{2,3},{3,4},{4,5},{5,6},{6,7},{7,8},{8,9},{9,10},{10,1... | collective-permute-start | bytes 98312 | tf_op jit(solution)/shard_map/ppermute | solution.py:102
  14.9 0.7 copy-start
  15.6 88.6 %all-gather.3.cloned.1.call-start = ((), (), s32[]{:S(2)}) async-start(), calls=%async_computation | async-start | bytes 2228224 | tf_op jit(solution)/shard_map/all_gather | solution.py:105
  15.7 8.9 %copy-start.3 = (s32[32,32]{1,0:T(8,128)S(1)}, s32[32,32]{1,0:T(8,128)}, u32[]{:S(2)}) copy-start(s32[32,32]{1,0:T(8,128)} %param.12) | copy-start | bytes 12292
  15.7 9.0 %copy-start.2 = (bf16[32,32,200]{2,1,0:T(8,128)(2,1)S(1)}, bf16[32,32,200]{2,1,0:T(8,128)(2,1)}, u32[]{:S(2)}) copy-start(bf16[32,32,200]{2,1,0:T(8,128)(2,1)} %param.13) | copy-start | bytes 1228804
  18.3 5.5 %collective-permute-start = (f32[8,1024]{1,0:T(8,128)S(1)}, f32[8,1024]{1,0:T(8,128)S(1)}, u32[]{:S(2)}, u32[]{:S(2)}) collective-permute-start(f32[8,1024]{1,0:T(8,128)S(1)} %slice.77), channel_id=1, source_target_pairs={{0,1},{1,2},{2,3},{3,4},{4,5},{5,6},{6,7},{7,8},{8,9},{9,10},{10,1... | collective-permute-start | bytes 98312 | tf_op jit(solution)/shard_map/ppermute | solution.py:102
  23.9 0.7 copy-start.1
Sparse Core Ops, SparseCore 0:
  15.7 46.1 all-gather.4
  64.0 40.1 all-gather.2

commit v10 on v8

--- a/solution.py
+++ b/solution.py
@@ -19,7 +19,7 @@
     return jnp.sum(picked, axis=2).astype(jnp.bfloat16)
 
 
-SHIFTS = 4
+SHIFTS = 2
 
 
 def conv_kernel(weight_ref, picked_ref, out_ref, shifted_ref):
@@ -88,10 +88,12 @@
     halo = (n_taps - 1 + DEC - 1) // DEC
     lowpass = lax.optimization_barrier(band_matrix(taps, local_t, local_j + halo))
     by_component = jnp.transpose(sgt, (1, 0, 2))
-    filtered = jnp.einsum("tj,ctp->cjp", lowpass, by_component, preferred_element_type=jnp.float32)
-    partial = jnp.sum(moment[:, None, :] * filtered, axis=0)
-    carried = lax.ppermute(partial[local_j:], "handler", [(i, i + 1) for i in range(n_handler - 1)])
-    own = partial[:local_j]
+    tail = jnp.einsum("tj,ctp->cjp", lowpass[local_t - n_taps:, local_j:], by_component[:, local_t - n_taps:, :],
+                      preferred_element_type=jnp.float32)
+    carried = lax.ppermute(jnp.sum(moment[:, None, :] * tail, axis=0), "handler",
+                           [(i, i + 1) for i in range(n_handler - 1)])
+    filtered = jnp.einsum("tj,ctp->cjp", lowpass[:, :local_j], by_component, preferred_element_type=jnp.float32)
+    own = jnp.sum(moment[:, None, :] * filtered, axis=0)
     own = own.at[:halo].add(carried)
     by_time = lax.all_gather(own.astype(jnp.bfloat16), "handler", axis=0, tiled=True)
     length = by_time.shape[1]

time: 102 us -> 101 us (level)
  waiting for transfers between devices: 51.3 us -> 48.5 us
  matrix products: 12.2 us -> 13.6 us
  local copies, waits for them, and re-layouts: 6 us -> 4.82 us
    all_gather x1, waiting for transfers between devices: 50.4 us -> 48.4 us  [body(): lax.all_gather(own.astype(jnp.bfloat16), 'handler', axis=0, tiled=True)]
    dot_general x1 -> x2, matrix products: 4.11 us -> 5.48 us  [the longest x1 4.05 us: body(): jnp.einsum('tj,ctp->cjp', lowpass[:, :local_j], by_component, preferred_e...]
    unnamed x7 -> x5, local copies, waits for them, and re-layouts: 2.18 us -> 1.5 us
  transfers between devices with their start and end apart: 2 -> 2, of which waited for: 2 -> 1; matrix products, arithmetic and copies ran while one was open for 5% -> 9% of each run, Pallas kernels for 0% -> 0%
where the time goes in v10:
time: 101 us; the launch traced here: 100 us
  waiting for transfers between devices  48.5 us (48%)
  Pallas kernels  15.1 us (15%)
  matrix products  13.6 us (13%)
  between operations  13.5 us (13%)
  local copies, waits for them, and re-layouts  4.82 us (5%)
  other arithmetic  2.52 us (2%)
  starting transfers between devices  2.49 us (2%)
    all_gather x1, waiting for transfers between devices, body(): lax.all_gather(own.astype(jnp.bfloat16), 'handler', axis=0, tiled=True)  48.4 us
    pallas_call x1, Pallas kernels, convolve(): pl.pallas_call(conv_kernel, grid=(v_local // vb,), in_specs=[pl.BlockSpec...  15.1 us
    dot_general x1, matrix products, body(): jnp.einsum('np,jp->nj', choose.astype(jnp.bfloat16), by_time, preferred_e...  8.08 us
    dot_general x1, matrix products, body(): jnp.einsum('tj,ctp->cjp', lowpass[:, :local_j], by_component, preferred_e...  4.05 us
    ppermute x1, starting transfers between devices, body(): lax.ppermute(jnp.sum(moment[:, None, :] * tail, axis=0), 'handler', [(i,...  2.49 us
  transfers between devices with their start and end apart: 2, of which 1 were waited for; matrix products, arithmetic and copies ran while one was open for 9% of the time, Pallas kernels for 0%

profile of v10, /device:TPU:0, one launch (start us, length us, event | category | flops | bytes accessed | tf_op | source)
XLA Modules:
  0.0 100.4 jit_solution(3109690266318360043)
XLA Ops:
  6.5 0.0 all-gather.2.cloned.1.call-start
  6.5 0.7 convert_element_type.15
  7.2 1.1 %select_reduce_fusion = bf16[256,72]{0,1:T(8,128)(2,1)S(1)} fusion(f32[32]{0:T(128)S(1)} %convert_element_type.15, s32[72]{0:T(128)S(1)} %iota_multiply_fusion), kind=kLoop, calls=%fused_computation.4 | loop fusion | flops 2340864 | bytes 37280 | tf_op jit(solution)/shard_map/reduce_sum | solution.py:19
  8.3 1.4 %fusion.3 = f32[8,2048]{1,0:T(8,128)S(1)} fusion(bf16[6,256,2048]{2,1,0:T(8,128)(2,1)} %bitcast.16, f32[6,2048]{1,0:T(8,128)} %param.9, bf16[256,72]{0,1:T(8,128)(2,1)S(1)} %select_reduce_fusion), kind=kOutput, calls=%fused_computation.8 | convolution fusion | flops 6471680 | bytes 919552 | tf_op jit(solution)/shard_map/tj,ctp->cjp/dot_general | solution.py:91
  9.8 0.0 copy-start.1
  9.8 0.0 copy-start
  9.8 2.5 %collective-permute-start = (f32[8,2048]{1,0:T(8,128)S(1)}, f32[8,2048]{1,0:T(8,128)S(1)}, u32[]{:S(2)}, u32[]{:S(2)}) collective-permute-start(f32[8,2048]{1,0:T(8,128)S(1)} %fusion.3), channel_id=1, source_target_pairs={{0,1},{1,2},{2,3},{3,4},{4,5},{5,6},{6,7},{7,8},{8,9},{9,10},{10,1... | collective-permute-start | bytes 196616 | tf_op jit(solution)/shard_map/ppermute | solution.py:93
  12.3 4.0 %multiply_reduce_fusion = f32[64,2048]{1,0:T(8,128)S(1)} fusion(f32[6,2048]{1,0:T(8,128)} %param.9, bf16[256,72]{0,1:T(8,128)(2,1)S(1)} %select_reduce_fusion, bf16[256,6,2048]{2,0,1:T(8,128)(2,1)} %param.7), kind=kOutput, calls=%fused_computation.3 | convolution fusion | flops 404094976 | bytes 6897664 | tf_op jit(solution)/shard_map/tj,ctp->cjp/dot_general | solution.py:95
  16.3 0.0 collective-permute-done
  16.4 0.7 convert_element_type.17
  17.1 0.0 all-gather.2.cloned.1.call-update
  17.1 0.0 copy-done.1
  17.1 0.1 min.12
  17.2 0.0 copy-done
  17.2 1.5 %copy.13 = bf16[32,32,200]{1,0,2:T(8,128)(2,1)S(1)} copy(bf16[32,32,200]{2,1,0:T(8,128)(2,1)S(1)} %copy-done) | data formatting | bytes 819200
  18.7 0.3 pad.6.clone
  19.0 1.7 %copy.11 = bf16[32,104,2,32]{1,3,2,0:T(8,128)(2,1)S(1)} copy(bf16[32,104,2,32]{3,0,2,1:T(8,128)(2,1)S(1)} %bitcast.15) | data formatting | bytes 851968 | tf_op jit(solution)/shard_map/transpose | solution.py:67
  20.8 1.2 %copy.12.weight_ref = bf16[32,104,64]{2,1,0:T(8,128)(2,1)} copy(bf16[32,104,64]{1,2,0:T(8,128)(2,1)S(1)} %bitcast.17) | data formatting | bytes 851968 | tf_op jit(solution)/shard_map/reshape | solution.py:67
  22.0 48.4 %all-gather.2.cloned.1.call-done = bf16[1024,2048]{1,0:T(8,128)(2,1)} async-done(((bf16[64,2048]{1,0:T(8,128)(2,1)}), bf16[1024,2048]{1,0:T(8,128)(2,1)}) %all-gather.2.cloned.1.call-update) | async-done | bytes 4194320 | tf_op jit(solution)/shard_map/all_gather | solution.py:98
  70.4 8.1 %fusion.2 = bf16[1024,1024]{1,0:T(8,128)(2,1)} fusion(bf16[1024,2048]{1,0:T(8,128)(2,1)} %all-gather.2.cloned.1.call-done, s32[1024]{0:T(1024)S(1)} %min.12), kind=kOutput, calls=%fused_computation.7 | convolution fusion | flops 4298113024 | bytes 6295552 | tf_op jit(solution)/shard_map/np,jp->nj/dot_general | solution.py:103
  78.5 15.1 %shard_map.55 = f32[32,1024]{1,0:T(8,128)} custom-call(bf16[32,104,64]{2,1,0:T(8,128)(2,1)} %copy.12.weight_ref, bf16[32,32,1024]{2,1,0:T(8,128)(2,1)} %bitcast.18), custom_call_target="tpu_custom_call" | custom-call | tf_op jit(solution)/shard_map/pallas_call | solution.py:69
  (3 shorter events, 0.0 us)
Async XLA Ops:
  6.5 63.9 %all-gather.2.cloned.1.call-start = ((), (), s32[]{:S(2)}) async-start(), calls=%async_computation | async-start | bytes 4456448 | tf_op jit(solution)/shard_map/all_gather | solution.py:98
  9.8 7.4 %copy-start.1 = (s32[32,32]{1,0:T(8,128)S(1)}, s32[32,32]{1,0:T(8,128)}, u32[]{:S(2)}) copy-start(s32[32,32]{1,0:T(8,128)} %param.10) | copy-start | bytes 12292
  9.8 7.4 %copy-start = (bf16[32,32,200]{2,1,0:T(8,128)(2,1)S(1)}, bf16[32,32,200]{2,1,0:T(8,128)(2,1)}, u32[]{:S(2)}) copy-start(bf16[32,32,200]{2,1,0:T(8,128)(2,1)} %param.11) | copy-start | bytes 1228804
  9.8 6.6 %collective-permute-start = (f32[8,2048]{1,0:T(8,128)S(1)}, f32[8,2048]{1,0:T(8,128)S(1)}, u32[]{:S(2)}, u32[]{:S(2)}) collective-permute-start(f32[8,2048]{1,0:T(8,128)S(1)} %fusion.3), channel_id=1, source_target_pairs={{0,1},{1,2},{2,3},{3,4},{4,5},{5,6},{6,7},{7,8},{8,9},{9,10},{10,1... | collective-permute-start | bytes 196616 | tf_op jit(solution)/shard_map/ppermute | solution.py:93
Sparse Core Ops, SparseCore 0:
  17.2 53.1 all-gather.1

commit v11 on v10

--- a/solution.py
+++ b/solution.py
@@ -19,7 +19,7 @@
     return jnp.sum(picked, axis=2).astype(jnp.bfloat16)
 
 
-SHIFTS = 2
+SHIFTS = 4
 
 
 def conv_kernel(weight_ref, picked_ref, out_ref, shifted_ref):

time: 101 us -> 99.9 us (0.989)
  no operation moved by 1% of the time
where the time goes in v11:
time: 99.9 us; the launch traced here: 99.6 us
  waiting for transfers between devices  48 us (48%)
  Pallas kernels  14.3 us (14%)
  matrix products  13.6 us (14%)
  between operations  13.5 us (14%)
  local copies, waits for them, and re-layouts  5.27 us (5%)
  other arithmetic  2.52 us (3%)
  starting transfers between devices  2.49 us (2%)
    all_gather x1, waiting for transfers between devices, body(): lax.all_gather(own.astype(jnp.bfloat16), 'handler', axis=0, tiled=True)  48 us
    pallas_call x1, Pallas kernels, convolve(): pl.pallas_call(conv_kernel, grid=(v_local // vb,), in_specs=[pl.BlockSpec...  14.3 us
    dot_general x1, matrix products, body(): jnp.einsum('np,jp->nj', choose.astype(jnp.bfloat16), by_time, preferred_e...  8.08 us
    dot_general x1, matrix products, body(): jnp.einsum('tj,ctp->cjp', lowpass[:, :local_j], by_component, preferred_e...  4.05 us
    ppermute x1, starting transfers between devices, body(): lax.ppermute(jnp.sum(moment[:, None, :] * tail, axis=0), 'handler', [(i,...  2.49 us
    transpose x1, local copies, waits for them, and re-layouts, convolve(): padded.reshape(v_local, k, n_rows, SHIFTS).transpose(0, 2, 3, 1)  2.28 us
  transfers between devices with their start and end apart: 2, of which 1 were waited for; matrix products, arithmetic and copies ran while one was open for 9% of the time, Pallas kernels for 0%

profile of v11, /device:TPU:0, one launch (start us, length us, event | category | flops | bytes accessed | tf_op | source)
XLA Modules:
  0.0 99.6 jit_solution(9385561369064572633)
XLA Ops:
  6.5 0.0 all-gather.2.cloned.1.call-start
  6.5 0.7 convert_element_type.15
  7.2 1.1 %select_reduce_fusion = bf16[256,72]{0,1:T(8,128)(2,1)S(1)} fusion(f32[32]{0:T(128)S(1)} %convert_element_type.15, s32[72]{0:T(128)S(1)} %iota_multiply_fusion), kind=kLoop, calls=%fused_computation.4 | loop fusion | flops 2340864 | bytes 37280 | tf_op jit(solution)/shard_map/reduce_sum | solution.py:19
  8.3 1.4 %fusion.3 = f32[8,2048]{1,0:T(8,128)S(1)} fusion(bf16[6,256,2048]{2,1,0:T(8,128)(2,1)} %bitcast.16, f32[6,2048]{1,0:T(8,128)} %param.9, bf16[256,72]{0,1:T(8,128)(2,1)S(1)} %select_reduce_fusion), kind=kOutput, calls=%fused_computation.8 | convolution fusion | flops 6471680 | bytes 919552 | tf_op jit(solution)/shard_map/tj,ctp->cjp/dot_general | solution.py:91
  9.8 0.0 copy-start.1
  9.8 0.0 copy-start
  9.8 2.5 %collective-permute-start = (f32[8,2048]{1,0:T(8,128)S(1)}, f32[8,2048]{1,0:T(8,128)S(1)}, u32[]{:S(2)}, u32[]{:S(2)}) collective-permute-start(f32[8,2048]{1,0:T(8,128)S(1)} %fusion.3), channel_id=1, source_target_pairs={{0,1},{1,2},{2,3},{3,4},{4,5},{5,6},{6,7},{7,8},{8,9},{9,10},{10,1... | collective-permute-start | bytes 196616 | tf_op jit(solution)/shard_map/ppermute | solution.py:93
  12.3 4.0 %multiply_reduce_fusion = f32[64,2048]{1,0:T(8,128)S(1)} fusion(f32[6,2048]{1,0:T(8,128)} %param.9, bf16[256,72]{0,1:T(8,128)(2,1)S(1)} %select_reduce_fusion, bf16[256,6,2048]{2,0,1:T(8,128)(2,1)} %param.7), kind=kOutput, calls=%fused_computation.3 | convolution fusion | flops 404094976 | bytes 6897664 | tf_op jit(solution)/shard_map/tj,ctp->cjp/dot_general | solution.py:95
  16.3 0.0 collective-permute-done
  16.4 0.7 convert_element_type.17
  17.1 0.0 all-gather.2.cloned.1.call-update
  17.1 0.0 copy-done.1
  17.1 0.1 min.12
  17.2 0.0 copy-done
  17.2 1.5 %copy.13 = bf16[32,32,200]{1,0,2:T(8,128)(2,1)S(1)} copy(bf16[32,32,200]{2,1,0:T(8,128)(2,1)S(1)} %copy-done) | data formatting | bytes 819200
  18.7 0.3 pad.6.clone
  19.0 2.3 %copy.11 = bf16[32,56,4,32]{1,3,2,0:T(8,128)(2,1)S(1)} copy(bf16[32,56,4,32]{3,0,2,1:T(8,128)(2,1)S(1)} %bitcast.15) | data formatting | bytes 917504 | tf_op jit(solution)/shard_map/transpose | solution.py:67
  21.3 1.1 %copy.12.weight_ref = bf16[32,56,128]{2,1,0:T(8,128)(2,1)} copy(bf16[32,56,128]{1,2,0:T(8,128)(2,1)S(1)} %bitcast.17) | data formatting | bytes 917504 | tf_op jit(solution)/shard_map/reshape | solution.py:67
  22.4 48.0 %all-gather.2.cloned.1.call-done = bf16[1024,2048]{1,0:T(8,128)(2,1)} async-done(((bf16[64,2048]{1,0:T(8,128)(2,1)}), bf16[1024,2048]{1,0:T(8,128)(2,1)}) %all-gather.2.cloned.1.call-update) | async-done | bytes 4194320 | tf_op jit(solution)/shard_map/all_gather | solution.py:98
  70.4 8.1 %fusion.2 = bf16[1024,1024]{1,0:T(8,128)(2,1)} fusion(bf16[1024,2048]{1,0:T(8,128)(2,1)} %all-gather.2.cloned.1.call-done, s32[1024]{0:T(1024)S(1)} %min.12), kind=kOutput, calls=%fused_computation.7 | convolution fusion | flops 4298113024 | bytes 6295552 | tf_op jit(solution)/shard_map/np,jp->nj/dot_general | solution.py:103
  78.5 14.3 %shard_map.55 = f32[32,1024]{1,0:T(8,128)} custom-call(bf16[32,56,128]{2,1,0:T(8,128)(2,1)} %copy.12.weight_ref, bf16[32,32,1024]{2,1,0:T(8,128)(2,1)} %bitcast.18), custom_call_target="tpu_custom_call" | custom-call | tf_op jit(solution)/shard_map/pallas_call | solution.py:69
  (3 shorter events, 0.0 us)
Async XLA Ops:
  6.5 63.9 %all-gather.2.cloned.1.call-start = ((), (), s32[]{:S(2)}) async-start(), calls=%async_computation | async-start | bytes 4456448 | tf_op jit(solution)/shard_map/all_gather | solution.py:98
  9.8 7.4 %copy-start.1 = (s32[32,32]{1,0:T(8,128)S(1)}, s32[32,32]{1,0:T(8,128)}, u32[]{:S(2)}) copy-start(s32[32,32]{1,0:T(8,128)} %param.10) | copy-start | bytes 12292
  9.8 7.4 %copy-start = (bf16[32,32,200]{2,1,0:T(8,128)(2,1)S(1)}, bf16[32,32,200]{2,1,0:T(8,128)(2,1)}, u32[]{:S(2)}) copy-start(bf16[32,32,200]{2,1,0:T(8,128)(2,1)} %param.11) | copy-start | bytes 1228804
  9.8 6.6 %collective-permute-start = (f32[8,2048]{1,0:T(8,128)S(1)}, f32[8,2048]{1,0:T(8,128)S(1)}, u32[]{:S(2)}, u32[]{:S(2)}) collective-permute-start(f32[8,2048]{1,0:T(8,128)S(1)} %fusion.3), channel_id=1, source_target_pairs={{0,1},{1,2},{2,3},{3,4},{4,5},{5,6},{6,7},{7,8},{8,9},{9,10},{10,1... | collective-permute-start | bytes 196616 | tf_op jit(solution)/shard_map/ppermute | solution.py:93
Sparse Core Ops, SparseCore 0:
  17.2 53.1 all-gather.1

commit v12 on v11

--- a/solution.py
+++ b/solution.py
@@ -34,14 +34,15 @@
     row = lax.broadcasted_iota(jnp.int32, (8, edge), 0)
     lag = col - SHIFTS * row
 
-    def one(v, carry):
+    for v in range(vb):
+        slot = v % 2
         rows = picked_ref[v]
-        shifted_ref[0:k, :] = rows
+        shifted_ref[slot, 0:k, :] = rows
         for b in range(1, SHIFTS):
             moved = pltpu.roll(rows, b, 1)
-            shifted_ref[b * k:(b + 1) * k, :128] = jnp.where(col_in >= b, moved[:, :128], jnp.zeros_like(moved[:, :128]))
-            shifted_ref[b * k:(b + 1) * k, 128:] = moved[:, 128:]
-        spread = jnp.dot(weight_ref[v], shifted_ref[...], preferred_element_type=jnp.float32)
+            shifted_ref[slot, b * k:(b + 1) * k, :128] = jnp.where(col_in >= b, moved[:, :128], jnp.zeros_like(moved[:, :128]))
+            shifted_ref[slot, b * k:(b + 1) * k, 128:] = moved[:, 128:]
+        spread = jnp.dot(weight_ref[v], shifted_ref[slot], preferred_element_type=jnp.float32)
         head = jnp.zeros((8, edge), jnp.float32)
         tail = jnp.zeros((8, width - edge), jnp.float32)
         for q in range(n_rows // 8):
@@ -50,12 +51,9 @@
             head = head + jnp.where(lag >= 8 * SHIFTS * q, moved[:, :edge], 0.0)
             if width > edge:
                 tail = tail + moved[:, edge:]
-        out_ref[pl.ds(v, 1), :edge] = jnp.sum(head, axis=0, keepdims=True)
+        out_ref[v:v + 1, :edge] = jnp.sum(head, axis=0, keepdims=True)
         if width > edge:
-            out_ref[pl.ds(v, 1), edge:] = jnp.sum(tail, axis=0, keepdims=True)
-        return carry
-
-    lax.fori_loop(0, vb, one, 0)
+            out_ref[v:v + 1, edge:] = jnp.sum(tail, axis=0, keepdims=True)
 
 
 def convolve(picked, slip):
@@ -75,7 +73,7 @@
         ],
         out_specs=pl.BlockSpec((vb, width), lambda i: (i, 0)),
         out_shape=jax.ShapeDtypeStruct((v_local, width), jnp.float32),
-        scratch_shapes=[pltpu.VMEM((SHIFTS * k, width), jnp.bfloat16)],
+        scratch_shapes=[pltpu.VMEM((2, SHIFTS * k, width), jnp.bfloat16)],
     )(weight, picked)
 
 

time: 99.9 us -> 95 us (0.951)
  Pallas kernels: 14.3 us -> 9.42 us
    pallas_call x1, Pallas kernels: 14.3 us -> 9.42 us  [convolve(): pl.pallas_call(conv_kernel, grid=(v_local // vb,), in_specs=[pl.BlockSpec...]
  transfers between devices with their start and end apart: 2 -> 2, of which waited for: 1 -> 1; matrix products, arithmetic and copies ran while one was open for 9% -> 10% of each run, Pallas kernels for 0% -> 0%
where the time goes in v12:
time: 95 us; the launch traced here: 94.8 us
  waiting for transfers between devices  48 us (51%)
  matrix products  13.6 us (14%)
  between operations  13.5 us (14%)
  Pallas kernels  9.42 us (10%)
  local copies, waits for them, and re-layouts  5.27 us (6%)
  other arithmetic  2.52 us (3%)
  starting transfers between devices  2.49 us (3%)
    all_gather x1, waiting for transfers between devices, body(): lax.all_gather(own.astype(jnp.bfloat16), 'handler', axis=0, tiled=True)  48 us
    pallas_call x1, Pallas kernels, convolve(): pl.pallas_call(conv_kernel, grid=(v_local // vb,), in_specs=[pl.BlockSpec...  9.42 us
    dot_general x1, matrix products, body(): jnp.einsum('np,jp->nj', choose.astype(jnp.bfloat16), by_time, preferred_e...  8.08 us
    dot_general x1, matrix products, body(): jnp.einsum('tj,ctp->cjp', lowpass[:, :local_j], by_component, preferred_e...  4.05 us
    ppermute x1, starting transfers between devices, body(): lax.ppermute(jnp.sum(moment[:, None, :] * tail, axis=0), 'handler', [(i,...  2.49 us
    transpose x1, local copies, waits for them, and re-layouts, convolve(): padded.reshape(v_local, k, n_rows, SHIFTS).transpose(0, 2, 3, 1)  2.28 us
  transfers between devices with their start and end apart: 2, of which 1 were waited for; matrix products, arithmetic and copies ran while one was open for 10% of the time, Pallas kernels for 0%

profile of v12, /device:TPU:0, one launch (start us, length us, event | category | flops | bytes accessed | tf_op | source)
XLA Modules:
  0.0 94.8 jit_solution(15627050571941403933)
XLA Ops:
  6.5 0.0 all-gather.2.cloned.1.call-start
  6.5 0.7 convert_element_type.15
  7.2 1.1 %select_reduce_fusion = bf16[256,72]{0,1:T(8,128)(2,1)S(1)} fusion(f32[32]{0:T(128)S(1)} %convert_element_type.15, s32[72]{0:T(128)S(1)} %iota_multiply_fusion), kind=kLoop, calls=%fused_computation.4 | loop fusion | flops 2340864 | bytes 37280 | tf_op jit(solution)/shard_map/reduce_sum | solution.py:19
  8.3 1.4 %fusion.3 = f32[8,2048]{1,0:T(8,128)S(1)} fusion(bf16[6,256,2048]{2,1,0:T(8,128)(2,1)} %bitcast.16, f32[6,2048]{1,0:T(8,128)} %param.9, bf16[256,72]{0,1:T(8,128)(2,1)S(1)} %select_reduce_fusion), kind=kOutput, calls=%fused_computation.8 | convolution fusion | flops 6471680 | bytes 919552 | tf_op jit(solution)/shard_map/tj,ctp->cjp/dot_general | solution.py:89
  9.8 0.0 copy-start.1
  9.8 0.0 copy-start
  9.8 2.5 %collective-permute-start = (f32[8,2048]{1,0:T(8,128)S(1)}, f32[8,2048]{1,0:T(8,128)S(1)}, u32[]{:S(2)}, u32[]{:S(2)}) collective-permute-start(f32[8,2048]{1,0:T(8,128)S(1)} %fusion.3), channel_id=1, source_target_pairs={{0,1},{1,2},{2,3},{3,4},{4,5},{5,6},{6,7},{7,8},{8,9},{9,10},{10,1... | collective-permute-start | bytes 196616 | tf_op jit(solution)/shard_map/ppermute | solution.py:91
  12.3 4.0 %multiply_reduce_fusion = f32[64,2048]{1,0:T(8,128)S(1)} fusion(f32[6,2048]{1,0:T(8,128)} %param.9, bf16[256,72]{0,1:T(8,128)(2,1)S(1)} %select_reduce_fusion, bf16[256,6,2048]{2,0,1:T(8,128)(2,1)} %param.7), kind=kOutput, calls=%fused_computation.3 | convolution fusion | flops 404094976 | bytes 6897664 | tf_op jit(solution)/shard_map/tj,ctp->cjp/dot_general | solution.py:93
  16.3 0.0 collective-permute-done
  16.4 0.7 convert_element_type.17
  17.1 0.0 all-gather.2.cloned.1.call-update
  17.1 0.0 copy-done.1
  17.1 0.1 min.12
  17.2 0.0 copy-done
  17.2 1.5 %copy.13 = bf16[32,32,200]{1,0,2:T(8,128)(2,1)S(1)} copy(bf16[32,32,200]{2,1,0:T(8,128)(2,1)S(1)} %copy-done) | data formatting | bytes 819200
  18.7 0.3 pad.6.clone
  19.0 2.3 %copy.11 = bf16[32,56,4,32]{1,3,2,0:T(8,128)(2,1)S(1)} copy(bf16[32,56,4,32]{3,0,2,1:T(8,128)(2,1)S(1)} %bitcast.15) | data formatting | bytes 917504 | tf_op jit(solution)/shard_map/transpose | solution.py:65
  21.3 1.1 %copy.12.weight_ref = bf16[32,56,128]{2,1,0:T(8,128)(2,1)} copy(bf16[32,56,128]{1,2,0:T(8,128)(2,1)S(1)} %bitcast.17) | data formatting | bytes 917504 | tf_op jit(solution)/shard_map/reshape | solution.py:65
  22.4 48.0 %all-gather.2.cloned.1.call-done = bf16[1024,2048]{1,0:T(8,128)(2,1)} async-done(((bf16[64,2048]{1,0:T(8,128)(2,1)}), bf16[1024,2048]{1,0:T(8,128)(2,1)}) %all-gather.2.cloned.1.call-update) | async-done | bytes 4194320 | tf_op jit(solution)/shard_map/all_gather | solution.py:96
  70.4 8.1 %fusion.2 = bf16[1024,1024]{1,0:T(8,128)(2,1)} fusion(bf16[1024,2048]{1,0:T(8,128)(2,1)} %all-gather.2.cloned.1.call-done, s32[1024]{0:T(1024)S(1)} %min.12), kind=kOutput, calls=%fused_computation.7 | convolution fusion | flops 4298113024 | bytes 6295552 | tf_op jit(solution)/shard_map/np,jp->nj/dot_general | solution.py:101
  78.5 9.4 %shard_map.55 = f32[32,1024]{1,0:T(8,128)} custom-call(bf16[32,56,128]{2,1,0:T(8,128)(2,1)} %copy.12.weight_ref, bf16[32,32,1024]{2,1,0:T(8,128)(2,1)} %bitcast.18), custom_call_target="tpu_custom_call" | custom-call | tf_op jit(solution)/shard_map/pallas_call | solution.py:67
  (3 shorter events, 0.0 us)
Async XLA Ops:
  6.5 63.9 %all-gather.2.cloned.1.call-start = ((), (), s32[]{:S(2)}) async-start(), calls=%async_computation | async-start | bytes 4456448 | tf_op jit(solution)/shard_map/all_gather | solution.py:96
  9.8 7.4 %copy-start.1 = (s32[32,32]{1,0:T(8,128)S(1)}, s32[32,32]{1,0:T(8,128)}, u32[]{:S(2)}) copy-start(s32[32,32]{1,0:T(8,128)} %param.10) | copy-start | bytes 12292
  9.8 7.4 %copy-start = (bf16[32,32,200]{2,1,0:T(8,128)(2,1)S(1)}, bf16[32,32,200]{2,1,0:T(8,128)(2,1)}, u32[]{:S(2)}) copy-start(bf16[32,32,200]{2,1,0:T(8,128)(2,1)} %param.11) | copy-start | bytes 1228804
  9.8 6.6 %collective-permute-start = (f32[8,2048]{1,0:T(8,128)S(1)}, f32[8,2048]{1,0:T(8,128)S(1)}, u32[]{:S(2)}, u32[]{:S(2)}) collective-permute-start(f32[8,2048]{1,0:T(8,128)S(1)} %fusion.3), channel_id=1, source_target_pairs={{0,1},{1,2},{2,3},{3,4},{4,5},{5,6},{6,7},{7,8},{8,9},{9,10},{10,1... | collective-permute-start | bytes 196616 | tf_op jit(solution)/shard_map/ppermute | solution.py:91
Sparse Core Ops, SparseCore 0:
  17.2 53.1 all-gather.1

commit v13 on v12

--- a/solution.py
+++ b/solution.py
@@ -19,7 +19,7 @@
     return jnp.sum(picked, axis=2).astype(jnp.bfloat16)
 
 
-SHIFTS = 4
+SHIFTS = 2
 
 
 def conv_kernel(weight_ref, picked_ref, out_ref, shifted_ref):

time: 95 us -> 96 us (1.011)
  Pallas kernels: 9.42 us -> 10.5 us
    pallas_call x1, Pallas kernels: 9.42 us -> 10.5 us  [convolve(): pl.pallas_call(conv_kernel, grid=(v_local // vb,), in_specs=[pl.BlockSpec...]
  transfers between devices with their start and end apart: 2 -> 2, of which waited for: 1 -> 1; matrix products, arithmetic and copies ran while one was open for 10% -> 9% of each run, Pallas kernels for 0% -> 0%
where the time goes in v13:
time: 96 us; the launch traced here: 95.8 us
  waiting for transfers between devices  48.5 us (51%)
  matrix products  13.6 us (14%)
  between operations  13.5 us (14%)
  Pallas kernels  10.5 us (11%)
  local copies, waits for them, and re-layouts  4.82 us (5%)
  other arithmetic  2.52 us (3%)
  starting transfers between devices  2.49 us (3%)
    all_gather x1, waiting for transfers between devices, body(): lax.all_gather(own.astype(jnp.bfloat16), 'handler', axis=0, tiled=True)  48.4 us
    pallas_call x1, Pallas kernels, convolve(): pl.pallas_call(conv_kernel, grid=(v_local // vb,), in_specs=[pl.BlockSpec...  10.5 us
    dot_general x1, matrix products, body(): jnp.einsum('np,jp->nj', choose.astype(jnp.bfloat16), by_time, preferred_e...  8.08 us
    dot_general x1, matrix products, body(): jnp.einsum('tj,ctp->cjp', lowpass[:, :local_j], by_component, preferred_e...  4.05 us
    ppermute x1, starting transfers between devices, body(): lax.ppermute(jnp.sum(moment[:, None, :] * tail, axis=0), 'handler', [(i,...  2.49 us
  transfers between devices with their start and end apart: 2, of which 1 were waited for; matrix products, arithmetic and copies ran while one was open for 9% of the time, Pallas kernels for 0%

profile of v13, /device:TPU:0, one launch (start us, length us, event | category | flops | bytes accessed | tf_op | source)
XLA Modules:
  0.0 95.8 jit_solution(14955178224260805920)
XLA Ops:
  6.5 0.0 all-gather.2.cloned.1.call-start
  6.5 0.7 convert_element_type.15
  7.2 1.1 %select_reduce_fusion = bf16[256,72]{0,1:T(8,128)(2,1)S(1)} fusion(f32[32]{0:T(128)S(1)} %convert_element_type.15, s32[72]{0:T(128)S(1)} %iota_multiply_fusion), kind=kLoop, calls=%fused_computation.4 | loop fusion | flops 2340864 | bytes 37280 | tf_op jit(solution)/shard_map/reduce_sum | solution.py:19
  8.3 1.4 %fusion.3 = f32[8,2048]{1,0:T(8,128)S(1)} fusion(bf16[6,256,2048]{2,1,0:T(8,128)(2,1)} %bitcast.16, f32[6,2048]{1,0:T(8,128)} %param.9, bf16[256,72]{0,1:T(8,128)(2,1)S(1)} %select_reduce_fusion), kind=kOutput, calls=%fused_computation.8 | convolution fusion | flops 6471680 | bytes 919552 | tf_op jit(solution)/shard_map/tj,ctp->cjp/dot_general | solution.py:89
  9.8 0.0 copy-start.1
  9.8 0.0 copy-start
  9.8 2.5 %collective-permute-start = (f32[8,2048]{1,0:T(8,128)S(1)}, f32[8,2048]{1,0:T(8,128)S(1)}, u32[]{:S(2)}, u32[]{:S(2)}) collective-permute-start(f32[8,2048]{1,0:T(8,128)S(1)} %fusion.3), channel_id=1, source_target_pairs={{0,1},{1,2},{2,3},{3,4},{4,5},{5,6},{6,7},{7,8},{8,9},{9,10},{10,1... | collective-permute-start | bytes 196616 | tf_op jit(solution)/shard_map/ppermute | solution.py:91
  12.3 4.0 %multiply_reduce_fusion = f32[64,2048]{1,0:T(8,128)S(1)} fusion(f32[6,2048]{1,0:T(8,128)} %param.9, bf16[256,72]{0,1:T(8,128)(2,1)S(1)} %select_reduce_fusion, bf16[256,6,2048]{2,0,1:T(8,128)(2,1)} %param.7), kind=kOutput, calls=%fused_computation.3 | convolution fusion | flops 404094976 | bytes 6897664 | tf_op jit(solution)/shard_map/tj,ctp->cjp/dot_general | solution.py:93
  16.3 0.0 collective-permute-done
  16.4 0.7 convert_element_type.17
  17.1 0.0 all-gather.2.cloned.1.call-update
  17.1 0.0 copy-done.1
  17.1 0.1 min.12
  17.2 0.0 copy-done
  17.2 1.5 %copy.13 = bf16[32,32,200]{1,0,2:T(8,128)(2,1)S(1)} copy(bf16[32,32,200]{2,1,0:T(8,128)(2,1)S(1)} %copy-done) | data formatting | bytes 819200
  18.7 0.3 pad.6.clone
  19.0 1.7 %copy.11 = bf16[32,104,2,32]{1,3,2,0:T(8,128)(2,1)S(1)} copy(bf16[32,104,2,32]{3,0,2,1:T(8,128)(2,1)S(1)} %bitcast.15) | data formatting | bytes 851968 | tf_op jit(solution)/shard_map/transpose | solution.py:65
  20.8 1.2 %copy.12.weight_ref = bf16[32,104,64]{2,1,0:T(8,128)(2,1)} copy(bf16[32,104,64]{1,2,0:T(8,128)(2,1)S(1)} %bitcast.17) | data formatting | bytes 851968 | tf_op jit(solution)/shard_map/reshape | solution.py:65
  22.0 48.4 %all-gather.2.cloned.1.call-done = bf16[1024,2048]{1,0:T(8,128)(2,1)} async-done(((bf16[64,2048]{1,0:T(8,128)(2,1)}), bf16[1024,2048]{1,0:T(8,128)(2,1)}) %all-gather.2.cloned.1.call-update) | async-done | bytes 4194320 | tf_op jit(solution)/shard_map/all_gather | solution.py:96
  70.4 8.1 %fusion.2 = bf16[1024,1024]{1,0:T(8,128)(2,1)} fusion(bf16[1024,2048]{1,0:T(8,128)(2,1)} %all-gather.2.cloned.1.call-done, s32[1024]{0:T(1024)S(1)} %min.12), kind=kOutput, calls=%fused_computation.7 | convolution fusion | flops 4298113024 | bytes 6295552 | tf_op jit(solution)/shard_map/np,jp->nj/dot_general | solution.py:101
  78.5 10.5 %shard_map.55 = f32[32,1024]{1,0:T(8,128)} custom-call(bf16[32,104,64]{2,1,0:T(8,128)(2,1)} %copy.12.weight_ref, bf16[32,32,1024]{2,1,0:T(8,128)(2,1)} %bitcast.18), custom_call_target="tpu_custom_call" | custom-call | tf_op jit(solution)/shard_map/pallas_call | solution.py:67
  (3 shorter events, 0.0 us)
Async XLA Ops:
  6.5 63.9 %all-gather.2.cloned.1.call-start = ((), (), s32[]{:S(2)}) async-start(), calls=%async_computation | async-start | bytes 4456448 | tf_op jit(solution)/shard_map/all_gather | solution.py:96
  9.8 7.4 %copy-start.1 = (s32[32,32]{1,0:T(8,128)S(1)}, s32[32,32]{1,0:T(8,128)}, u32[]{:S(2)}) copy-start(s32[32,32]{1,0:T(8,128)} %param.10) | copy-start | bytes 12292
  9.8 7.4 %copy-start = (bf16[32,32,200]{2,1,0:T(8,128)(2,1)S(1)}, bf16[32,32,200]{2,1,0:T(8,128)(2,1)}, u32[]{:S(2)}) copy-start(bf16[32,32,200]{2,1,0:T(8,128)(2,1)} %param.11) | copy-start | bytes 1228804
  9.8 6.6 %collective-permute-start = (f32[8,2048]{1,0:T(8,128)S(1)}, f32[8,2048]{1,0:T(8,128)S(1)}, u32[]{:S(2)}, u32[]{:S(2)}) collective-permute-start(f32[8,2048]{1,0:T(8,128)S(1)} %fusion.3), channel_id=1, source_target_pairs={{0,1},{1,2},{2,3},{3,4},{4,5},{5,6},{6,7},{7,8},{8,9},{9,10},{10,1... | collective-permute-start | bytes 196616 | tf_op jit(solution)/shard_map/ppermute | solution.py:91
Sparse Core Ops, SparseCore 0:
  17.2 53.1 all-gather.1

commit v14 on v12

--- a/solution.py
+++ b/solution.py
@@ -6,7 +6,7 @@
 from jax.sharding import PartitionSpec as P
 
 DEC = 4
-V_BLOCK = 8
+V_BLOCK = 16
 
 
 def band_matrix(taps, rows, cols):

time: 95 us -> 96.8 us (1.019)
  Pallas kernels: 9.42 us -> 11.2 us
    pallas_call x1, Pallas kernels: 9.42 us -> 11.2 us  [convolve(): pl.pallas_call(conv_kernel, grid=(v_local // vb,), in_specs=[pl.BlockSpec...]
where the time goes in v14:
time: 96.8 us; the launch traced here: 96.6 us
  waiting for transfers between devices  48 us (50%)
  matrix products  13.6 us (14%)
  between operations  13.5 us (14%)
  Pallas kernels  11.2 us (12%)
  local copies, waits for them, and re-layouts  5.27 us (5%)
  other arithmetic  2.52 us (3%)
  starting transfers between devices  2.49 us (3%)
    all_gather x1, waiting for transfers between devices, body(): lax.all_gather(own.astype(jnp.bfloat16), 'handler', axis=0, tiled=True)  48 us
    pallas_call x1, Pallas kernels, convolve(): pl.pallas_call(conv_kernel, grid=(v_local // vb,), in_specs=[pl.BlockSpec...  11.2 us
    dot_general x1, matrix products, body(): jnp.einsum('np,jp->nj', choose.astype(jnp.bfloat16), by_time, preferred_e...  8.08 us
    dot_general x1, matrix products, body(): jnp.einsum('tj,ctp->cjp', lowpass[:, :local_j], by_component, preferred_e...  4.05 us
    ppermute x1, starting transfers between devices, body(): lax.ppermute(jnp.sum(moment[:, None, :] * tail, axis=0), 'handler', [(i,...  2.49 us
    transpose x1, local copies, waits for them, and re-layouts, convolve(): padded.reshape(v_local, k, n_rows, SHIFTS).transpose(0, 2, 3, 1)  2.28 us
  transfers between devices with their start and end apart: 2, of which 1 were waited for; matrix products, arithmetic and copies ran while one was open for 10% of the time, Pallas kernels for 0%

profile of v14, /device:TPU:0, one launch (start us, length us, event | category | flops | bytes accessed | tf_op | source)
XLA Modules:
  0.0 96.6 jit_solution(13172275331246748155)
XLA Ops:
  6.5 0.0 all-gather.2.cloned.1.call-start
  6.5 0.7 convert_element_type.15
  7.2 1.1 %select_reduce_fusion = bf16[256,72]{0,1:T(8,128)(2,1)S(1)} fusion(f32[32]{0:T(128)S(1)} %convert_element_type.15, s32[72]{0:T(128)S(1)} %iota_multiply_fusion), kind=kLoop, calls=%fused_computation.4 | loop fusion | flops 2340864 | bytes 37280 | tf_op jit(solution)/shard_map/reduce_sum | solution.py:19
  8.3 1.4 %fusion.3 = f32[8,2048]{1,0:T(8,128)S(1)} fusion(bf16[6,256,2048]{2,1,0:T(8,128)(2,1)} %bitcast.16, f32[6,2048]{1,0:T(8,128)} %param.9, bf16[256,72]{0,1:T(8,128)(2,1)S(1)} %select_reduce_fusion), kind=kOutput, calls=%fused_computation.8 | convolution fusion | flops 6471680 | bytes 919552 | tf_op jit(solution)/shard_map/tj,ctp->cjp/dot_general | solution.py:89
  9.8 0.0 copy-start.1
  9.8 0.0 copy-start
  9.8 2.5 %collective-permute-start = (f32[8,2048]{1,0:T(8,128)S(1)}, f32[8,2048]{1,0:T(8,128)S(1)}, u32[]{:S(2)}, u32[]{:S(2)}) collective-permute-start(f32[8,2048]{1,0:T(8,128)S(1)} %fusion.3), channel_id=1, source_target_pairs={{0,1},{1,2},{2,3},{3,4},{4,5},{5,6},{6,7},{7,8},{8,9},{9,10},{10,1... | collective-permute-start | bytes 196616 | tf_op jit(solution)/shard_map/ppermute | solution.py:91
  12.3 4.0 %multiply_reduce_fusion = f32[64,2048]{1,0:T(8,128)S(1)} fusion(f32[6,2048]{1,0:T(8,128)} %param.9, bf16[256,72]{0,1:T(8,128)(2,1)S(1)} %select_reduce_fusion, bf16[256,6,2048]{2,0,1:T(8,128)(2,1)} %param.7), kind=kOutput, calls=%fused_computation.3 | convolution fusion | flops 404094976 | bytes 6897664 | tf_op jit(solution)/shard_map/tj,ctp->cjp/dot_general | solution.py:93
  16.3 0.0 collective-permute-done
  16.4 0.7 convert_element_type.17
  17.1 0.0 all-gather.2.cloned.1.call-update
  17.1 0.0 copy-done.1
  17.1 0.1 min.12
  17.2 0.0 copy-done
  17.2 1.5 %copy.13 = bf16[32,32,200]{1,0,2:T(8,128)(2,1)S(1)} copy(bf16[32,32,200]{2,1,0:T(8,128)(2,1)S(1)} %copy-done) | data formatting | bytes 819200
  18.7 0.3 pad.6.clone
  19.0 2.3 %copy.11 = bf16[32,56,4,32]{1,3,2,0:T(8,128)(2,1)S(1)} copy(bf16[32,56,4,32]{3,0,2,1:T(8,128)(2,1)S(1)} %bitcast.15) | data formatting | bytes 917504 | tf_op jit(solution)/shard_map/transpose | solution.py:65
  21.3 1.1 %copy.12.weight_ref = bf16[32,56,128]{2,1,0:T(8,128)(2,1)} copy(bf16[32,56,128]{1,2,0:T(8,128)(2,1)S(1)} %bitcast.17) | data formatting | bytes 917504 | tf_op jit(solution)/shard_map/reshape | solution.py:65
  22.4 48.0 %all-gather.2.cloned.1.call-done = bf16[1024,2048]{1,0:T(8,128)(2,1)} async-done(((bf16[64,2048]{1,0:T(8,128)(2,1)}), bf16[1024,2048]{1,0:T(8,128)(2,1)}) %all-gather.2.cloned.1.call-update) | async-done | bytes 4194320 | tf_op jit(solution)/shard_map/all_gather | solution.py:96
  70.4 8.1 %fusion.2 = bf16[1024,1024]{1,0:T(8,128)(2,1)} fusion(bf16[1024,2048]{1,0:T(8,128)(2,1)} %all-gather.2.cloned.1.call-done, s32[1024]{0:T(1024)S(1)} %min.12), kind=kOutput, calls=%fused_computation.7 | convolution fusion | flops 4298113024 | bytes 6295552 | tf_op jit(solution)/shard_map/np,jp->nj/dot_general | solution.py:101
  78.5 11.2 %shard_map.55 = f32[32,1024]{1,0:T(8,128)} custom-call(bf16[32,56,128]{2,1,0:T(8,128)(2,1)} %copy.12.weight_ref, bf16[32,32,1024]{2,1,0:T(8,128)(2,1)} %bitcast.18), custom_call_target="tpu_custom_call" | custom-call | tf_op jit(solution)/shard_map/pallas_call | solution.py:67
  (3 shorter events, 0.0 us)
Async XLA Ops:
  6.5 63.9 %all-gather.2.cloned.1.call-start = ((), (), s32[]{:S(2)}) async-start(), calls=%async_computation | async-start | bytes 4456448 | tf_op jit(solution)/shard_map/all_gather | solution.py:96
  9.8 7.4 %copy-start.1 = (s32[32,32]{1,0:T(8,128)S(1)}, s32[32,32]{1,0:T(8,128)}, u32[]{:S(2)}) copy-start(s32[32,32]{1,0:T(8,128)} %param.10) | copy-start | bytes 12292
  9.8 7.4 %copy-start = (bf16[32,32,200]{2,1,0:T(8,128)(2,1)S(1)}, bf16[32,32,200]{2,1,0:T(8,128)(2,1)}, u32[]{:S(2)}) copy-start(bf16[32,32,200]{2,1,0:T(8,128)(2,1)} %param.11) | copy-start | bytes 1228804
  9.8 6.6 %collective-permute-start = (f32[8,2048]{1,0:T(8,128)S(1)}, f32[8,2048]{1,0:T(8,128)S(1)}, u32[]{:S(2)}, u32[]{:S(2)}) collective-permute-start(f32[8,2048]{1,0:T(8,128)S(1)} %fusion.3), channel_id=1, source_target_pairs={{0,1},{1,2},{2,3},{3,4},{4,5},{5,6},{6,7},{7,8},{8,9},{9,10},{10,1... | collective-permute-start | bytes 196616 | tf_op jit(solution)/shard_map/ppermute | solution.py:91
Sparse Core Ops, SparseCore 0:
  17.2 53.1 all-gather.1

commit v15 on v12

--- a/solution.py
+++ b/solution.py
@@ -15,8 +15,8 @@
     col_ids = lax.broadcasted_iota(jnp.int32, (rows, cols, n_taps), 1)
     tap_ids = lax.broadcasted_iota(jnp.int32, (rows, cols, n_taps), 2)
     hit = DEC * col_ids - row_ids == tap_ids
-    picked = jnp.where(hit, taps.astype(jnp.float32)[None, None, :], 0.0)
-    return jnp.sum(picked, axis=2).astype(jnp.bfloat16)
+    picked = jnp.where(hit, taps[None, None, :], jnp.zeros((), taps.dtype))
+    return jnp.sum(picked, axis=2, dtype=jnp.bfloat16)
 
 
 SHIFTS = 4
@@ -92,8 +92,8 @@
                            [(i, i + 1) for i in range(n_handler - 1)])
     filtered = jnp.einsum("tj,ctp->cjp", lowpass[:, :local_j], by_component, preferred_element_type=jnp.float32)
     own = jnp.sum(moment[:, None, :] * filtered, axis=0)
-    own = own.at[:halo].add(carried)
-    by_time = lax.all_gather(own.astype(jnp.bfloat16), "handler", axis=0, tiled=True)
+    green = (own + jnp.pad(carried, ((0, local_j - halo), (0, 0)))).astype(jnp.bfloat16)
+    by_time = lax.all_gather(green, "handler", axis=0, tiled=True)
     length = by_time.shape[1]
     v_local, k = index.shape
     flat_index = jnp.clip(index.reshape(-1), 0, length - 1)

time: 95 us -> 95 us (level)
  no operation moved by 1% of the time
where the time goes in v15:
time: 95 us; the launch traced here: 94.7 us
  waiting for transfers between devices  48 us (51%)
  matrix products  13.6 us (14%)
  between operations  13.5 us (14%)
  Pallas kernels  9.42 us (10%)
  local copies, waits for them, and re-layouts  5.27 us (6%)
  other arithmetic  2.51 us (3%)
  starting transfers between devices  2.49 us (3%)
    all_gather x1, waiting for transfers between devices, body(): by_time = lax.all_gather(green, 'handler', axis=0, tiled=True)  48 us
    pallas_call x1, Pallas kernels, convolve(): pl.pallas_call(conv_kernel, grid=(v_local // vb,), in_specs=[pl.BlockSpec...  9.42 us
    dot_general x1, matrix products, body(): jnp.einsum('np,jp->nj', choose.astype(jnp.bfloat16), by_time, preferred_e...  8.08 us
    dot_general x1, matrix products, body(): jnp.einsum('tj,ctp->cjp', lowpass[:, :local_j], by_component, preferred_e...  4.05 us
    ppermute x1, starting transfers between devices, body(): lax.ppermute(jnp.sum(moment[:, None, :] * tail, axis=0), 'handler', [(i,...  2.49 us
    transpose x1, local copies, waits for them, and re-layouts, convolve(): padded.reshape(v_local, k, n_rows, SHIFTS).transpose(0, 2, 3, 1)  2.28 us
  transfers between devices with their start and end apart: 2, of which 1 were waited for; matrix products, arithmetic and copies ran while one was open for 10% of the time, Pallas kernels for 0%

profile of v15, /device:TPU:0, one launch (start us, length us, event | category | flops | bytes accessed | tf_op | source)
XLA Modules:
  0.0 94.7 jit_solution(5459773879669447815)
XLA Ops:
  6.5 0.0 all-gather.2.cloned.1.call-start
  6.5 1.8 %fusion.4 = bf16[256,72]{0,1:T(8,128)(2,1)S(1)} fusion(s32[72]{0:T(128)S(1)} %iota_multiply_fusion, bf16[32]{0:T(256)(128)(2,1)} %param.6), kind=kLoop, calls=%fused_computation.8 | loop fusion | flops 2340864 | bytes 37216 | tf_op jit(solution)/shard_map/reduce_sum | solution.py:19
  8.3 1.4 %fusion.5 = f32[8,2048]{1,0:T(8,128)S(1)} fusion(bf16[6,256,2048]{2,1,0:T(8,128)(2,1)} %bitcast.16, f32[6,2048]{1,0:T(8,128)} %param.7, bf16[256,72]{0,1:T(8,128)(2,1)S(1)} %fusion.4), kind=kOutput, calls=%fused_computation.9 | convolution fusion | flops 6471680 | bytes 919552 | tf_op jit(solution)/shard_map/tj,ctp->cjp/dot_general | solution.py:89
  9.8 0.0 copy-start.1
  9.8 0.0 copy-start
  9.8 2.5 %collective-permute-start = (f32[8,2048]{1,0:T(8,128)S(1)}, f32[8,2048]{1,0:T(8,128)S(1)}, u32[]{:S(2)}, u32[]{:S(2)}) collective-permute-start(f32[8,2048]{1,0:T(8,128)S(1)} %fusion.5), channel_id=1, source_target_pairs={{0,1},{1,2},{2,3},{3,4},{4,5},{5,6},{6,7},{7,8},{8,9},{9,10},{10,1... | collective-permute-start | bytes 196616 | tf_op jit(solution)/shard_map/ppermute | solution.py:91
  12.3 4.0 %multiply_reduce_fusion = f32[64,2048]{1,0:T(8,128)S(1)} fusion(f32[6,2048]{1,0:T(8,128)} %param.7, bf16[256,72]{0,1:T(8,128)(2,1)S(1)} %fusion.4, bf16[256,6,2048]{2,0,1:T(8,128)(2,1)} %param.5), kind=kOutput, calls=%fused_computation.3 | convolution fusion | flops 404094976 | bytes 6897664 | tf_op jit(solution)/shard_map/tj,ctp->cjp/dot_general | solution.py:93
  16.3 0.0 collective-permute-done
  16.4 0.7 add_convert_fusion
  17.1 0.0 all-gather.2.cloned.1.call-update
  17.1 0.0 copy-done.1
  17.1 0.1 min.12
  17.2 0.0 copy-done
  17.2 1.5 %copy.13 = bf16[32,32,200]{1,0,2:T(8,128)(2,1)S(1)} copy(bf16[32,32,200]{2,1,0:T(8,128)(2,1)S(1)} %copy-done) | data formatting | bytes 819200
  18.7 0.3 pad.8.clone
  19.0 2.3 %copy.11 = bf16[32,56,4,32]{1,3,2,0:T(8,128)(2,1)S(1)} copy(bf16[32,56,4,32]{3,0,2,1:T(8,128)(2,1)S(1)} %bitcast.15) | data formatting | bytes 917504 | tf_op jit(solution)/shard_map/transpose | solution.py:65
  21.3 1.1 %copy.12.weight_ref = bf16[32,56,128]{2,1,0:T(8,128)(2,1)} copy(bf16[32,56,128]{1,2,0:T(8,128)(2,1)S(1)} %bitcast.17) | data formatting | bytes 917504 | tf_op jit(solution)/shard_map/reshape | solution.py:65
  22.4 48.0 %all-gather.2.cloned.1.call-done = bf16[1024,2048]{1,0:T(8,128)(2,1)} async-done(((bf16[64,2048]{1,0:T(8,128)(2,1)}), bf16[1024,2048]{1,0:T(8,128)(2,1)}) %all-gather.2.cloned.1.call-update) | async-done | bytes 4194320 | tf_op jit(solution)/shard_map/all_gather | solution.py:96
  70.4 8.1 %fusion.3 = bf16[1024,1024]{1,0:T(8,128)(2,1)} fusion(bf16[1024,2048]{1,0:T(8,128)(2,1)} %all-gather.2.cloned.1.call-done, s32[1024]{0:T(1024)S(1)} %min.12), kind=kOutput, calls=%fused_computation.7 | convolution fusion | flops 4298113024 | bytes 6295552 | tf_op jit(solution)/shard_map/np,jp->nj/dot_general | solution.py:101
  78.5 9.4 %shard_map.55 = f32[32,1024]{1,0:T(8,128)} custom-call(bf16[32,56,128]{2,1,0:T(8,128)(2,1)} %copy.12.weight_ref, bf16[32,32,1024]{2,1,0:T(8,128)(2,1)} %bitcast.18), custom_call_target="tpu_custom_call" | custom-call | tf_op jit(solution)/shard_map/pallas_call | solution.py:67
  (2 shorter events, 0.0 us)
Async XLA Ops:
  6.5 63.9 %all-gather.2.cloned.1.call-start = ((), (), s32[]{:S(2)}) async-start(), calls=%async_computation | async-start | bytes 4456448 | tf_op jit(solution)/shard_map/all_gather | solution.py:96
  9.8 7.3 %copy-start.1 = (s32[32,32]{1,0:T(8,128)S(1)}, s32[32,32]{1,0:T(8,128)}, u32[]{:S(2)}) copy-start(s32[32,32]{1,0:T(8,128)} %param.8) | copy-start | bytes 12292
  9.8 7.4 %copy-start = (bf16[32,32,200]{2,1,0:T(8,128)(2,1)S(1)}, bf16[32,32,200]{2,1,0:T(8,128)(2,1)}, u32[]{:S(2)}) copy-start(bf16[32,32,200]{2,1,0:T(8,128)(2,1)} %param.9) | copy-start | bytes 1228804
  9.8 6.6 %collective-permute-start = (f32[8,2048]{1,0:T(8,128)S(1)}, f32[8,2048]{1,0:T(8,128)S(1)}, u32[]{:S(2)}, u32[]{:S(2)}) collective-permute-start(f32[8,2048]{1,0:T(8,128)S(1)} %fusion.5), channel_id=1, source_target_pairs={{0,1},{1,2},{2,3},{3,4},{4,5},{5,6},{6,7},{7,8},{8,9},{9,10},{10,1... | collective-permute-start | bytes 196616 | tf_op jit(solution)/shard_map/ppermute | solution.py:91
Sparse Core Ops, SparseCore 0:
  17.2 53.1 all-gather.1

commit v16 on v15

--- a/solution.py
+++ b/solution.py
@@ -86,12 +86,10 @@
     halo = (n_taps - 1 + DEC - 1) // DEC
     lowpass = lax.optimization_barrier(band_matrix(taps, local_t, local_j + halo))
     by_component = jnp.transpose(sgt, (1, 0, 2))
-    tail = jnp.einsum("tj,ctp->cjp", lowpass[local_t - n_taps:, local_j:], by_component[:, local_t - n_taps:, :],
-                      preferred_element_type=jnp.float32)
-    carried = lax.ppermute(jnp.sum(moment[:, None, :] * tail, axis=0), "handler",
-                           [(i, i + 1) for i in range(n_handler - 1)])
-    filtered = jnp.einsum("tj,ctp->cjp", lowpass[:, :local_j], by_component, preferred_element_type=jnp.float32)
-    own = jnp.sum(moment[:, None, :] * filtered, axis=0)
+    filtered = jnp.einsum("tj,ctp->cjp", lowpass, by_component, preferred_element_type=jnp.float32)
+    partial = jnp.sum(moment[:, None, :] * filtered, axis=0)
+    carried = lax.ppermute(partial[local_j:], "handler", [(i, i + 1) for i in range(n_handler - 1)])
+    own = partial[:local_j]
     green = (own + jnp.pad(carried, ((0, local_j - halo), (0, 0)))).astype(jnp.bfloat16)
     by_time = lax.all_gather(green, "handler", axis=0, tiled=True)
     length = by_time.shape[1]

time: 95 us -> 96.8 us (1.019)
  waiting for transfers between devices: 48 us -> 51.3 us
  matrix products: 13.6 us -> 12.2 us
    all_gather x1, waiting for transfers between devices: 48 us -> 50.4 us  [body(): by_time = lax.all_gather(green, 'handler', axis=0, tiled=True)]
    dot_general x2 -> x1, matrix products: 5.48 us -> 4.11 us  [body(): jnp.einsum('tj,ctp->cjp', lowpass, by_component, preferred_element_type=j...]
  transfers between devices with their start and end apart: 2 -> 2, of which waited for: 1 -> 2; matrix products, arithmetic and copies ran while one was open for 10% -> 5% of each run, Pallas kernels for 0% -> 0%
where the time goes in v16:
time: 96.8 us; the launch traced here: 96.6 us
  waiting for transfers between devices  51.3 us (53%)
  between operations  13.5 us (14%)
  matrix products  12.2 us (13%)
  Pallas kernels  9.42 us (10%)
  local copies, waits for them, and re-layouts  5.29 us (5%)
  other arithmetic  2.51 us (3%)
  starting transfers between devices  2.36 us (2%)
    all_gather x1, waiting for transfers between devices, body(): by_time = lax.all_gather(green, 'handler', axis=0, tiled=True)  50.4 us
    pallas_call x1, Pallas kernels, convolve(): pl.pallas_call(conv_kernel, grid=(v_local // vb,), in_specs=[pl.BlockSpec...  9.42 us
    dot_general x1, matrix products, body(): jnp.einsum('np,jp->nj', choose.astype(jnp.bfloat16), by_time, preferred_e...  8.07 us
    dot_general x1, matrix products, body(): jnp.einsum('tj,ctp->cjp', lowpass, by_component, preferred_element_type=j...  4.11 us
    ppermute x1, starting transfers between devices, body(): lax.ppermute(partial[local_j:], 'handler', [(i, i + 1) for i in range(n_h...  2.36 us
    transpose x1, local copies, waits for them, and re-layouts, convolve(): padded.reshape(v_local, k, n_rows, SHIFTS).transpose(0, 2, 3, 1)  2.28 us
  transfers between devices with their start and end apart: 2, of which 2 were waited for; matrix products, arithmetic and copies ran while one was open for 5% of the time, Pallas kernels for 0%

profile of v16, /device:TPU:0, one launch (start us, length us, event | category | flops | bytes accessed | tf_op | source)
XLA Modules:
  0.0 96.6 jit_solution(9387180342861594792)
XLA Ops:
  6.5 0.0 all-gather.2.cloned.1.call-start
  6.5 1.8 %fusion.8 = bf16[256,72]{0,1:T(8,128)(2,1)S(1)} fusion(s32[72]{0:T(128)S(1)} %iota_multiply_fusion, bf16[32]{0:T(256)(128)(2,1)} %param.6), kind=kLoop, calls=%fused_computation.9 | loop fusion | flops 2340864 | bytes 37216 | tf_op jit(solution)/shard_map/reduce_sum | solution.py:19
  8.3 0.0 copy-start.1
  8.3 0.0 copy-start
  8.4 4.1 %multiply_reduce_fusion = f32[72,2048]{1,0:T(8,128)S(1)} fusion(bf16[256,6,2048]{2,0,1:T(8,128)(2,1)} %param.5, f32[6,2048]{1,0:T(8,128)} %param.7, bf16[256,72]{0,1:T(8,128)(2,1)S(1)} %fusion.8), kind=kOutput, calls=%fused_computation.5 | convolution fusion | flops 454606848 | bytes 6967296 | tf_op jit(solution)/shard_map/tj,ctp->cjp/dot_general | solution.py:89
  12.5 2.4 %collective-permute-start = (f32[8,2048]{1,0:T(8,128)S(1)}, f32[8,2048]{1,0:T(8,128)S(1)}, u32[]{:S(2)}, u32[]{:S(2)}) collective-permute-start(f32[8,2048]{1,0:T(8,128)S(1)} %slice.9), channel_id=1, source_target_pairs={{0,1},{1,2},{2,3},{3,4},{4,5},{5,6},{6,7},{7,8},{8,9},{9,10},{10,1... | collective-permute-start | bytes 196616 | tf_op jit(solution)/shard_map/ppermute | solution.py:91
  14.8 0.9 collective-permute-done
  15.7 0.7 fusion.9
  16.5 0.0 all-gather.2.cloned.1.call-update
  16.5 0.0 copy-done.1
  16.5 0.1 min.12
  16.6 0.0 copy-done
  16.6 1.5 %copy.13 = bf16[32,32,200]{1,0,2:T(8,128)(2,1)S(1)} copy(bf16[32,32,200]{2,1,0:T(8,128)(2,1)S(1)} %copy-done) | data formatting | bytes 819200
  18.1 0.3 pad.8.clone
  18.4 2.3 %copy.11 = bf16[32,56,4,32]{1,3,2,0:T(8,128)(2,1)S(1)} copy(bf16[32,56,4,32]{3,0,2,1:T(8,128)(2,1)S(1)} %bitcast.14) | data formatting | bytes 917504 | tf_op jit(solution)/shard_map/transpose | solution.py:65
  20.7 1.1 %copy.12.weight_ref = bf16[32,56,128]{2,1,0:T(8,128)(2,1)} copy(bf16[32,56,128]{1,2,0:T(8,128)(2,1)S(1)} %bitcast.15) | data formatting | bytes 917504 | tf_op jit(solution)/shard_map/reshape | solution.py:65
  21.8 50.4 %all-gather.2.cloned.1.call-done = bf16[1024,2048]{1,0:T(8,128)(2,1)} async-done(((bf16[64,2048]{1,0:T(8,128)(2,1)}), bf16[1024,2048]{1,0:T(8,128)(2,1)}) %all-gather.2.cloned.1.call-update) | async-done | bytes 4194320 | tf_op jit(solution)/shard_map/all_gather | solution.py:94
  72.2 8.1 %fusion.7 = bf16[1024,1024]{1,0:T(8,128)(2,1)} fusion(bf16[1024,2048]{1,0:T(8,128)(2,1)} %all-gather.2.cloned.1.call-done, s32[1024]{0:T(1024)S(1)} %min.12), kind=kOutput, calls=%fused_computation.8 | convolution fusion | flops 4298113024 | bytes 6295552 | tf_op jit(solution)/shard_map/np,jp->nj/dot_general | solution.py:99
  80.3 9.4 %shard_map.55 = f32[32,1024]{1,0:T(8,128)} custom-call(bf16[32,56,128]{2,1,0:T(8,128)(2,1)} %copy.12.weight_ref, bf16[32,32,1024]{2,1,0:T(8,128)(2,1)} %bitcast.16), custom_call_target="tpu_custom_call" | custom-call | tf_op jit(solution)/shard_map/pallas_call | solution.py:67
  (3 shorter events, 0.0 us)
Async XLA Ops:
  6.5 65.7 %all-gather.2.cloned.1.call-start = ((), (), s32[]{:S(2)}) async-start(), calls=%async_computation | async-start | bytes 4456448 | tf_op jit(solution)/shard_map/all_gather | solution.py:94
  8.3 8.1 %copy-start.1 = (s32[32,32]{1,0:T(8,128)S(1)}, s32[32,32]{1,0:T(8,128)}, u32[]{:S(2)}) copy-start(s32[32,32]{1,0:T(8,128)} %param.8) | copy-start | bytes 12292
  8.3 8.2 %copy-start = (bf16[32,32,200]{2,1,0:T(8,128)(2,1)S(1)}, bf16[32,32,200]{2,1,0:T(8,128)(2,1)}, u32[]{:S(2)}) copy-start(bf16[32,32,200]{2,1,0:T(8,128)(2,1)} %param.9) | copy-start | bytes 1228804
  12.5 3.2 %collective-permute-start = (f32[8,2048]{1,0:T(8,128)S(1)}, f32[8,2048]{1,0:T(8,128)S(1)}, u32[]{:S(2)}, u32[]{:S(2)}) collective-permute-start(f32[8,2048]{1,0:T(8,128)S(1)} %slice.9), channel_id=1, source_target_pairs={{0,1},{1,2},{2,3},{3,4},{4,5},{5,6},{6,7},{7,8},{8,9},{9,10},{10,1... | collective-permute-start | bytes 196616 | tf_op jit(solution)/shard_map/ppermute | solution.py:91
Sparse Core Ops, SparseCore 0:
  16.6 55.5 all-gather.1

commit v17 on v12

--- a/solution.py
+++ b/solution.py
@@ -22,7 +22,7 @@
 SHIFTS = 4
 
 
-def conv_kernel(weight_ref, picked_ref, out_ref, shifted_ref):
+def conv_kernel(weight_ref, picked_ref, out_ref, shifted_ref, acc_ref):
     vb = out_ref.shape[0]
     n_rows = weight_ref.shape[1]
     k = picked_ref.shape[1]
@@ -51,9 +51,15 @@
             head = head + jnp.where(lag >= 8 * SHIFTS * q, moved[:, :edge], 0.0)
             if width > edge:
                 tail = tail + moved[:, edge:]
-        out_ref[v:v + 1, :edge] = jnp.sum(head, axis=0, keepdims=True)
-        if width > edge:
-            out_ref[v:v + 1, edge:] = jnp.sum(tail, axis=0, keepdims=True)
+        for t in range(edge // 128):
+            acc_ref[t, 8 * v:8 * v + 8, :] = head[:, 128 * t:128 * (t + 1)]
+        for t in range((width - edge) // 128):
+            acc_ref[edge // 128 + t, 8 * v:8 * v + 8, :] = tail[:, 128 * t:128 * (t + 1)]
+    for t in range(width // 128):
+        total = acc_ref[t, pl.ds(0, vb, stride=8), :]
+        for s in range(1, 8):
+            total = total + acc_ref[t, pl.ds(s, vb, stride=8), :]
+        out_ref[:, 128 * t:128 * (t + 1)] = total
 
 
 def convolve(picked, slip):
@@ -73,7 +79,7 @@
         ],
         out_specs=pl.BlockSpec((vb, width), lambda i: (i, 0)),
         out_shape=jax.ShapeDtypeStruct((v_local, width), jnp.float32),
-        scratch_shapes=[pltpu.VMEM((2, SHIFTS * k, width), jnp.bfloat16)],
+        scratch_shapes=[pltpu.VMEM((2, SHIFTS * k, width), jnp.bfloat16), pltpu.VMEM((width // 128, 8 * vb, 128), jnp.float32)],
     )(weight, picked)
 
 

time: 95 us -> 94.4 us (level)
  no operation moved by 1% of the time
where the time goes in v17:
time: 94.4 us; the launch traced here: 94.2 us
  waiting for transfers between devices  48 us (51%)
  matrix products  13.6 us (14%)
  between operations  13.5 us (14%)
  Pallas kernels  8.88 us (9%)
  local copies, waits for them, and re-layouts  5.27 us (6%)
  other arithmetic  2.52 us (3%)
  starting transfers between devices  2.49 us (3%)
    all_gather x1, waiting for transfers between devices, body(): lax.all_gather(own.astype(jnp.bfloat16), 'handler', axis=0, tiled=True)  48 us
    pallas_call x1, Pallas kernels, convolve(): pl.pallas_call(conv_kernel, grid=(v_local // vb,), in_specs=[pl.BlockSpec...  8.88 us
    dot_general x1, matrix products, body(): jnp.einsum('np,jp->nj', choose.astype(jnp.bfloat16), by_time, preferred_e...  8.08 us
    dot_general x1, matrix products, body(): jnp.einsum('tj,ctp->cjp', lowpass[:, :local_j], by_component, preferred_e...  4.05 us
    ppermute x1, starting transfers between devices, body(): lax.ppermute(jnp.sum(moment[:, None, :] * tail, axis=0), 'handler', [(i,...  2.49 us
    transpose x1, local copies, waits for them, and re-layouts, convolve(): padded.reshape(v_local, k, n_rows, SHIFTS).transpose(0, 2, 3, 1)  2.28 us
  transfers between devices with their start and end apart: 2, of which 1 were waited for; matrix products, arithmetic and copies ran while one was open for 10% of the time, Pallas kernels for 0%

profile of v17, /device:TPU:0, one launch (start us, length us, event | category | flops | bytes accessed | tf_op | source)
XLA Modules:
  0.0 94.2 jit_solution(473435350784753733)
XLA Ops:
  6.5 0.0 all-gather.2.cloned.1.call-start
  6.5 0.7 convert_element_type.15
  7.2 1.1 %select_reduce_fusion = bf16[256,72]{0,1:T(8,128)(2,1)S(1)} fusion(f32[32]{0:T(128)S(1)} %convert_element_type.15, s32[72]{0:T(128)S(1)} %iota_multiply_fusion), kind=kLoop, calls=%fused_computation.4 | loop fusion | flops 2340864 | bytes 37280 | tf_op jit(solution)/shard_map/reduce_sum | solution.py:19
  8.3 1.4 %fusion.3 = f32[8,2048]{1,0:T(8,128)S(1)} fusion(bf16[6,256,2048]{2,1,0:T(8,128)(2,1)} %bitcast.16, f32[6,2048]{1,0:T(8,128)} %param.9, bf16[256,72]{0,1:T(8,128)(2,1)S(1)} %select_reduce_fusion), kind=kOutput, calls=%fused_computation.8 | convolution fusion | flops 6471680 | bytes 919552 | tf_op jit(solution)/shard_map/tj,ctp->cjp/dot_general | solution.py:95
  9.8 0.0 copy-start.1
  9.8 0.0 copy-start
  9.8 2.5 %collective-permute-start = (f32[8,2048]{1,0:T(8,128)S(1)}, f32[8,2048]{1,0:T(8,128)S(1)}, u32[]{:S(2)}, u32[]{:S(2)}) collective-permute-start(f32[8,2048]{1,0:T(8,128)S(1)} %fusion.3), channel_id=1, source_target_pairs={{0,1},{1,2},{2,3},{3,4},{4,5},{5,6},{6,7},{7,8},{8,9},{9,10},{10,1... | collective-permute-start | bytes 196616 | tf_op jit(solution)/shard_map/ppermute | solution.py:97
  12.3 4.0 %multiply_reduce_fusion = f32[64,2048]{1,0:T(8,128)S(1)} fusion(f32[6,2048]{1,0:T(8,128)} %param.9, bf16[256,72]{0,1:T(8,128)(2,1)S(1)} %select_reduce_fusion, bf16[256,6,2048]{2,0,1:T(8,128)(2,1)} %param.7), kind=kOutput, calls=%fused_computation.3 | convolution fusion | flops 404094976 | bytes 6897664 | tf_op jit(solution)/shard_map/tj,ctp->cjp/dot_general | solution.py:99
  16.3 0.0 collective-permute-done
  16.4 0.7 convert_element_type.17
  17.1 0.0 all-gather.2.cloned.1.call-update
  17.1 0.0 copy-done.1
  17.1 0.1 min.12
  17.2 0.0 copy-done
  17.2 1.5 %copy.13 = bf16[32,32,200]{1,0,2:T(8,128)(2,1)S(1)} copy(bf16[32,32,200]{2,1,0:T(8,128)(2,1)S(1)} %copy-done) | data formatting | bytes 819200
  18.7 0.3 pad.6.clone
  19.0 2.3 %copy.11 = bf16[32,56,4,32]{1,3,2,0:T(8,128)(2,1)S(1)} copy(bf16[32,56,4,32]{3,0,2,1:T(8,128)(2,1)S(1)} %bitcast.15) | data formatting | bytes 917504 | tf_op jit(solution)/shard_map/transpose | solution.py:71
  21.3 1.1 %copy.12.weight_ref = bf16[32,56,128]{2,1,0:T(8,128)(2,1)} copy(bf16[32,56,128]{1,2,0:T(8,128)(2,1)S(1)} %bitcast.17) | data formatting | bytes 917504 | tf_op jit(solution)/shard_map/reshape | solution.py:71
  22.4 48.0 %all-gather.2.cloned.1.call-done = bf16[1024,2048]{1,0:T(8,128)(2,1)} async-done(((bf16[64,2048]{1,0:T(8,128)(2,1)}), bf16[1024,2048]{1,0:T(8,128)(2,1)}) %all-gather.2.cloned.1.call-update) | async-done | bytes 4194320 | tf_op jit(solution)/shard_map/all_gather | solution.py:102
  70.4 8.1 %fusion.2 = bf16[1024,1024]{1,0:T(8,128)(2,1)} fusion(bf16[1024,2048]{1,0:T(8,128)(2,1)} %all-gather.2.cloned.1.call-done, s32[1024]{0:T(1024)S(1)} %min.12), kind=kOutput, calls=%fused_computation.7 | convolution fusion | flops 4298113024 | bytes 6295552 | tf_op jit(solution)/shard_map/np,jp->nj/dot_general | solution.py:107
  78.5 8.9 %shard_map.55 = f32[32,1024]{1,0:T(8,128)} custom-call(bf16[32,56,128]{2,1,0:T(8,128)(2,1)} %copy.12.weight_ref, bf16[32,32,1024]{2,1,0:T(8,128)(2,1)} %bitcast.18), custom_call_target="tpu_custom_call" | custom-call | tf_op jit(solution)/shard_map/pallas_call | solution.py:73
  (3 shorter events, 0.0 us)
Async XLA Ops:
  6.5 63.9 %all-gather.2.cloned.1.call-start = ((), (), s32[]{:S(2)}) async-start(), calls=%async_computation | async-start | bytes 4456448 | tf_op jit(solution)/shard_map/all_gather | solution.py:102
  9.8 7.4 %copy-start.1 = (s32[32,32]{1,0:T(8,128)S(1)}, s32[32,32]{1,0:T(8,128)}, u32[]{:S(2)}) copy-start(s32[32,32]{1,0:T(8,128)} %param.10) | copy-start | bytes 12292
  9.8 7.4 %copy-start = (bf16[32,32,200]{2,1,0:T(8,128)(2,1)S(1)}, bf16[32,32,200]{2,1,0:T(8,128)(2,1)}, u32[]{:S(2)}) copy-start(bf16[32,32,200]{2,1,0:T(8,128)(2,1)} %param.11) | copy-start | bytes 1228804
  9.8 6.6 %collective-permute-start = (f32[8,2048]{1,0:T(8,128)S(1)}, f32[8,2048]{1,0:T(8,128)S(1)}, u32[]{:S(2)}, u32[]{:S(2)}) collective-permute-start(f32[8,2048]{1,0:T(8,128)S(1)} %fusion.3), channel_id=1, source_target_pairs={{0,1},{1,2},{2,3},{3,4},{4,5},{5,6},{6,7},{7,8},{8,9},{9,10},{10,1... | collective-permute-start | bytes 196616 | tf_op jit(solution)/shard_map/ppermute | solution.py:97
Sparse Core Ops, SparseCore 0:
  17.2 53.1 all-gather.1

commit v18 on v17

--- a/solution.py
+++ b/solution.py
@@ -6,7 +6,7 @@
 from jax.sharding import PartitionSpec as P
 
 DEC = 4
-V_BLOCK = 8
+V_BLOCK = 16
 
 
 def band_matrix(taps, rows, cols):

time: 94.4 us -> 96.5 us (1.022)
  Pallas kernels: 8.88 us -> 11 us
    pallas_call x1, Pallas kernels: 8.88 us -> 11 us  [convolve(): pl.pallas_call(conv_kernel, grid=(v_local // vb,), in_specs=[pl.BlockSpec...]
where the time goes in v18:
time: 96.5 us; the launch traced here: 96.3 us
  waiting for transfers between devices  48 us (50%)
  matrix products  13.6 us (14%)
  between operations  13.5 us (14%)
  Pallas kernels  11 us (11%)
  local copies, waits for them, and re-layouts  5.27 us (5%)
  other arithmetic  2.52 us (3%)
  starting transfers between devices  2.49 us (3%)
    all_gather x1, waiting for transfers between devices, body(): lax.all_gather(own.astype(jnp.bfloat16), 'handler', axis=0, tiled=True)  48 us
    pallas_call x1, Pallas kernels, convolve(): pl.pallas_call(conv_kernel, grid=(v_local // vb,), in_specs=[pl.BlockSpec...  11 us
    dot_general x1, matrix products, body(): jnp.einsum('np,jp->nj', choose.astype(jnp.bfloat16), by_time, preferred_e...  8.08 us
    dot_general x1, matrix products, body(): jnp.einsum('tj,ctp->cjp', lowpass[:, :local_j], by_component, preferred_e...  4.05 us
    ppermute x1, starting transfers between devices, body(): lax.ppermute(jnp.sum(moment[:, None, :] * tail, axis=0), 'handler', [(i,...  2.49 us
    transpose x1, local copies, waits for them, and re-layouts, convolve(): padded.reshape(v_local, k, n_rows, SHIFTS).transpose(0, 2, 3, 1)  2.28 us
  transfers between devices with their start and end apart: 2, of which 1 were waited for; matrix products, arithmetic and copies ran while one was open for 10% of the time, Pallas kernels for 0%

profile of v18, /device:TPU:0, one launch (start us, length us, event | category | flops | bytes accessed | tf_op | source)
XLA Modules:
  0.0 96.3 jit_solution(2768977707885595998)
XLA Ops:
  6.5 0.0 all-gather.2.cloned.1.call-start
  6.5 0.7 convert_element_type.15
  7.2 1.1 %select_reduce_fusion = bf16[256,72]{0,1:T(8,128)(2,1)S(1)} fusion(f32[32]{0:T(128)S(1)} %convert_element_type.15, s32[72]{0:T(128)S(1)} %iota_multiply_fusion), kind=kLoop, calls=%fused_computation.4 | loop fusion | flops 2340864 | bytes 37280 | tf_op jit(solution)/shard_map/reduce_sum | solution.py:19
  8.3 1.4 %fusion.3 = f32[8,2048]{1,0:T(8,128)S(1)} fusion(bf16[6,256,2048]{2,1,0:T(8,128)(2,1)} %bitcast.16, f32[6,2048]{1,0:T(8,128)} %param.9, bf16[256,72]{0,1:T(8,128)(2,1)S(1)} %select_reduce_fusion), kind=kOutput, calls=%fused_computation.8 | convolution fusion | flops 6471680 | bytes 919552 | tf_op jit(solution)/shard_map/tj,ctp->cjp/dot_general | solution.py:95
  9.8 0.0 copy-start.1
  9.8 0.0 copy-start
  9.8 2.5 %collective-permute-start = (f32[8,2048]{1,0:T(8,128)S(1)}, f32[8,2048]{1,0:T(8,128)S(1)}, u32[]{:S(2)}, u32[]{:S(2)}) collective-permute-start(f32[8,2048]{1,0:T(8,128)S(1)} %fusion.3), channel_id=1, source_target_pairs={{0,1},{1,2},{2,3},{3,4},{4,5},{5,6},{6,7},{7,8},{8,9},{9,10},{10,1... | collective-permute-start | bytes 196616 | tf_op jit(solution)/shard_map/ppermute | solution.py:97
  12.3 4.0 %multiply_reduce_fusion = f32[64,2048]{1,0:T(8,128)S(1)} fusion(f32[6,2048]{1,0:T(8,128)} %param.9, bf16[256,72]{0,1:T(8,128)(2,1)S(1)} %select_reduce_fusion, bf16[256,6,2048]{2,0,1:T(8,128)(2,1)} %param.7), kind=kOutput, calls=%fused_computation.3 | convolution fusion | flops 404094976 | bytes 6897664 | tf_op jit(solution)/shard_map/tj,ctp->cjp/dot_general | solution.py:99
  16.3 0.0 collective-permute-done
  16.4 0.7 convert_element_type.17
  17.1 0.0 all-gather.2.cloned.1.call-update
  17.1 0.0 copy-done.1
  17.1 0.1 min.12
  17.2 0.0 copy-done
  17.2 1.5 %copy.13 = bf16[32,32,200]{1,0,2:T(8,128)(2,1)S(1)} copy(bf16[32,32,200]{2,1,0:T(8,128)(2,1)S(1)} %copy-done) | data formatting | bytes 819200
  18.7 0.3 pad.6.clone
  19.0 2.3 %copy.11 = bf16[32,56,4,32]{1,3,2,0:T(8,128)(2,1)S(1)} copy(bf16[32,56,4,32]{3,0,2,1:T(8,128)(2,1)S(1)} %bitcast.15) | data formatting | bytes 917504 | tf_op jit(solution)/shard_map/transpose | solution.py:71
  21.3 1.1 %copy.12.weight_ref = bf16[32,56,128]{2,1,0:T(8,128)(2,1)} copy(bf16[32,56,128]{1,2,0:T(8,128)(2,1)S(1)} %bitcast.17) | data formatting | bytes 917504 | tf_op jit(solution)/shard_map/reshape | solution.py:71
  22.4 48.0 %all-gather.2.cloned.1.call-done = bf16[1024,2048]{1,0:T(8,128)(2,1)} async-done(((bf16[64,2048]{1,0:T(8,128)(2,1)}), bf16[1024,2048]{1,0:T(8,128)(2,1)}) %all-gather.2.cloned.1.call-update) | async-done | bytes 4194320 | tf_op jit(solution)/shard_map/all_gather | solution.py:102
  70.4 8.1 %fusion.2 = bf16[1024,1024]{1,0:T(8,128)(2,1)} fusion(bf16[1024,2048]{1,0:T(8,128)(2,1)} %all-gather.2.cloned.1.call-done, s32[1024]{0:T(1024)S(1)} %min.12), kind=kOutput, calls=%fused_computation.7 | convolution fusion | flops 4298113024 | bytes 6295552 | tf_op jit(solution)/shard_map/np,jp->nj/dot_general | solution.py:107
  78.5 11.0 %shard_map.55 = f32[32,1024]{1,0:T(8,128)} custom-call(bf16[32,56,128]{2,1,0:T(8,128)(2,1)} %copy.12.weight_ref, bf16[32,32,1024]{2,1,0:T(8,128)(2,1)} %bitcast.18), custom_call_target="tpu_custom_call" | custom-call | tf_op jit(solution)/shard_map/pallas_call | solution.py:73
  (3 shorter events, 0.0 us)
Async XLA Ops:
  6.5 63.9 %all-gather.2.cloned.1.call-start = ((), (), s32[]{:S(2)}) async-start(), calls=%async_computation | async-start | bytes 4456448 | tf_op jit(solution)/shard_map/all_gather | solution.py:102
  9.8 7.4 %copy-start.1 = (s32[32,32]{1,0:T(8,128)S(1)}, s32[32,32]{1,0:T(8,128)}, u32[]{:S(2)}) copy-start(s32[32,32]{1,0:T(8,128)} %param.10) | copy-start | bytes 12292
  9.8 7.4 %copy-start = (bf16[32,32,200]{2,1,0:T(8,128)(2,1)S(1)}, bf16[32,32,200]{2,1,0:T(8,128)(2,1)}, u32[]{:S(2)}) copy-start(bf16[32,32,200]{2,1,0:T(8,128)(2,1)} %param.11) | copy-start | bytes 1228804
  9.8 6.6 %collective-permute-start = (f32[8,2048]{1,0:T(8,128)S(1)}, f32[8,2048]{1,0:T(8,128)S(1)}, u32[]{:S(2)}, u32[]{:S(2)}) collective-permute-start(f32[8,2048]{1,0:T(8,128)S(1)} %fusion.3), channel_id=1, source_target_pairs={{0,1},{1,2},{2,3},{3,4},{4,5},{5,6},{6,7},{7,8},{8,9},{9,10},{10,1... | collective-permute-start | bytes 196616 | tf_op jit(solution)/shard_map/ppermute | solution.py:97
Sparse Core Ops, SparseCore 0:
  17.2 53.1 all-gather.1

commit v19 on v17

--- a/solution.py
+++ b/solution.py
@@ -15,7 +15,7 @@
     col_ids = lax.broadcasted_iota(jnp.int32, (rows, cols, n_taps), 1)
     tap_ids = lax.broadcasted_iota(jnp.int32, (rows, cols, n_taps), 2)
     hit = DEC * col_ids - row_ids == tap_ids
-    picked = jnp.where(hit, taps.astype(jnp.float32)[None, None, :], 0.0)
+    picked = jnp.where(hit, taps[None, None, :], jnp.zeros((), taps.dtype)).astype(jnp.float32)
     return jnp.sum(picked, axis=2).astype(jnp.bfloat16)
 
 

time: 94.4 us -> 94.4 us (level)
  no operation moved by 1% of the time
where the time goes in v19:
time: 94.4 us; the launch traced here: 94.2 us
  waiting for transfers between devices  48 us (51%)
  matrix products  13.6 us (14%)
  between operations  13.5 us (14%)
  Pallas kernels  8.88 us (9%)
  local copies, waits for them, and re-layouts  5.27 us (6%)
  other arithmetic  2.52 us (3%)
  starting transfers between devices  2.49 us (3%)
    all_gather x1, waiting for transfers between devices, body(): lax.all_gather(own.astype(jnp.bfloat16), 'handler', axis=0, tiled=True)  48 us
    pallas_call x1, Pallas kernels, convolve(): pl.pallas_call(conv_kernel, grid=(v_local // vb,), in_specs=[pl.BlockSpec...  8.88 us
    dot_general x1, matrix products, body(): jnp.einsum('np,jp->nj', choose.astype(jnp.bfloat16), by_time, preferred_e...  8.08 us
    dot_general x1, matrix products, body(): jnp.einsum('tj,ctp->cjp', lowpass[:, :local_j], by_component, preferred_e...  4.05 us
    ppermute x1, starting transfers between devices, body(): lax.ppermute(jnp.sum(moment[:, None, :] * tail, axis=0), 'handler', [(i,...  2.49 us
    transpose x1, local copies, waits for them, and re-layouts, convolve(): padded.reshape(v_local, k, n_rows, SHIFTS).transpose(0, 2, 3, 1)  2.28 us
  transfers between devices with their start and end apart: 2, of which 1 were waited for; matrix products, arithmetic and copies ran while one was open for 10% of the time, Pallas kernels for 0%

profile of v19, /device:TPU:0, one launch (start us, length us, event | category | flops | bytes accessed | tf_op | source)
XLA Modules:
  0.0 94.2 jit_solution(8525248287072000045)
XLA Ops:
  6.5 0.0 all-gather.2.cloned.1.call-start
  6.5 1.8 %fusion.4 = bf16[256,72]{0,1:T(8,128)(2,1)S(1)} fusion(s32[72]{0:T(128)S(1)} %iota_multiply_fusion, bf16[32]{0:T(256)(128)(2,1)} %param.8), kind=kLoop, calls=%fused_computation.8 | loop fusion | flops 2340864 | bytes 37216 | tf_op jit(solution)/shard_map/reduce_sum | solution.py:19
  8.3 1.4 %fusion.5 = f32[8,2048]{1,0:T(8,128)S(1)} fusion(bf16[6,256,2048]{2,1,0:T(8,128)(2,1)} %bitcast.16, f32[6,2048]{1,0:T(8,128)} %param.9, bf16[256,72]{0,1:T(8,128)(2,1)S(1)} %fusion.4), kind=kOutput, calls=%fused_computation.9 | convolution fusion | flops 6471680 | bytes 919552 | tf_op jit(solution)/shard_map/tj,ctp->cjp/dot_general | solution.py:95
  9.8 0.0 copy-start.1
  9.8 0.0 copy-start
  9.8 2.5 %collective-permute-start = (f32[8,2048]{1,0:T(8,128)S(1)}, f32[8,2048]{1,0:T(8,128)S(1)}, u32[]{:S(2)}, u32[]{:S(2)}) collective-permute-start(f32[8,2048]{1,0:T(8,128)S(1)} %fusion.5), channel_id=1, source_target_pairs={{0,1},{1,2},{2,3},{3,4},{4,5},{5,6},{6,7},{7,8},{8,9},{9,10},{10,1... | collective-permute-start | bytes 196616 | tf_op jit(solution)/shard_map/ppermute | solution.py:97
  12.3 4.0 %multiply_reduce_fusion = f32[64,2048]{1,0:T(8,128)S(1)} fusion(f32[6,2048]{1,0:T(8,128)} %param.9, bf16[256,72]{0,1:T(8,128)(2,1)S(1)} %fusion.4, bf16[256,6,2048]{2,0,1:T(8,128)(2,1)} %param.7), kind=kOutput, calls=%fused_computation.3 | convolution fusion | flops 404094976 | bytes 6897664 | tf_op jit(solution)/shard_map/tj,ctp->cjp/dot_general | solution.py:99
  16.3 0.0 collective-permute-done
  16.4 0.7 convert_element_type.5
  17.1 0.0 all-gather.2.cloned.1.call-update
  17.1 0.0 copy-done.1
  17.1 0.1 min.12
  17.2 0.0 copy-done
  17.2 1.5 %copy.13 = bf16[32,32,200]{1,0,2:T(8,128)(2,1)S(1)} copy(bf16[32,32,200]{2,1,0:T(8,128)(2,1)S(1)} %copy-done) | data formatting | bytes 819200
  18.7 0.3 pad.6.clone
  19.0 2.3 %copy.11 = bf16[32,56,4,32]{1,3,2,0:T(8,128)(2,1)S(1)} copy(bf16[32,56,4,32]{3,0,2,1:T(8,128)(2,1)S(1)} %bitcast.15) | data formatting | bytes 917504 | tf_op jit(solution)/shard_map/transpose | solution.py:71
  21.3 1.1 %copy.12.weight_ref = bf16[32,56,128]{2,1,0:T(8,128)(2,1)} copy(bf16[32,56,128]{1,2,0:T(8,128)(2,1)S(1)} %bitcast.17) | data formatting | bytes 917504 | tf_op jit(solution)/shard_map/reshape | solution.py:71
  22.4 48.0 %all-gather.2.cloned.1.call-done = bf16[1024,2048]{1,0:T(8,128)(2,1)} async-done(((bf16[64,2048]{1,0:T(8,128)(2,1)}), bf16[1024,2048]{1,0:T(8,128)(2,1)}) %all-gather.2.cloned.1.call-update) | async-done | bytes 4194320 | tf_op jit(solution)/shard_map/all_gather | solution.py:102
  70.4 8.1 %fusion.3 = bf16[1024,1024]{1,0:T(8,128)(2,1)} fusion(bf16[1024,2048]{1,0:T(8,128)(2,1)} %all-gather.2.cloned.1.call-done, s32[1024]{0:T(1024)S(1)} %min.12), kind=kOutput, calls=%fused_computation.7 | convolution fusion | flops 4298113024 | bytes 6295552 | tf_op jit(solution)/shard_map/np,jp->nj/dot_general | solution.py:107
  78.5 8.9 %shard_map.55 = f32[32,1024]{1,0:T(8,128)} custom-call(bf16[32,56,128]{2,1,0:T(8,128)(2,1)} %copy.12.weight_ref, bf16[32,32,1024]{2,1,0:T(8,128)(2,1)} %bitcast.18), custom_call_target="tpu_custom_call" | custom-call | tf_op jit(solution)/shard_map/pallas_call | solution.py:73
  (3 shorter events, 0.0 us)
Async XLA Ops:
  6.5 63.9 %all-gather.2.cloned.1.call-start = ((), (), s32[]{:S(2)}) async-start(), calls=%async_computation | async-start | bytes 4456448 | tf_op jit(solution)/shard_map/all_gather | solution.py:102
  9.8 7.4 %copy-start.1 = (s32[32,32]{1,0:T(8,128)S(1)}, s32[32,32]{1,0:T(8,128)}, u32[]{:S(2)}) copy-start(s32[32,32]{1,0:T(8,128)} %param.10) | copy-start | bytes 12292
  9.8 7.4 %copy-start = (bf16[32,32,200]{2,1,0:T(8,128)(2,1)S(1)}, bf16[32,32,200]{2,1,0:T(8,128)(2,1)}, u32[]{:S(2)}) copy-start(bf16[32,32,200]{2,1,0:T(8,128)(2,1)} %param.11) | copy-start | bytes 1228804
  9.8 6.6 %collective-permute-start = (f32[8,2048]{1,0:T(8,128)S(1)}, f32[8,2048]{1,0:T(8,128)S(1)}, u32[]{:S(2)}, u32[]{:S(2)}) collective-permute-start(f32[8,2048]{1,0:T(8,128)S(1)} %fusion.5), channel_id=1, source_target_pairs={{0,1},{1,2},{2,3},{3,4},{4,5},{5,6},{6,7},{7,8},{8,9},{9,10},{10,1... | collective-permute-start | bytes 196616 | tf_op jit(solution)/shard_map/ppermute | solution.py:97
Sparse Core Ops, SparseCore 0:
  17.2 53.1 all-gather.1

commit v20 on v19

--- a/solution.py
+++ b/solution.py
@@ -11,12 +11,16 @@
 
 def band_matrix(taps, rows, cols):
     n_taps = taps.shape[0]
-    row_ids = lax.broadcasted_iota(jnp.int32, (rows, cols, n_taps), 0)
-    col_ids = lax.broadcasted_iota(jnp.int32, (rows, cols, n_taps), 1)
-    tap_ids = lax.broadcasted_iota(jnp.int32, (rows, cols, n_taps), 2)
-    hit = DEC * col_ids - row_ids == tap_ids
-    picked = jnp.where(hit, taps[None, None, :], jnp.zeros((), taps.dtype)).astype(jnp.float32)
-    return jnp.sum(picked, axis=2).astype(jnp.bfloat16)
+    span = -(-(n_taps + DEC - 1) // DEC)
+    padded = jnp.pad(taps, (DEC - 1, span * DEC - n_taps - DEC + 1))
+    phase = padded.reshape(span, DEC)[:, ::-1].T
+    s_ids = lax.broadcasted_iota(jnp.int32, (rows // DEC, DEC, cols), 0)
+    j_ids = lax.broadcasted_iota(jnp.int32, (rows // DEC, DEC, cols), 2)
+    lag = j_ids - s_ids
+    matrix = jnp.zeros((rows // DEC, DEC, cols), taps.dtype)
+    for d in range(span):
+        matrix = jnp.where(lag == d, phase[None, :, d, None], matrix)
+    return matrix.reshape(rows, cols)
 
 
 SHIFTS = 4

time: 94.4 us -> 94.9 us (level)
  local copies, waits for them, and re-layouts: 5.27 us -> 7.35 us
  other arithmetic: 2.52 us -> 0.8 us
    reduce_sum x1 -> x0, other arithmetic: 1.78 us -> none  [band_matrix(): return jnp.sum(picked, axis=2).astype(jnp.bfloat16)]
    broadcast_in_dim x0 -> x19, local copies, waits for them, and re-layouts: none -> 1.05 us  [band_matrix(): matrix = jnp.where(lag == d, phase[None, :, d, None], matrix)]
where the time goes in v20:
time: 94.9 us; the launch traced here: 94.7 us
  waiting for transfers between devices  48 us (51%)
  between operations  13.6 us (14%)
  matrix products  13.5 us (14%)
  Pallas kernels  8.88 us (9%)
  local copies, waits for them, and re-layouts  7.35 us (8%)
  starting transfers between devices  2.49 us (3%)
    all_gather x1, waiting for transfers between devices, body(): lax.all_gather(own.astype(jnp.bfloat16), 'handler', axis=0, tiled=True)  48 us
    pallas_call x1, Pallas kernels, convolve(): pl.pallas_call(conv_kernel, grid=(v_local // vb,), in_specs=[pl.BlockSpec...  8.88 us
    dot_general x1, matrix products, body(): jnp.einsum('np,jp->nj', choose.astype(jnp.bfloat16), by_time, preferred_e...  8.07 us
    dot_general x1, matrix products, body(): jnp.einsum('tj,ctp->cjp', lowpass[:, :local_j], by_component, preferred_e...  4.05 us
    ppermute x1, starting transfers between devices, body(): lax.ppermute(jnp.sum(moment[:, None, :] * tail, axis=0), 'handler', [(i,...  2.49 us
    transpose x1, local copies, waits for them, and re-layouts, convolve(): padded.reshape(v_local, k, n_rows, SHIFTS).transpose(0, 2, 3, 1)  2.28 us
  transfers between devices with their start and end apart: 2, of which 1 were waited for; matrix products, arithmetic and copies ran while one was open for 10% of the time, Pallas kernels for 0%

profile of v20, /device:TPU:0, one launch (start us, length us, event | category | flops | bytes accessed | tf_op | source)
XLA Modules:
  0.0 94.7 jit_solution(11895419752272955267)
XLA Ops:
  6.5 0.0 all-gather.2.cloned.1.call-start
  6.5 0.7 pad.11
  7.3 0.1 reshape.71
  7.4 0.1 rev.3
  7.5 0.1 broadcast_in_dim.110
  7.6 0.1 broadcast_in_dim.142
  7.7 0.1 broadcast_in_dim.138
  7.8 0.1 broadcast_in_dim.134
  8.0 0.1 broadcast_in_dim.130
  8.1 0.1 broadcast_in_dim.126
  8.2 0.1 broadcast_in_dim.122
  8.3 0.1 broadcast_in_dim.118
  8.5 0.1 broadcast_in_dim.114
  8.6 0.1 iota.89
  8.7 0.1 fusion.14
  8.8 1.4 %fusion.3 = f32[8,2048]{1,0:T(8,128)S(1)} fusion(bf16[6,256,2048]{2,1,0:T(8,128)(2,1)} %bitcast.35, f32[6,2048]{1,0:T(8,128)} %param.9, bf16[256,72]{0,1:T(8,128)(2,1)S(1)} %fusion.14), kind=kOutput, calls=%fused_computation.6 | convolution fusion | flops 6471680 | bytes 919552 | tf_op jit(solution)/shard_map/tj,ctp->cjp/dot_general | solution.py:99
  10.2 0.0 copy-start.1
  10.2 0.0 copy-start
  10.2 2.5 %collective-permute-start = (f32[8,2048]{1,0:T(8,128)S(1)}, f32[8,2048]{1,0:T(8,128)S(1)}, u32[]{:S(2)}, u32[]{:S(2)}) collective-permute-start(f32[8,2048]{1,0:T(8,128)S(1)} %fusion.3), channel_id=1, source_target_pairs={{0,1},{1,2},{2,3},{3,4},{4,5},{5,6},{6,7},{7,8},{8,9},{9,10},{10,1... | collective-permute-start | bytes 196616 | tf_op jit(solution)/shard_map/ppermute | solution.py:101
  12.7 4.0 %multiply_reduce_fusion = f32[64,2048]{1,0:T(8,128)S(1)} fusion(f32[6,2048]{1,0:T(8,128)} %param.9, bf16[256,72]{0,1:T(8,128)(2,1)S(1)} %fusion.14, bf16[256,6,2048]{2,0,1:T(8,128)(2,1)} %param.7), kind=kOutput, calls=%fused_computation.3 | convolution fusion | flops 404094976 | bytes 6897664 | tf_op jit(solution)/shard_map/tj,ctp->cjp/dot_general | solution.py:103
  16.8 0.0 collective-permute-done
  16.8 0.7 convert_element_type.11
  17.5 0.0 all-gather.2.cloned.1.call-update
  17.6 0.0 copy-done.1
  17.6 0.1 min.12
  17.7 0.0 copy-done
  17.7 1.5 %copy.13 = bf16[32,32,200]{1,0,2:T(8,128)(2,1)S(1)} copy(bf16[32,32,200]{2,1,0:T(8,128)(2,1)S(1)} %copy-done) | data formatting | bytes 819200
  19.2 0.3 pad.10.clone
  19.5 2.3 %copy.11 = bf16[32,56,4,32]{1,3,2,0:T(8,128)(2,1)S(1)} copy(bf16[32,56,4,32]{3,0,2,1:T(8,128)(2,1)S(1)} %bitcast.34) | data formatting | bytes 917504 | tf_op jit(solution)/shard_map/transpose | solution.py:75
  21.8 1.1 %copy.12.weight_ref = bf16[32,56,128]{2,1,0:T(8,128)(2,1)} copy(bf16[32,56,128]{1,2,0:T(8,128)(2,1)S(1)} %bitcast.36) | data formatting | bytes 917504 | tf_op jit(solution)/shard_map/reshape | solution.py:75
  22.9 48.0 %all-gather.2.cloned.1.call-done = bf16[1024,2048]{1,0:T(8,128)(2,1)} async-done(((bf16[64,2048]{1,0:T(8,128)(2,1)}), bf16[1024,2048]{1,0:T(8,128)(2,1)}) %all-gather.2.cloned.1.call-update) | async-done | bytes 4194320 | tf_op jit(solution)/shard_map/all_gather | solution.py:106
  70.9 8.1 %fusion.2 = bf16[1024,1024]{1,0:T(8,128)(2,1)} fusion(bf16[1024,2048]{1,0:T(8,128)(2,1)} %all-gather.2.cloned.1.call-done, s32[1024]{0:T(1024)S(1)} %min.12), kind=kOutput, calls=%fused_computation.5 | convolution fusion | flops 4298113024 | bytes 6295552 | tf_op jit(solution)/shard_map/np,jp->nj/dot_general | solution.py:111
  78.9 8.9 %shard_map.55 = f32[32,1024]{1,0:T(8,128)} custom-call(bf16[32,56,128]{2,1,0:T(8,128)(2,1)} %copy.12.weight_ref, bf16[32,32,1024]{2,1,0:T(8,128)(2,1)} %bitcast.37), custom_call_target="tpu_custom_call" | custom-call | tf_op jit(solution)/shard_map/pallas_call | solution.py:77
  (13 shorter events, 0.1 us)
Async XLA Ops:
  6.5 64.3 %all-gather.2.cloned.1.call-start = ((), (), s32[]{:S(2)}) async-start(), calls=%async_computation | async-start | bytes 4456448 | tf_op jit(solution)/shard_map/all_gather | solution.py:106
  10.2 7.4 %copy-start.1 = (s32[32,32]{1,0:T(8,128)S(1)}, s32[32,32]{1,0:T(8,128)}, u32[]{:S(2)}) copy-start(s32[32,32]{1,0:T(8,128)} %param.10) | copy-start | bytes 12292
  10.2 7.4 %copy-start = (bf16[32,32,200]{2,1,0:T(8,128)(2,1)S(1)}, bf16[32,32,200]{2,1,0:T(8,128)(2,1)}, u32[]{:S(2)}) copy-start(bf16[32,32,200]{2,1,0:T(8,128)(2,1)} %param.11) | copy-start | bytes 1228804
  10.2 6.6 %collective-permute-start = (f32[8,2048]{1,0:T(8,128)S(1)}, f32[8,2048]{1,0:T(8,128)S(1)}, u32[]{:S(2)}, u32[]{:S(2)}) collective-permute-start(f32[8,2048]{1,0:T(8,128)S(1)} %fusion.3), channel_id=1, source_target_pairs={{0,1},{1,2},{2,3},{3,4},{4,5},{5,6},{6,7},{7,8},{8,9},{9,10},{10,1... | collective-permute-start | bytes 196616 | tf_op jit(solution)/shard_map/ppermute | solution.py:101
Sparse Core Ops, SparseCore 0:
  17.7 53.1 all-gather.1

commit v21 on v20

--- a/solution.py
+++ b/solution.py
@@ -12,14 +12,16 @@
 def band_matrix(taps, rows, cols):
     n_taps = taps.shape[0]
     span = -(-(n_taps + DEC - 1) // DEC)
-    padded = jnp.pad(taps, (DEC - 1, span * DEC - n_taps - DEC + 1))
-    phase = padded.reshape(span, DEC)[:, ::-1].T
     s_ids = lax.broadcasted_iota(jnp.int32, (rows // DEC, DEC, cols), 0)
     j_ids = lax.broadcasted_iota(jnp.int32, (rows // DEC, DEC, cols), 2)
     lag = j_ids - s_ids
     matrix = jnp.zeros((rows // DEC, DEC, cols), taps.dtype)
     for d in range(span):
-        matrix = jnp.where(lag == d, phase[None, :, d, None], matrix)
+        low, high = DEC * d - DEC + 1, DEC * d + 1
+        column = taps[max(low, 0):min(high, n_taps)][::-1]
+        column = jnp.concatenate([jnp.zeros((max(high - n_taps, 0),), taps.dtype), column,
+                                  jnp.zeros((max(-low, 0),), taps.dtype)])
+        matrix = jnp.where(lag == d, column[None, :, None], matrix)
     return matrix.reshape(rows, cols)
 
 

time: 94.9 us -> 96.6 us (1.018)
  other arithmetic: 0.8 us -> 1.91 us
    slice x0 -> x1, other arithmetic: none -> 1.03 us  [band_matrix(): column = taps[max(low, 0):min(high, n_taps)][::-1]]
where the time goes in v21:
time: 96.6 us; the launch traced here: 96.4 us
  waiting for transfers between devices  48 us (50%)
  matrix products  13.6 us (14%)
  between operations  13.6 us (14%)
  Pallas kernels  8.88 us (9%)
  local copies, waits for them, and re-layouts  7.96 us (8%)
  starting transfers between devices  2.49 us (3%)
  other arithmetic  1.91 us (2%)
    all_gather x1, waiting for transfers between devices, body(): lax.all_gather(own.astype(jnp.bfloat16), 'handler', axis=0, tiled=True)  48 us
    pallas_call x1, Pallas kernels, convolve(): pl.pallas_call(conv_kernel, grid=(v_local // vb,), in_specs=[pl.BlockSpec...  8.88 us
    dot_general x1, matrix products, body(): jnp.einsum('np,jp->nj', choose.astype(jnp.bfloat16), by_time, preferred_e...  8.07 us
    dot_general x1, matrix products, body(): jnp.einsum('tj,ctp->cjp', lowpass[:, :local_j], by_component, preferred_e...  4.05 us
    ppermute x1, starting transfers between devices, body(): lax.ppermute(jnp.sum(moment[:, None, :] * tail, axis=0), 'handler', [(i,...  2.49 us
    transpose x1, local copies, waits for them, and re-layouts, convolve(): padded.reshape(v_local, k, n_rows, SHIFTS).transpose(0, 2, 3, 1)  2.28 us
  transfers between devices with their start and end apart: 2, of which 1 were waited for; matrix products, arithmetic and copies ran while one was open for 10% of the time, Pallas kernels for 0%

profile of v21, /device:TPU:0, one launch (start us, length us, event | category | flops | bytes accessed | tf_op | source)
XLA Modules:
  0.0 96.4 jit_solution(10964166799992719787)
XLA Ops:
  6.5 0.0 all-gather.2.cloned.1.call-start
  6.5 0.7 slice.56
  7.3 0.1 rev.24
  7.4 1.0 %fusion.25 = (bf16[4]{0:T(256)(128)(2,1)S(1)}, bf16[4]{0:T(256)(128)(2,1)S(1)}, bf16[4]{0:T(256)(128)(2,1)S(1)}, bf16[4]{0:T(256)(128)(2,1)S(1)}, bf16[4]{0:T(25...) fusion(bf16[32]{0:T(256)(128)(2,1)} %param.8, ...), kind=kLoop, calls=%fused_computation.35 | loop fusion | flops 4 | bytes 132 | tf_op jit(solution)/shard_map/slice | solution.py:21
  8.4 0.1 rev.25
  8.5 0.1 rev.30
  8.6 0.1 rev.29
  8.7 0.1 rev.28
  8.8 0.1 rev.27
  8.9 0.1 rev.26
  9.0 0.1 rev.31
  9.1 0.1 broadcast_in_dim.121
  9.2 0.1 broadcast_in_dim.106
  9.3 0.1 broadcast_in_dim.109
  9.5 0.1 broadcast_in_dim.112
  9.6 0.1 broadcast_in_dim.115
  9.7 0.1 broadcast_in_dim.118
  9.8 0.1 broadcast_in_dim.103
  10.0 0.1 pad_maximum_fusion
  10.0 0.1 broadcast_in_dim.100
  10.2 0.1 broadcast_in_dim.124
  10.3 0.1 iota.89
  10.4 0.1 fusion.14
  10.5 1.4 %fusion.3 = f32[8,2048]{1,0:T(8,128)S(1)} fusion(bf16[6,256,2048]{2,1,0:T(8,128)(2,1)} %bitcast.16, f32[6,2048]{1,0:T(8,128)} %param.9, bf16[256,72]{0,1:T(8,128)(2,1)S(1)} %fusion.14), kind=kOutput, calls=%fused_computation.6 | convolution fusion | flops 6471680 | bytes 919552 | tf_op jit(solution)/shard_map/tj,ctp->cjp/dot_general | solution.py:101
  11.9 0.0 copy-start.1
  11.9 0.0 copy-start
  11.9 2.5 %collective-permute-start = (f32[8,2048]{1,0:T(8,128)S(1)}, f32[8,2048]{1,0:T(8,128)S(1)}, u32[]{:S(2)}, u32[]{:S(2)}) collective-permute-start(f32[8,2048]{1,0:T(8,128)S(1)} %fusion.3), channel_id=1, source_target_pairs={{0,1},{1,2},{2,3},{3,4},{4,5},{5,6},{6,7},{7,8},{8,9},{9,10},{10,1... | collective-permute-start | bytes 196616 | tf_op jit(solution)/shard_map/ppermute | solution.py:103
  14.4 4.1 %multiply_reduce_fusion = f32[64,2048]{1,0:T(8,128)S(1)} fusion(f32[6,2048]{1,0:T(8,128)} %param.9, bf16[256,72]{0,1:T(8,128)(2,1)S(1)} %fusion.14, bf16[256,6,2048]{2,0,1:T(8,128)(2,1)} %param.7), kind=kOutput, calls=%fused_computation.3 | convolution fusion | flops 404094976 | bytes 6897664 | tf_op jit(solution)/shard_map/tj,ctp->cjp/dot_general | solution.py:105
  18.5 0.0 collective-permute-done
  18.5 0.7 convert_element_type.9
  19.3 0.0 all-gather.2.cloned.1.call-update
  19.3 0.0 copy-done.1
  19.3 0.1 min.12
  19.4 0.0 copy-done
  19.4 1.5 %copy.13 = bf16[32,32,200]{1,0,2:T(8,128)(2,1)S(1)} copy(bf16[32,32,200]{2,1,0:T(8,128)(2,1)S(1)} %copy-done) | data formatting | bytes 819200
  20.9 0.3 pad.7.clone
  21.2 2.3 %copy.11 = bf16[32,56,4,32]{1,3,2,0:T(8,128)(2,1)S(1)} copy(bf16[32,56,4,32]{3,0,2,1:T(8,128)(2,1)S(1)} %bitcast.15) | data formatting | bytes 917504 | tf_op jit(solution)/shard_map/transpose | solution.py:77
  23.5 1.1 %copy.12.weight_ref = bf16[32,56,128]{2,1,0:T(8,128)(2,1)} copy(bf16[32,56,128]{1,2,0:T(8,128)(2,1)S(1)} %bitcast.17) | data formatting | bytes 917504 | tf_op jit(solution)/shard_map/reshape | solution.py:77
  24.6 48.0 %all-gather.2.cloned.1.call-done = bf16[1024,2048]{1,0:T(8,128)(2,1)} async-done(((bf16[64,2048]{1,0:T(8,128)(2,1)}), bf16[1024,2048]{1,0:T(8,128)(2,1)}) %all-gather.2.cloned.1.call-update) | async-done | bytes 4194320 | tf_op jit(solution)/shard_map/all_gather | solution.py:108
  72.6 8.1 %fusion.2 = bf16[1024,1024]{1,0:T(8,128)(2,1)} fusion(bf16[1024,2048]{1,0:T(8,128)(2,1)} %all-gather.2.cloned.1.call-done, s32[1024]{0:T(1024)S(1)} %min.12), kind=kOutput, calls=%fused_computation.5 | convolution fusion | flops 4298113024 | bytes 6295552 | tf_op jit(solution)/shard_map/np,jp->nj/dot_general | solution.py:113
  80.6 8.9 %shard_map.55 = f32[32,1024]{1,0:T(8,128)} custom-call(bf16[32,56,128]{2,1,0:T(8,128)(2,1)} %copy.12.weight_ref, bf16[32,32,1024]{2,1,0:T(8,128)(2,1)} %bitcast.18), custom_call_target="tpu_custom_call" | custom-call | tf_op jit(solution)/shard_map/pallas_call | solution.py:79
  (12 shorter events, 0.1 us)
Async XLA Ops:
  6.5 66.0 %all-gather.2.cloned.1.call-start = ((), (), s32[]{:S(2)}) async-start(), calls=%async_computation | async-start | bytes 4456448 | tf_op jit(solution)/shard_map/all_gather | solution.py:108
  11.9 7.4 %copy-start.1 = (s32[32,32]{1,0:T(8,128)S(1)}, s32[32,32]{1,0:T(8,128)}, u32[]{:S(2)}) copy-start(s32[32,32]{1,0:T(8,128)} %param.10) | copy-start | bytes 12292
  11.9 7.5 %copy-start = (bf16[32,32,200]{2,1,0:T(8,128)(2,1)S(1)}, bf16[32,32,200]{2,1,0:T(8,128)(2,1)}, u32[]{:S(2)}) copy-start(bf16[32,32,200]{2,1,0:T(8,128)(2,1)} %param.11) | copy-start | bytes 1228804
  11.9 6.6 %collective-permute-start = (f32[8,2048]{1,0:T(8,128)S(1)}, f32[8,2048]{1,0:T(8,128)S(1)}, u32[]{:S(2)}, u32[]{:S(2)}) collective-permute-start(f32[8,2048]{1,0:T(8,128)S(1)} %fusion.3), channel_id=1, source_target_pairs={{0,1},{1,2},{2,3},{3,4},{4,5},{5,6},{6,7},{7,8},{8,9},{9,10},{10,1... | collective-permute-start | bytes 196616 | tf_op jit(solution)/shard_map/ppermute | solution.py:103
Sparse Core Ops, SparseCore 0:
  19.4 53.1 all-gather.1

commit v22 on v17

--- a/solution.py
+++ b/solution.py
@@ -35,7 +35,7 @@
     lag = col - SHIFTS * row
 
     for v in range(vb):
-        slot = v % 2
+        slot = v % 3
         rows = picked_ref[v]
         shifted_ref[slot, 0:k, :] = rows
         for b in range(1, SHIFTS):
@@ -79,7 +79,7 @@
         ],
         out_specs=pl.BlockSpec((vb, width), lambda i: (i, 0)),
         out_shape=jax.ShapeDtypeStruct((v_local, width), jnp.float32),
-        scratch_shapes=[pltpu.VMEM((2, SHIFTS * k, width), jnp.bfloat16), pltpu.VMEM((width // 128, 8 * vb, 128), jnp.float32)],
+        scratch_shapes=[pltpu.VMEM((3, SHIFTS * k, width), jnp.bfloat16), pltpu.VMEM((width // 128, 8 * vb, 128), jnp.float32)],
     )(weight, picked)
 
 

time: 94.4 us -> 94.5 us (level)
  no operation moved by 1% of the time
where the time goes in v22:
time: 94.5 us; the launch traced here: 94.3 us
  waiting for transfers between devices  48 us (51%)
  matrix products  13.6 us (14%)
  between operations  13.5 us (14%)
  Pallas kernels  8.94 us (9%)
  local copies, waits for them, and re-layouts  5.27 us (6%)
  other arithmetic  2.52 us (3%)
  starting transfers between devices  2.49 us (3%)
    all_gather x1, waiting for transfers between devices, body(): lax.all_gather(own.astype(jnp.bfloat16), 'handler', axis=0, tiled=True)  48 us
    pallas_call x1, Pallas kernels, convolve(): pl.pallas_call(conv_kernel, grid=(v_local // vb,), in_specs=[pl.BlockSpec...  8.94 us
    dot_general x1, matrix products, body(): jnp.einsum('np,jp->nj', choose.astype(jnp.bfloat16), by_time, preferred_e...  8.08 us
    dot_general x1, matrix products, body(): jnp.einsum('tj,ctp->cjp', lowpass[:, :local_j], by_component, preferred_e...  4.05 us
    ppermute x1, starting transfers between devices, body(): lax.ppermute(jnp.sum(moment[:, None, :] * tail, axis=0), 'handler', [(i,...  2.49 us
    transpose x1, local copies, waits for them, and re-layouts, convolve(): padded.reshape(v_local, k, n_rows, SHIFTS).transpose(0, 2, 3, 1)  2.28 us
  transfers between devices with their start and end apart: 2, of which 1 were waited for; matrix products, arithmetic and copies ran while one was open for 10% of the time, Pallas kernels for 0%

profile of v22, /device:TPU:0, one launch (start us, length us, event | category | flops | bytes accessed | tf_op | source)
XLA Modules:
  0.0 94.3 jit_solution(10794076817490162923)
XLA Ops:
  6.5 0.0 all-gather.2.cloned.1.call-start
  6.5 0.7 convert_element_type.15
  7.2 1.1 %select_reduce_fusion = bf16[256,72]{0,1:T(8,128)(2,1)S(1)} fusion(f32[32]{0:T(128)S(1)} %convert_element_type.15, s32[72]{0:T(128)S(1)} %iota_multiply_fusion), kind=kLoop, calls=%fused_computation.4 | loop fusion | flops 2340864 | bytes 37280 | tf_op jit(solution)/shard_map/reduce_sum | solution.py:19
  8.3 1.4 %fusion.3 = f32[8,2048]{1,0:T(8,128)S(1)} fusion(bf16[6,256,2048]{2,1,0:T(8,128)(2,1)} %bitcast.16, f32[6,2048]{1,0:T(8,128)} %param.9, bf16[256,72]{0,1:T(8,128)(2,1)S(1)} %select_reduce_fusion), kind=kOutput, calls=%fused_computation.8 | convolution fusion | flops 6471680 | bytes 919552 | tf_op jit(solution)/shard_map/tj,ctp->cjp/dot_general | solution.py:95
  9.8 0.0 copy-start.1
  9.8 0.0 copy-start
  9.8 2.5 %collective-permute-start = (f32[8,2048]{1,0:T(8,128)S(1)}, f32[8,2048]{1,0:T(8,128)S(1)}, u32[]{:S(2)}, u32[]{:S(2)}) collective-permute-start(f32[8,2048]{1,0:T(8,128)S(1)} %fusion.3), channel_id=1, source_target_pairs={{0,1},{1,2},{2,3},{3,4},{4,5},{5,6},{6,7},{7,8},{8,9},{9,10},{10,1... | collective-permute-start | bytes 196616 | tf_op jit(solution)/shard_map/ppermute | solution.py:97
  12.3 4.0 %multiply_reduce_fusion = f32[64,2048]{1,0:T(8,128)S(1)} fusion(f32[6,2048]{1,0:T(8,128)} %param.9, bf16[256,72]{0,1:T(8,128)(2,1)S(1)} %select_reduce_fusion, bf16[256,6,2048]{2,0,1:T(8,128)(2,1)} %param.7), kind=kOutput, calls=%fused_computation.3 | convolution fusion | flops 404094976 | bytes 6897664 | tf_op jit(solution)/shard_map/tj,ctp->cjp/dot_general | solution.py:99
  16.3 0.0 collective-permute-done
  16.4 0.7 convert_element_type.17
  17.1 0.0 all-gather.2.cloned.1.call-update
  17.1 0.0 copy-done.1
  17.1 0.1 min.12
  17.2 0.0 copy-done
  17.2 1.5 %copy.13 = bf16[32,32,200]{1,0,2:T(8,128)(2,1)S(1)} copy(bf16[32,32,200]{2,1,0:T(8,128)(2,1)S(1)} %copy-done) | data formatting | bytes 819200
  18.7 0.3 pad.6.clone
  19.0 2.3 %copy.11 = bf16[32,56,4,32]{1,3,2,0:T(8,128)(2,1)S(1)} copy(bf16[32,56,4,32]{3,0,2,1:T(8,128)(2,1)S(1)} %bitcast.15) | data formatting | bytes 917504 | tf_op jit(solution)/shard_map/transpose | solution.py:71
  21.3 1.1 %copy.12.weight_ref = bf16[32,56,128]{2,1,0:T(8,128)(2,1)} copy(bf16[32,56,128]{1,2,0:T(8,128)(2,1)S(1)} %bitcast.17) | data formatting | bytes 917504 | tf_op jit(solution)/shard_map/reshape | solution.py:71
  22.4 48.0 %all-gather.2.cloned.1.call-done = bf16[1024,2048]{1,0:T(8,128)(2,1)} async-done(((bf16[64,2048]{1,0:T(8,128)(2,1)}), bf16[1024,2048]{1,0:T(8,128)(2,1)}) %all-gather.2.cloned.1.call-update) | async-done | bytes 4194320 | tf_op jit(solution)/shard_map/all_gather | solution.py:102
  70.4 8.1 %fusion.2 = bf16[1024,1024]{1,0:T(8,128)(2,1)} fusion(bf16[1024,2048]{1,0:T(8,128)(2,1)} %all-gather.2.cloned.1.call-done, s32[1024]{0:T(1024)S(1)} %min.12), kind=kOutput, calls=%fused_computation.7 | convolution fusion | flops 4298113024 | bytes 6295552 | tf_op jit(solution)/shard_map/np,jp->nj/dot_general | solution.py:107
  78.5 8.9 %shard_map.55 = f32[32,1024]{1,0:T(8,128)} custom-call(bf16[32,56,128]{2,1,0:T(8,128)(2,1)} %copy.12.weight_ref, bf16[32,32,1024]{2,1,0:T(8,128)(2,1)} %bitcast.18), custom_call_target="tpu_custom_call" | custom-call | tf_op jit(solution)/shard_map/pallas_call | solution.py:73
  (3 shorter events, 0.0 us)
Async XLA Ops:
  6.5 63.9 %all-gather.2.cloned.1.call-start = ((), (), s32[]{:S(2)}) async-start(), calls=%async_computation | async-start | bytes 4456448 | tf_op jit(solution)/shard_map/all_gather | solution.py:102
  9.8 7.4 %copy-start.1 = (s32[32,32]{1,0:T(8,128)S(1)}, s32[32,32]{1,0:T(8,128)}, u32[]{:S(2)}) copy-start(s32[32,32]{1,0:T(8,128)} %param.10) | copy-start | bytes 12292
  9.8 7.4 %copy-start = (bf16[32,32,200]{2,1,0:T(8,128)(2,1)S(1)}, bf16[32,32,200]{2,1,0:T(8,128)(2,1)}, u32[]{:S(2)}) copy-start(bf16[32,32,200]{2,1,0:T(8,128)(2,1)} %param.11) | copy-start | bytes 1228804
  9.8 6.6 %collective-permute-start = (f32[8,2048]{1,0:T(8,128)S(1)}, f32[8,2048]{1,0:T(8,128)S(1)}, u32[]{:S(2)}, u32[]{:S(2)}) collective-permute-start(f32[8,2048]{1,0:T(8,128)S(1)} %fusion.3), channel_id=1, source_target_pairs={{0,1},{1,2},{2,3},{3,4},{4,5},{5,6},{6,7},{7,8},{8,9},{9,10},{10,1... | collective-permute-start | bytes 196616 | tf_op jit(solution)/shard_map/ppermute | solution.py:97
Sparse Core Ops, SparseCore 0:
  17.2 53.1 all-gather.1
